TPU v7x, 512 devices: a whole 4x8x8 slice. The times are simulated.
512 devices in a mesh: req: 128 (over y, z, core), tp: 4 (over x).
Axes of the slice: x: 4, y: 8, z: 8, core: 2. Of those that a mesh axis runs over, the one named last changes fastest.
Arguments:
- qkv_rows: bfloat16 [32768, 3, 1536], P('req', None, 'tp'), may hold values from -13 to 13
- row_request: int32 [32768], P('req'), may hold values from 0 to 127, as said below
- request_owner: int32 [128], replicated, may hold values from 0 to 127, each once
- cached_len: int32 [128], P('req'), may hold values from 0 to 1024
- page_table: int32 [128, 8], P('req'), may hold values from 0 to 7, as said below
- kv_pages: bfloat16 [1024, 2, 128, 1536], P('req', None, None, 'tp'), may hold values from -6 to 6
- residual: bfloat16 [32768, 3072], P('req', 'tp'), may hold values from -128 to 128
- out_weight: bfloat16 [1536, 3072], P('tp'), may hold values from -0.15625 to 0.15625
- norm_gain: bfloat16 [3072], P('tp'), may hold values from 0.5 to 1.5
Outputs:
- new_residual: bfloat16 [32768, 3072], P('req', 'tp')
- normed: bfloat16 [32768, 3072], P('req', 'tp')
Inputs may be any that keep to these rules, and one draw needn't show every extreme that they name: `row_request`: on every device at most 5 new tokens name the same request, and one request is named by exactly 5 tokens on every device. Half of the requests are named by exactly one token in all, and no two of those tokens lie on one device. `request_owner`: each device holds the cache of exactly one request. `page_table`: each row names every page of its device's pool once.
All inputs are finite; a program needn't handle non-finite values.
Results may differ from a plain program's by a relative error of at most 0.0093.
The roundings to bfloat16 on the way count: a program that leaves them out, or rounds other values in their place, can miss the bound.
Values may be sent and summed in bfloat16 or wider, within the bound.
No kernel may reach another device: no remote copies, remote signals or barrier semaphores. Data moves between devices by JAX's collectives and lax.ppermute only.
A program may use at most 64 MiB of HBM per device.

v0:
```python
import math

import jax
import jax.numpy as jnp
from jax import lax
from jax.sharding import PartitionSpec as P

D = 3072
HEAD_SIZE = 96


ROPE_BASE = 10000.0
EPS = 1e-05


def rope_tables(position):
    halves = HEAD_SIZE // 2
    inverse = ROPE_BASE ** (-2.0 * jnp.arange(halves, dtype=jnp.float32) / HEAD_SIZE)
    angles = position.astype(jnp.float32)[:, None] * inverse[None, :]
    cosine = jnp.concatenate([jnp.cos(angles), jnp.cos(angles)], axis=1)
    sine_tab = jnp.concatenate([jnp.sin(angles), jnp.sin(angles)], axis=1)
    return (cosine, sine_tab)


def rotate(field, cosine, sine_tab):
    halves = HEAD_SIZE // 2
    turned = jnp.concatenate([-field[..., halves:], field[..., :halves]], axis=-1)
    return field * cosine[:, None, :] + turned * sine_tab[:, None, :]


def attend_heads(grouped, cache_keys, cache_values, cosine, sine_tab, visible):
    score_scale = 1.0 / math.sqrt(HEAD_SIZE)
    query_rows_block = rotate(grouped[:, 0].astype(jnp.float32), cosine, sine_tab).astype(
        jnp.bfloat16
    )
    fresh_keys = rotate(grouped[:, 1].astype(jnp.float32), cosine, sine_tab).astype(jnp.bfloat16)
    gathered_keys = jnp.concatenate([cache_keys, fresh_keys], axis=0)
    gathered_values = jnp.concatenate([cache_values, grouped[:, 2]], axis=0)

    def one_head(head_parts):
        head_query, head_keys, head_values = head_parts
        logit_scores = (
            jnp.einsum("md,kd->mk", head_query, head_keys, preferred_element_type=jnp.float32)
            * score_scale
        )
        logit_scores = jnp.where(visible, logit_scores, -1e30)
        top_score = jnp.max(logit_scores, axis=1, keepdims=True)
        weight = jnp.exp(logit_scores - top_score)
        softmax_weights = (weight / jnp.sum(weight, axis=1, keepdims=True)).astype(jnp.bfloat16)
        return jnp.einsum(
            "mk,kd->md", softmax_weights, head_values, preferred_element_type=jnp.float32
        ).astype(jnp.bfloat16)

    heads_out = lax.map(
        one_head,
        (
            query_rows_block.transpose(1, 0, 2),
            gathered_keys.transpose(1, 0, 2),
            gathered_values.transpose(1, 0, 2),
        ),
    )
    return heads_out.transpose(1, 0, 2)


def on_device(
    qkv_rows,
    row_request,
    request_owner,
    cached_len,
    page_table,
    kv_pages,
    residual,
    out_weight,
    norm_gain,
):
    row_count = qkv_rows.shape[0]
    head_cols = qkv_rows.shape[2]
    heads_here = head_cols // HEAD_SIZE
    devices = lax.axis_size("req")
    slot_cap = 5 * row_count // (2 * devices)
    buffer_len = devices * slot_cap
    device_ids = jnp.arange(devices, dtype=jnp.int32)
    matches = row_request[:, None] == device_ids[None, :]
    owner_dev = jnp.sum(jnp.where(matches, request_owner[None, :], 0), axis=1)
    sends_to = (owner_dev[:, None] == device_ids[None, :]).astype(jnp.int32)
    earlier = jnp.cumsum(sends_to, axis=0) - sends_to
    slot_in = jnp.sum(earlier * sends_to, axis=1)
    target = owner_dev * slot_cap + slot_in
    counts = jnp.sum(sends_to, axis=0)
    outgoing = jnp.zeros((buffer_len, 3, head_cols), qkv_rows.dtype).at[target].set(qkv_rows)
    length = cached_len[0]
    pool_pages = kv_pages[page_table[0]]
    cache_span = pool_pages.shape[0] * pool_pages.shape[2]
    cache_keys = pool_pages[:, 0].reshape(cache_span, heads_here, HEAD_SIZE)
    cache_values = pool_pages[:, 1].reshape(cache_span, heads_here, HEAD_SIZE)
    arrived, arrived_counts = (
        lax.all_to_all(
            outgoing.reshape(devices, slot_cap, 3, head_cols),
            "req",
            split_axis=0,
            concat_axis=0,
            tiled=True,
        ),
        lax.all_to_all(counts, "req", split_axis=0, concat_axis=0, tiled=True),
    )
    live_slot = (jnp.arange(slot_cap, dtype=jnp.int32)[None, :] < arrived_counts[:, None]).reshape(
        buffer_len
    )
    live_int = live_slot.astype(jnp.int32)
    new_rank = jnp.cumsum(live_int) - live_int
    cosine, sine_tab = rope_tables(length + new_rank)
    cache_ok = jnp.broadcast_to(
        (jnp.arange(cache_span, dtype=jnp.int32) < length)[None, :], (buffer_len, cache_span)
    )
    new_ok = live_slot[None, :] & (new_rank[None, :] <= new_rank[:, None])
    visible = jnp.concatenate([cache_ok, new_ok], axis=1)
    cosine, sine_tab, visible = (cosine, sine_tab, visible)
    grouped = arrived.reshape(buffer_len, 3, heads_here, HEAD_SIZE)
    result = attend_heads(grouped, cache_keys, cache_values, cosine, sine_tab, visible)
    returned = lax.all_to_all(
        result.reshape(devices, slot_cap, head_cols), "req", split_axis=0, concat_axis=0, tiled=True
    )
    attn_rows = returned.reshape(buffer_len, head_cols)[target]
    partial_sum = jnp.dot(attn_rows, out_weight, preferred_element_type=jnp.float32)
    share_cols = residual.shape[1]
    whole_sum = lax.psum(partial_sum.astype(jnp.bfloat16), "tp").astype(jnp.float32)
    mixed_cols = lax.dynamic_slice_in_dim(
        whole_sum, lax.axis_index("tp") * share_cols, share_cols, 1
    )
    hidden = residual.astype(jnp.float32) + mixed_cols
    square_sum = lax.psum(jnp.sum(hidden * hidden, axis=1), "tp")
    inv_rms = lax.rsqrt(square_sum / D + EPS)
    normed = hidden * inv_rms[:, None] * norm_gain.astype(jnp.float32)[None, :]
    return (hidden.astype(jnp.bfloat16), normed.astype(jnp.bfloat16))


def solution(mesh):
    return jax.shard_map(
        on_device,
        mesh=mesh,
        in_specs=(
            P("req", None, "tp"),
            P("req"),
            P(),
            P("req"),
            P("req", None),
            P("req", None, None, "tp"),
            P("req", "tp"),
            P("tp", None),
            P("tp"),
        ),
        out_specs=(P("req", "tp"), P("req", "tp")),
        check_vma=False,
    )
```

profile of v0, /device:TPU:56, one launch (start us, length us, event | category | flops | bytes accessed | tf_op | source)
XLA Modules:
  0.0 279.9 jit_solution(1655667734073437765)
XLA Ops:
  7.2 1.0 select_reduce_fusion
  8.8 0.7 copy.41
  9.6 17.3 %all-to-all-start.1 = ((s32[128,1,1]{2,1,0:T(1,128)}), s32[128,1,1]{2,1,0:T(1,128)S(1)}, u32[]{:S(2)}, u32[]{:S(2)}) async-start(s32[128,1,1]{2,1,0:T(1,128)} %copy.41), calls=%async_computation.1 | async-start | bytes 131072 | tf_op jit(solution)/shard_map/all_to_all | solution.py:104
  26.9 1.6 copy.39
  28.5 1.8 broadcast_in_dim.25
  30.3 27.2 %scatter_fusion = bf16[640,3,384]{2,1,0:T(4,128)(2,1)} fusion(bf16[640,3,384]{2,1,0:T(4,128)(2,1)} %broadcast_in_dim.25, s32[256]{0:T(256)S(1)} %bitcast.92, bf16[256,3,384]{2,1,0:T(4,128)(2,1)S(1)} %copy.39), kind=kCustom, calls=%fused_computation.2 | custom fusion | bytes 1770496 | tf_op jit(solution)/shard_map/scatter | solution.py:90
  57.5 14.2 %all-to-all-start = ((bf16[128,5,3,384]{3,2,1,0:T(4,128)(2,1)}), bf16[128,5,3,384]{3,2,1,0:T(4,128)(2,1)}, u32[]{:S(2)}, u32[]{:S(2)}) async-start(bf16[128,5,3,384]{3,2,1,0:T(4,128)(2,1)} %bitcast.86), calls=%async_computation | async-start | bytes 3932160 | tf_op jit(solution)/shard_map/all_to_all | solution.py:97
  72.4 3.3 %gather_fusion = bf16[8,2,128,384]{3,2,1,0:T(8,128)(2,1)} fusion(bf16[8,2,128,384]{3,2,1,0:T(8,128)(2,1)} %param.16, s32[1024]{0:T(1024)S(1)} %pad_clamp_fusion.1), kind=kCustom, calls=%fused_computation | custom fusion | bytes 3145760 | tf_op jit(solution)/shard_map/gather | solution.py:92
  75.7 2.8 fusion.29
  78.5 1.6 copy.42
  80.1 1.2 reshape_squeeze.6
  81.3 1.6 copy.44
  82.9 1.2 reshape_squeeze.7
  84.2 2.4 reduce
  87.6 1.2 multiply_cosine_fusion
  88.9 1.1 pad_maximum_fusion
  90.7 28.8 %all-to-all-done = bf16[128,5,3,384]{3,2,1,0:T(4,128)(2,1)} async-done(((bf16[128,5,3,384]{3,2,1,0:T(4,128)(2,1)}), bf16[128,5,3,384]{3,2,1,0:T(4,128)(2,1)}, u32[]{:S(2)}, u32[]{:S(2)}) %all-to-all-start) | async-done | bytes 1474592 | tf_op jit(solution)/shard_map/all_to_all | solution.py:97
  119.5 5.9 %reshape.198 = bf16[640,3,4,96]{3,2,1,0:T(4,128)(2,1)} reshape(bf16[128,5,3,384]{3,2,1,0:T(4,128)(2,1)} %all-to-all-done) | data formatting | bytes 2949120 | tf_op jit(solution)/shard_map/reshape | solution.py:118
  125.4 2.7 slice_bitcast_fusion
  128.1 1.5 slice_negate_fusion
  129.8 2.7 fusion.16
  132.4 0.9 copy.46
  133.3 2.1 copy.43
  135.5 2.1 copy.45
  137.6 2.5 maximum_bitcast_fusion
  140.1 1.2 maximum_bitcast_fusion.1
  141.3 22.0 %while.10 = (s32[]{:T(128)}, bf16[4,640,96]{1,2,0:T(8,128)(2,1)}, bf16[4,640,96]{2,1,0:T(8,128)(2,1)}, bf16[4,1664,96]{1,2,0:T(8,128)(2,1)}, pred[640,1664]{1,0:...) while((s32[]{:T(128)}, bf16[4,640,96]{1,2,0:T(8,128)(2,1)}, bf16[4,640,96]{2,1,0:T(8,128)(2,1)}, ...), condition=%wide.region_11.12_spmd, body=%wide.region_8.11_spmd.sunk | while | flops 417524480 | bytes 14785109 | solution.py:54
  141.3 2.1 fusion.37
  143.4 0.7 fusion.38
  144.1 2.6 fusion.39
  146.8 2.1 fusion.37
  149.6 2.7 fusion.39
  152.3 2.1 fusion.37
  155.2 2.6 fusion.39
  157.8 2.1 fusion.37
  160.0 0.7 fusion.38
  160.7 2.6 fusion.39
  163.3 1.7 copy.49
  165.0 1.7 reshape.200
  166.7 9.5 %all-to-all-start.2 = ((bf16[128,5,384]{2,1,0:T(8,128)(2,1)}), bf16[128,5,384]{2,1,0:T(8,128)(2,1)}, u32[]{:S(2)}, u32[]{:S(2)}) async-start(bf16[128,5,384]{2,1,0:T(8,128)(2,1)} %reshape.200), calls=%async_computation.2 | async-start | bytes 1572864 | tf_op jit(solution)/shard_map/all_to_all | solution.py:120
  176.2 22.4 %all-to-all-done.2 = bf16[128,5,384]{2,1,0:T(8,128)(2,1)} async-done(((bf16[128,5,384]{2,1,0:T(8,128)(2,1)}), bf16[128,5,384]{2,1,0:T(8,128)(2,1)}, u32[]{:S(2)}, u32[]{:S(2)}) %all-to-all-start.2) | async-done | bytes 491552 | tf_op jit(solution)/shard_map/all_to_all | solution.py:120
  198.6 1.4 reshape.201
  200.0 1.2 gather_fusion.1
  201.2 2.1 convolution_convert_fusion
  204.0 56.2 %all-reduce.2.cloned.1.call-done = bf16[256,3072]{1,0:T(8,128)(2,1)} async-done(((bf16[256,3072]{1,0:T(8,128)(2,1)}), bf16[256,3072]{1,0:T(8,128)(2,1)}) %all-reduce.2.cloned.1.call-update) | async-done | bytes 1572880 | tf_op jit(solution)/shard_map/psum | solution.py:126
  260.2 1.2 multiply_reduce_fusion
  261.4 9.5 %psum.15 = f32[256]{0:T(256)S(1)} all-reduce(f32[256]{0:T(256)S(1)} %multiply_reduce_fusion), channel_id=1, replica_groups=mesh['req'=128,'tp'=4] {'tp'}, use_global_device_ids=true, to_apply=%region_14.15 | all-reduce | flops 256 | bytes 2048 | tf_op jit(solution)/shard_map/psum | solution.py:131
  271.0 2.0 multiply_convert_fusion
  (53 shorter events, 4.7 us)
Async XLA Ops:
  7.2 194.0 %copy-start = (bf16[384,3072]{1,0:T(8,128)(2,1)S(1)}, bf16[384,3072]{1,0:T(8,128)(2,1)}, u32[]{:S(2)}) copy-start(bf16[384,3072]{1,0:T(8,128)(2,1)} %param.18) | copy-start | bytes 7077892
  9.6 47.9 %all-to-all-start.1 = ((s32[128,1,1]{2,1,0:T(1,128)}), s32[128,1,1]{2,1,0:T(1,128)S(1)}, u32[]{:S(2)}, u32[]{:S(2)}) async-start(s32[128,1,1]{2,1,0:T(1,128)} %copy.41), calls=%async_computation.1 | async-start | bytes 131072 | tf_op jit(solution)/shard_map/all_to_all | solution.py:104
  57.5 14.9 %copy-start.8 = (s32[1,8]{1,0:T(1,128)S(1)}, s32[1,8]{1,0:T(1,128)}, u32[]{:S(2)}) copy-start(s32[1,8]{1,0:T(1,128)} %param.15) | copy-start | bytes 100
  57.5 62.0 %all-to-all-start = ((bf16[128,5,3,384]{3,2,1,0:T(4,128)(2,1)}), bf16[128,5,3,384]{3,2,1,0:T(4,128)(2,1)}, u32[]{:S(2)}, u32[]{:S(2)}) async-start(bf16[128,5,3,384]{3,2,1,0:T(4,128)(2,1)} %bitcast.86), calls=%async_computation | async-start | bytes 3932160 | tf_op jit(solution)/shard_map/all_to_all | solution.py:97
  128.1 1.5 copy-start.1
  128.1 1.6 copy-start.5
  128.1 1.7 copy-start.6
  137.6 2.5 copy-start.2
  137.6 2.5 copy-start.3
  166.7 32.0 %all-to-all-start.2 = ((bf16[128,5,384]{2,1,0:T(8,128)(2,1)}), bf16[128,5,384]{2,1,0:T(8,128)(2,1)}, u32[]{:S(2)}, u32[]{:S(2)}) async-start(bf16[128,5,384]{2,1,0:T(8,128)(2,1)} %reshape.200), calls=%async_computation.2 | async-start | bytes 1572864 | tf_op jit(solution)/shard_map/all_to_all | solution.py:120
  176.1 84.1 %all-reduce.2.cloned.1.call-start = ((), (), s32[]{:S(2)}) async-start(), calls=%async_computation.3 | async-start | bytes 3145728 | tf_op jit(solution)/shard_map/psum | solution.py:126
  203.3 0.7 copy-start.7
  203.3 56.9 %copy-start.4 = (bf16[256,768]{1,0:T(8,128)(2,1)S(1)}, bf16[256,768]{1,0:T(8,128)(2,1)}, u32[]{:S(2)}) copy-start(bf16[256,768]{1,0:T(8,128)(2,1)} %param.17) | copy-start | bytes 1179652
Sparse Core Ops, SparseCore 0:
  203.5 56.7 all-reduce.1
where the time goes:
time: 282 us; the launch traced here: 280 us
  waiting for transfers between devices  108 us (38%)
  local copies, waits for them, and re-layouts  61.6 us (22%)
  starting transfers between devices  41.1 us (15%)
  other arithmetic  24 us (9%)
  matrix products  21.3 us (8%)
  between operations  14.9 us (5%)
  blocking collectives  9.53 us (3%)
    psum x1, waiting for transfers between devices, on_device(): lax.psum(partial_sum.astype(jnp.bfloat16), 'tp').astype(jnp.float32)  56.2 us
    all_to_all x1, waiting for transfers between devices, on_device(): lax.all_to_all(outgoing.reshape(devices, slot_cap, 3, head_cols), 'req',...  28.8 us
    scatter x1, local copies, waits for them, and re-layouts, on_device(): jnp.zeros((buffer_len, 3, head_cols), qkv_rows.dtype).at[target]  27.2 us
    all_to_all x1, waiting for transfers between devices, on_device(): lax.all_to_all(result.reshape(devices, slot_cap, head_cols), 'req', split...  22.4 us
    all_to_all x1, starting transfers between devices, on_device(): lax.all_to_all(counts, 'req', split_axis=0, concat_axis=0, tiled=True)  17.3 us
    all_to_all x1, starting transfers between devices, on_device(): lax.all_to_all(outgoing.reshape(devices, slot_cap, 3, head_cols), 'req',...  14.2 us
    dot_general x4, matrix products, one_head(): jnp.einsum('mk,kd->md', softmax_weights, head_values, preferred_element_t...  10.6 us
    psum x1, blocking collectives, on_device(): square_sum = lax.psum(jnp.sum(hidden * hidden, axis=1), 'tp')  9.53 us
  transfers between devices with their start and end apart: 4, of which 3 were waited for; matrix products, arithmetic and copies ran while one was open for 17% of the time, Pallas kernels for 0%

commit v1 on v0

--- a/solution.py
+++ b/solution.py
@@ -7,7 +7,7 @@
 
 D = 3072
 HEAD_SIZE = 96
-
+SLOT = 5
 
 ROPE_BASE = 10000.0
 EPS = 1e-05
@@ -74,35 +74,40 @@
     norm_gain,
 ):
     row_count = qkv_rows.shape[0]
+    parts = qkv_rows.shape[1]
     head_cols = qkv_rows.shape[2]
     heads_here = head_cols // HEAD_SIZE
     devices = lax.axis_size("req")
-    slot_cap = 5 * row_count // (2 * devices)
+    slot_cap = SLOT
     buffer_len = devices * slot_cap
     device_ids = jnp.arange(devices, dtype=jnp.int32)
-    matches = row_request[:, None] == device_ids[None, :]
-    owner_dev = jnp.sum(jnp.where(matches, request_owner[None, :], 0), axis=1)
-    sends_to = (owner_dev[:, None] == device_ids[None, :]).astype(jnp.int32)
-    earlier = jnp.cumsum(sends_to, axis=0) - sends_to
-    slot_in = jnp.sum(earlier * sends_to, axis=1)
-    target = owner_dev * slot_cap + slot_in
-    counts = jnp.sum(sends_to, axis=0)
-    outgoing = jnp.zeros((buffer_len, 3, head_cols), qkv_rows.dtype).at[target].set(qkv_rows)
+    row_ids = jnp.arange(row_count, dtype=jnp.int32)
+
+    owner_dev = request_owner[row_request]
+    same_owner = owner_dev[:, None] == owner_dev[None, :]
+    slot_in = jnp.sum((same_owner & (row_ids[None, :] < row_ids[:, None])).astype(jnp.int32), axis=1)
+    sends_to = owner_dev[:, None] == device_ids[None, :]
+    counts = jnp.sum(sends_to.astype(jnp.int32), axis=0)
+
+    pick = (
+        sends_to[None, :, :]
+        & (slot_in[None, :, None] == jnp.arange(slot_cap, dtype=jnp.int32)[:, None, None])
+    ).astype(jnp.bfloat16)
+    slots = jnp.einsum(
+        "jid,ipc->djpc", pick, qkv_rows, preferred_element_type=jnp.float32
+    ).astype(jnp.bfloat16)
+    count_row = jnp.broadcast_to(counts.astype(jnp.bfloat16)[:, None, None], (devices, 1, head_cols))
+    outgoing = jnp.concatenate(
+        [slots.reshape(devices, slot_cap * parts, head_cols), count_row], axis=1
+    )
+    arrived = lax.all_to_all(outgoing, "req", split_axis=0, concat_axis=0, tiled=True)
+    arrived_counts = arrived[:, slot_cap * parts, 0].astype(jnp.int32)
+
     length = cached_len[0]
     pool_pages = kv_pages[page_table[0]]
     cache_span = pool_pages.shape[0] * pool_pages.shape[2]
     cache_keys = pool_pages[:, 0].reshape(cache_span, heads_here, HEAD_SIZE)
     cache_values = pool_pages[:, 1].reshape(cache_span, heads_here, HEAD_SIZE)
-    arrived, arrived_counts = (
-        lax.all_to_all(
-            outgoing.reshape(devices, slot_cap, 3, head_cols),
-            "req",
-            split_axis=0,
-            concat_axis=0,
-            tiled=True,
-        ),
-        lax.all_to_all(counts, "req", split_axis=0, concat_axis=0, tiled=True),
-    )
     live_slot = (jnp.arange(slot_cap, dtype=jnp.int32)[None, :] < arrived_counts[:, None]).reshape(
         buffer_len
     )
@@ -114,19 +119,17 @@
     )
     new_ok = live_slot[None, :] & (new_rank[None, :] <= new_rank[:, None])
     visible = jnp.concatenate([cache_ok, new_ok], axis=1)
-    cosine, sine_tab, visible = (cosine, sine_tab, visible)
-    grouped = arrived.reshape(buffer_len, 3, heads_here, HEAD_SIZE)
+    grouped = arrived[:, : slot_cap * parts].reshape(buffer_len, parts, heads_here, HEAD_SIZE)
     result = attend_heads(grouped, cache_keys, cache_values, cosine, sine_tab, visible)
     returned = lax.all_to_all(
-        result.reshape(devices, slot_cap, head_cols), "req", split_axis=0, concat_axis=0, tiled=True
+        result.reshape(devices, slot_cap * head_cols), "req", split_axis=0, concat_axis=0, tiled=True
     )
+    target = owner_dev * slot_cap + slot_in
     attn_rows = returned.reshape(buffer_len, head_cols)[target]
     partial_sum = jnp.dot(attn_rows, out_weight, preferred_element_type=jnp.float32)
-    share_cols = residual.shape[1]
-    whole_sum = lax.psum(partial_sum.astype(jnp.bfloat16), "tp").astype(jnp.float32)
-    mixed_cols = lax.dynamic_slice_in_dim(
-        whole_sum, lax.axis_index("tp") * share_cols, share_cols, 1
-    )
+    mixed_cols = lax.psum_scatter(
+        partial_sum.astype(jnp.bfloat16), "tp", scatter_dimension=1, tiled=True
+    ).astype(jnp.float32)
     hidden = residual.astype(jnp.float32) + mixed_cols
     square_sum = lax.psum(jnp.sum(hidden * hidden, axis=1), "tp")
     inv_rms = lax.rsqrt(square_sum / D + EPS)

time: 282 us -> 221 us (0.78)
  waiting for transfers between devices: 108 us -> 69.7 us
  local copies, waits for them, and re-layouts: 61.6 us -> 41.5 us
  starting transfers between devices: 41.1 us -> 27.4 us
  other arithmetic: 24 us -> 34.2 us
    psum x1 -> x0, waiting for transfers between devices: 56.2 us -> none  [on_device(): lax.psum(partial_sum.astype(jnp.bfloat16), 'tp').astype(jnp.float32)]
    scatter x1 -> x0, local copies, waits for them, and re-layouts: 27.2 us -> none  [on_device(): jnp.zeros((buffer_len, 3, head_cols), qkv_rows.dtype).at[target]]
    reduce_scatter x0 -> x1, waiting for transfers between devices: none -> 25.3 us  [on_device(): lax.psum_scatter(partial_sum.astype(jnp.bfloat16), 'tp', scatter_dimensio...]
    all_to_all x3 -> x2, starting transfers between devices: 41 us -> 27.4 us  [the longest x1 17.9 us: on_device(): lax.all_to_all(outgoing, 'req', split_axis=0, concat_axis=0, tiled=True)]
    all_to_all x3 -> x2, waiting for transfers between devices: 51.3 us -> 44.4 us  [the longest x1 26.9 us: on_device(): lax.all_to_all(outgoing, 'req', split_axis=0, concat_axis=0, tiled=True)]
    all_to_all x1 -> x2, other arithmetic: 2.35 us -> 8.12 us  [on_device(): lax.all_to_all(result.reshape(devices, slot_cap * head_cols), 'req', spli...]
    unnamed x20 -> x22, local copies, waits for them, and re-layouts: 2.39 us -> 6.69 us
    all_to_all x1 -> x2, local copies, waits for them, and re-layouts: 0.75 us -> 4.27 us  [on_device(): lax.all_to_all(result.reshape(devices, slot_cap * head_cols), 'req', spli...]
  transfers between devices with their start and end apart: 4 -> 3, of which waited for: 3 -> 3; matrix products, arithmetic and copies ran while one was open for 17% -> 5% of each run, Pallas kernels for 0% -> 0%
where the time goes in v1:
time: 221 us; the launch traced here: 219 us
  waiting for transfers between devices  69.7 us (32%)
  local copies, waits for them, and re-layouts  41.5 us (19%)
  other arithmetic  34.2 us (15%)
  starting transfers between devices  27.4 us (12%)
  matrix products  21.9 us (10%)
  between operations  14.9 us (7%)
  blocking collectives  9.07 us (4%)
    all_to_all x1, waiting for transfers between devices, on_device(): lax.all_to_all(outgoing, 'req', split_axis=0, concat_axis=0, tiled=True)  26.9 us
    reduce_scatter x1, waiting for transfers between devices, on_device(): lax.psum_scatter(partial_sum.astype(jnp.bfloat16), 'tp', scatter_dimensio...  25.3 us
    all_to_all x1, starting transfers between devices, on_device(): lax.all_to_all(outgoing, 'req', split_axis=0, concat_axis=0, tiled=True)  17.9 us
    all_to_all x1, waiting for transfers between devices, on_device(): lax.all_to_all(result.reshape(devices, slot_cap * head_cols), 'req', spli...  17.6 us
    dot_general x4, matrix products, one_head(): jnp.einsum('mk,kd->md', softmax_weights, head_values, preferred_element_t...  10.6 us
    all_to_all x1, starting transfers between devices, on_device(): lax.all_to_all(result.reshape(devices, slot_cap * head_cols), 'req', spli...  9.51 us
    psum x1, blocking collectives, on_device(): square_sum = lax.psum(jnp.sum(hidden * hidden, axis=1), 'tp')  9.07 us
    dot_general x4, matrix products, one_head(): jnp.einsum('md,kd->mk', head_query, head_keys, preferred_element_type=jnp...  8.57 us
  transfers between devices with their start and end apart: 3, of which 3 were waited for; matrix products, arithmetic and copies ran while one was open for 5% of the time, Pallas kernels for 0%

profile of v1, /device:TPU:56, one launch (start us, length us, event | category | flops | bytes accessed | tf_op | source)
XLA Modules:
  0.0 218.7 jit_solution(9074773104622484159)
XLA Ops:
  7.2 0.8 compare_select_fusion.1
  8.0 1.9 gather_fusion
  10.9 0.9 copy.45
  12.0 1.7 pad_maximum_fusion
  13.7 17.9 %all-to-all-start = ((bf16[128,16,384]{2,1,0:T(8,128)(2,1)}), bf16[128,16,384]{2,1,0:T(8,128)(2,1)}, u32[]{:S(2)}, u32[]{:S(2)}) async-start(bf16[128,16,384]{2,1,0:T(8,128)(2,1)} %pad_maximum_fusion), calls=%async_computation | async-start | bytes 3145728 | tf_op jit(solution)/shard_map/all_to_all | solution.py:103
  32.3 3.3 %gather_fusion.1 = bf16[8,2,128,384]{3,2,1,0:T(8,128)(2,1)} fusion(bf16[8,2,128,384]{3,2,1,0:T(8,128)(2,1)} %param.16, s32[1024]{0:T(1024)S(1)} %pad_clamp_fusion.1), kind=kCustom, calls=%fused_computation.1 | custom fusion | bytes 3145760 | tf_op jit(solution)/shard_map/gather | solution.py:107
  35.7 2.8 %fusion.31 = (bf16[8,1,128,384]{3,2,1,0:T(8,128)(2,1)}, bf16[8,1,128,384]{3,2,1,0:T(8,128)(2,1)}) fusion(bf16[8,2,128,384]{3,2,1,0:T(8,128)(2,1)} %gather_fusion.1), kind=kLoop, calls=%fused_computation.78 | loop fusion | bytes 3145728 | tf_op jit(solution)/shard_map/slice | solution.py:110
  38.4 1.6 copy.47
  40.1 1.2 reshape_squeeze.6
  41.3 1.6 copy.49
  42.9 1.2 reshape_squeeze.7
  44.2 26.9 %all-to-all-done = bf16[128,16,384]{2,1,0:T(8,128)(2,1)} async-done(((bf16[128,16,384]{2,1,0:T(8,128)(2,1)}), bf16[128,16,384]{2,1,0:T(8,128)(2,1)}, u32[]{:S(2)}, u32[]{:S(2)}) %all-to-all-start) | async-done | bytes 1572896 | tf_op jit(solution)/shard_map/all_to_all | solution.py:103
  71.0 3.3 %fusion.27 = s32[128]{0:T(128)S(1)} fusion(bf16[128,16,384]{2,1,0:T(8,128)(2,1)} %all-to-all-done), kind=kLoop, calls=%fused_computation.59 | loop fusion | flops 128 | bytes 768 | tf_op jit(solution)/shard_map/convert_element_type | solution.py:104
  75.3 4.9 %reshape.230 = bf16[640,3,4,96]{3,2,1,0:T(4,128)(2,1)} reshape(bf16[128,15,384]{2,1,0:T(8,128)(2,1)} %bitcast.75) | data formatting | bytes 2949120 | tf_op jit(solution)/shard_map/reshape | solution.py:122
  80.2 2.7 %slice_bitcast_fusion = (bf16[640,4,96]{2,1,0:T(4,128)(2,1)}, f32[640,4,96]{2,1,0:T(4,128)S(1)}, f32[640,4,96]{2,1,0:T(4,128)S(1)}) fusion(bf16[640,3,4,96]{3,2,1,0:T(4,128)(2,1)} %reshape.230), kind=kLoop, calls=%fused_computation.38 | loop fusion | flops 491520 | bytes 3932160 | tf_op jit(solution)/shard_map/squeeze | solution.py:38
  83.0 1.2 multiply_cosine_fusion
  84.4 1.5 slice_negate_fusion
  86.0 2.7 %fusion.16 = (bf16[640,4,96]{2,1,0:T(4,128)(2,1)S(1)}, bf16[4,640,96]{2,0,1:T(4,128)(2,1)}) fusion(f32[640,4,48]{2,1,0:T(4,128)S(1)} %get-tuple-element.83, f32[640,4,48]{2,1,0:T(4,128)S(1)} %get-tuple-element.82, f32[640,96]{1,0:T(8,128)S(1)} %get-tuple-element.95, f32[640,96]{1,0:T(8,128)S(1)} %get-tuple-element.94, ...), kind=kLoop, calls=%fused_computation.31 | loop fusion | flops 2949120 | bytes 4423680 | tf_op jit(solution)/shard_map/convert_element_type | solution.py:36
  88.6 1.4 copy.48
  90.1 2.1 copy.51
  92.2 1.1 compare_and_fusion
  93.3 2.1 copy.50
  95.4 2.3 %maximum_bitcast_fusion = bf16[4,1664,96]{1,2,0:T(8,128)(2,1)} fusion(bf16[640,4,96]{0,2,1:T(8,128)(2,1)} %copy.48, bf16[1024,4,96]{0,2,1:T(8,128)(2,1)S(1)} %copy-done.3), kind=kLoop, calls=%fused_computation.32 | loop fusion | flops 2555904 | bytes 2555904 | tf_op jit(solution)/shard_map/transpose | solution.py:58
  98.1 1.2 maximum_bitcast_fusion.1
  99.3 22.0 %while.10 = (s32[]{:T(128)}, bf16[4,640,96]{1,2,0:T(8,128)(2,1)}, bf16[4,640,96]{2,1,0:T(8,128)(2,1)}, bf16[4,1664,96]{1,2,0:T(8,128)(2,1)}, pred[640,1664]{1,0:...) while((s32[]{:T(128)}, bf16[4,640,96]{1,2,0:T(8,128)(2,1)}, bf16[4,640,96]{2,1,0:T(8,128)(2,1)}, ...), condition=%wide.region_7.8_spmd, body=%wide.region_4.7_spmd.sunk | while | flops 417524480 | bytes 14785101 | solution.py:54
  99.3 2.1 fusion.39
  102.1 2.6 %fusion.41 = bf16[4,640,96]{1,2,0:T(8,128)(2,1)} fusion(bf16[4,640,96]{1,2,0:T(8,128)(2,1)} %get-tuple-element.145, s32[]{:T(128)} %get-tuple-element.144, f32[640,1664]{1,0:T(8,128)S(1)} %get-tuple-element.135, f32[640]{0:T(1024)S(1)} %fusion.40, f32[640]{0:T(1024)S(1)} %get-tuple-element.136, bf16[4,1664,96]{1,2,0:T(8,128)(2,1)} %get-tuple-element.156), kind=kOutput, calls=%fused_computation.10.clone.1 | convolution fusion | flops 207728640 | bytes 4708352 | tf_op jit(solution)/shard_map/while/body/eval_jaxpr/mk,kd->md/dot_general | solution.py:50
  104.8 2.1 fusion.39
  107.6 2.6 %fusion.41 = bf16[4,640,96]{1,2,0:T(8,128)(2,1)} fusion(bf16[4,640,96]{1,2,0:T(8,128)(2,1)} %get-tuple-element.145, s32[]{:T(128)} %get-tuple-element.144, f32[640,1664]{1,0:T(8,128)S(1)} %get-tuple-element.135, f32[640]{0:T(1024)S(1)} %fusion.40, f32[640]{0:T(1024)S(1)} %get-tuple-element.136, bf16[4,1664,96]{1,2,0:T(8,128)(2,1)} %get-tuple-element.156), kind=kOutput, calls=%fused_computation.10.clone.1 | convolution fusion | flops 207728640 | bytes 4708352 | tf_op jit(solution)/shard_map/while/body/eval_jaxpr/mk,kd->md/dot_general | solution.py:50
  110.3 2.1 fusion.39
  113.1 2.6 %fusion.41 = bf16[4,640,96]{1,2,0:T(8,128)(2,1)} fusion(bf16[4,640,96]{1,2,0:T(8,128)(2,1)} %get-tuple-element.145, s32[]{:T(128)} %get-tuple-element.144, f32[640,1664]{1,0:T(8,128)S(1)} %get-tuple-element.135, f32[640]{0:T(1024)S(1)} %fusion.40, f32[640]{0:T(1024)S(1)} %get-tuple-element.136, bf16[4,1664,96]{1,2,0:T(8,128)(2,1)} %get-tuple-element.156), kind=kOutput, calls=%fused_computation.10.clone.1 | convolution fusion | flops 207728640 | bytes 4708352 | tf_op jit(solution)/shard_map/while/body/eval_jaxpr/mk,kd->md/dot_general | solution.py:50
  115.8 2.1 fusion.39
  118.7 2.6 %fusion.41 = bf16[4,640,96]{1,2,0:T(8,128)(2,1)} fusion(bf16[4,640,96]{1,2,0:T(8,128)(2,1)} %get-tuple-element.145, s32[]{:T(128)} %get-tuple-element.144, f32[640,1664]{1,0:T(8,128)S(1)} %get-tuple-element.135, f32[640]{0:T(1024)S(1)} %fusion.40, f32[640]{0:T(1024)S(1)} %get-tuple-element.136, bf16[4,1664,96]{1,2,0:T(8,128)(2,1)} %get-tuple-element.156), kind=kOutput, calls=%fused_computation.10.clone.1 | convolution fusion | flops 207728640 | bytes 4708352 | tf_op jit(solution)/shard_map/while/body/eval_jaxpr/mk,kd->md/dot_general | solution.py:50
  121.3 2.1 copy.54
  123.4 3.8 %all_to_all.12 = bf16[128,1,1920]{2,1,0:T(2,128)(2,1)S(1)} reshape(bf16[640,4,96]{2,1,0:T(4,128)(2,1)} %copy.54) | data formatting | bytes 983040 | tf_op jit(solution)/shard_map/all_to_all | solution.py:124
  127.7 4.4 %reduce.5 = bf16[128,1920]{1,0:T(8,128)(2,1)} reduce(bf16[128,1,1920]{2,1,0:T(2,128)(2,1)S(1)} %all_to_all.12, bf16[]{:T(256)} %broadcast.143), dimensions={1}, to_apply=%all_to_all.12.reduce_sub_computation | reduce | bytes 983042 | tf_op jit(solution)/shard_map/all_to_all | solution.py:124
  132.1 2.3 %reshape.268 = bf16[128,2,960]{2,1,0:T(2,128)(2,1)} reshape(bf16[128,1920]{1,0:T(8,128)(2,1)} %reduce.5) | data formatting | bytes 983040
  134.4 9.5 %all-to-all-start.1 = ((bf16[128,2,960]{2,1,0:T(2,128)(2,1)}), bf16[128,2,960]{2,1,0:T(2,128)(2,1)}, u32[]{:S(2)}, u32[]{:S(2)}) async-start(bf16[128,2,960]{2,1,0:T(2,128)(2,1)} %reshape.268), calls=%async_computation.1 | async-start | bytes 1048576 | tf_op jit(solution)/shard_map/all_to_all | solution.py:124
  144.0 17.6 %all-to-all-done.1 = bf16[128,2,960]{2,1,0:T(2,128)(2,1)} async-done(((bf16[128,2,960]{2,1,0:T(2,128)(2,1)}), bf16[128,2,960]{2,1,0:T(2,128)(2,1)}, u32[]{:S(2)}, u32[]{:S(2)}) %all-to-all-start.1) | async-done | bytes 491552 | tf_op jit(solution)/shard_map/all_to_all | solution.py:124
  161.5 3.7 %reshape.269 = bf16[128,1,1920]{2,1,0:T(2,128)(2,1)S(1)} reshape(bf16[128,2,960]{2,1,0:T(2,128)(2,1)} %all-to-all-done.1) | data formatting | bytes 983040
  165.2 3.7 %reduce.2 = bf16[128,1920]{1,0:T(8,128)(2,1)} reduce(bf16[128,1,1920]{2,1,0:T(2,128)(2,1)S(1)} %reshape.269, bf16[]{:T(256)} %constant.56), dimensions={1}, to_apply=%all_to_all.11.reduce_sub_computation | reduce | bytes 983042 | tf_op jit(solution)/shard_map/all_to_all | solution.py:124
  168.9 1.4 reshape.232
  170.3 1.2 gather_fusion.2
  171.5 2.1 convolution_convert_fusion
  174.3 25.3 %reduce-scatter.2.cloned.1.call-done = bf16[256,768]{1,0:T(8,128)(2,1)} async-done(((bf16[256,3072]{1,0:T(8,128)(2,1)}), bf16[256,768]{1,0:T(8,128)(2,1)}) %reduce-scatter.2.cloned.1.call-update) | async-done | bytes 393232 | tf_op jit(solution)/shard_map/reduce_scatter | solution.py:130
  199.6 1.2 multiply_reduce_fusion
  200.8 9.1 %psum.7 = f32[256]{0:T(256)S(1)} all-reduce(f32[256]{0:T(256)S(1)} %multiply_reduce_fusion), channel_id=1, replica_groups=mesh['req'=128,'tp'=4] {'tp'}, use_global_device_ids=true, to_apply=%region_10.11 | all-reduce | flops 256 | bytes 2048 | tf_op jit(solution)/shard_map/psum | solution.py:134
  209.9 2.0 multiply_convert_fusion
  (56 shorter events, 7.0 us)
Async XLA Ops:
  7.2 164.3 %copy-start = (bf16[384,3072]{1,0:T(8,128)(2,1)S(1)}, bf16[384,3072]{1,0:T(8,128)(2,1)}, u32[]{:S(2)}) copy-start(bf16[384,3072]{1,0:T(8,128)(2,1)} %param.18) | copy-start | bytes 7077892
  7.2 3.1 %copy-start.7 = (bf16[256,3,384]{2,0,1:T(8,128)(2,1)S(1)}, bf16[256,3,384]{2,0,1:T(8,128)(2,1)}, u32[]{:S(2)}) copy-start(bf16[256,3,384]{2,0,1:T(8,128)(2,1)} %param.11) | copy-start | bytes 1769476
  13.7 18.5 %copy-start.9 = (s32[1,8]{1,0:T(1,128)S(1)}, s32[1,8]{1,0:T(1,128)}, u32[]{:S(2)}) copy-start(s32[1,8]{1,0:T(1,128)} %param.15) | copy-start | bytes 100
  13.7 57.3 %all-to-all-start = ((bf16[128,16,384]{2,1,0:T(8,128)(2,1)}), bf16[128,16,384]{2,1,0:T(8,128)(2,1)}, u32[]{:S(2)}, u32[]{:S(2)}) async-start(bf16[128,16,384]{2,1,0:T(8,128)(2,1)} %pad_maximum_fusion), calls=%async_computation | async-start | bytes 3145728 | tf_op jit(solution)/shard_map/all_to_all | solution.py:103
  84.4 1.5 copy-start.1
  90.1 5.3 %copy-start.3 = (bf16[1024,4,96]{0,2,1:T(8,128)(2,1)S(1)}, bf16[1024,4,96]{0,2,1:T(8,128)(2,1)}, u32[]{:S(2)}) copy-start(bf16[1024,4,96]{0,2,1:T(8,128)(2,1)} %reshape_squeeze.6) | copy-start | bytes 2359300
  95.4 2.3 %copy-start.5 = (pred[640,640]{1,0:T(32,128)(4,1)S(1)}, pred[640,640]{1,0:T(32,128)(4,1)}, u32[]{:S(2)}) copy-start(pred[640,640]{1,0:T(32,128)(4,1)} %compare_and_fusion) | copy-start | bytes 1228804
  95.4 2.7 %copy-start.2 = (bf16[1024,4,96]{0,2,1:T(8,128)(2,1)S(1)}, bf16[1024,4,96]{0,2,1:T(8,128)(2,1)}, u32[]{:S(2)}) copy-start(bf16[1024,4,96]{0,2,1:T(8,128)(2,1)} %reshape_squeeze.7) | copy-start | bytes 2359300
  95.4 2.7 %copy-start.4 = (bf16[640,4,96]{0,2,1:T(8,128)(2,1)S(1)}, bf16[640,4,96]{0,2,1:T(8,128)(2,1)}, u32[]{:S(2)}) copy-start(bf16[640,4,96]{0,2,1:T(8,128)(2,1)} %copy.50) | copy-start | bytes 1474564
  134.4 27.2 %all-to-all-start.1 = ((bf16[128,2,960]{2,1,0:T(2,128)(2,1)}), bf16[128,2,960]{2,1,0:T(2,128)(2,1)}, u32[]{:S(2)}, u32[]{:S(2)}) async-start(bf16[128,2,960]{2,1,0:T(2,128)(2,1)} %reshape.268), calls=%async_computation.1 | async-start | bytes 1048576 | tf_op jit(solution)/shard_map/all_to_all | solution.py:124
  143.9 55.7 %reduce-scatter.2.cloned.1.call-start = ((), (), s32[]{:S(2)}) async-start(), calls=%async_computation.3 | async-start | bytes 1966080 | tf_op jit(solution)/shard_map/reduce_scatter | solution.py:130
  173.6 0.7 copy-start.8
  173.6 26.0 %copy-start.6 = (bf16[256,768]{1,0:T(8,128)(2,1)S(1)}, bf16[256,768]{1,0:T(8,128)(2,1)}, u32[]{:S(2)}) copy-start(bf16[256,768]{1,0:T(8,128)(2,1)} %param.17) | copy-start | bytes 1179652
Sparse Core Ops, SparseCore 0:
  173.8 25.7 reduce-scatter.1

commit v2 on v1

--- a/solution.py
+++ b/solution.py
@@ -8,6 +8,8 @@
 D = 3072
 HEAD_SIZE = 96
 SLOT = 5
+REQ = ("ry", "rz", "rc")
+OUTER = 8
 
 ROPE_BASE = 10000.0
 EPS = 1e-05
@@ -62,6 +64,15 @@
     return heads_out.transpose(1, 0, 2)
 
 
+def two_stage_all_to_all(x):
+    devices = x.shape[0]
+    inner = devices // OUTER
+    x = x.reshape((OUTER, inner) + x.shape[1:])
+    x = lax.all_to_all(x, "ry", split_axis=0, concat_axis=0, tiled=True)
+    x = lax.all_to_all(x, ("rz", "rc"), split_axis=1, concat_axis=1, tiled=True)
+    return x.reshape((devices,) + x.shape[2:])
+
+
 def on_device(
     qkv_rows,
     row_request,
@@ -77,7 +88,7 @@
     parts = qkv_rows.shape[1]
     head_cols = qkv_rows.shape[2]
     heads_here = head_cols // HEAD_SIZE
-    devices = lax.axis_size("req")
+    devices = lax.axis_size(REQ)
     slot_cap = SLOT
     buffer_len = devices * slot_cap
     device_ids = jnp.arange(devices, dtype=jnp.int32)
@@ -100,7 +111,7 @@
     outgoing = jnp.concatenate(
         [slots.reshape(devices, slot_cap * parts, head_cols), count_row], axis=1
     )
-    arrived = lax.all_to_all(outgoing, "req", split_axis=0, concat_axis=0, tiled=True)
+    arrived = two_stage_all_to_all(outgoing)
     arrived_counts = arrived[:, slot_cap * parts, 0].astype(jnp.int32)
 
     length = cached_len[0]
@@ -121,9 +132,7 @@
     visible = jnp.concatenate([cache_ok, new_ok], axis=1)
     grouped = arrived[:, : slot_cap * parts].reshape(buffer_len, parts, heads_here, HEAD_SIZE)
     result = attend_heads(grouped, cache_keys, cache_values, cosine, sine_tab, visible)
-    returned = lax.all_to_all(
-        result.reshape(devices, slot_cap * head_cols), "req", split_axis=0, concat_axis=0, tiled=True
-    )
+    returned = two_stage_all_to_all(result.reshape(devices, slot_cap * parts, head_cols // parts))
     target = owner_dev * slot_cap + slot_in
     attn_rows = returned.reshape(buffer_len, head_cols)[target]
     partial_sum = jnp.dot(attn_rows, out_weight, preferred_element_type=jnp.float32)
@@ -138,20 +147,25 @@
 
 
 def solution(mesh):
+    req_size = mesh.shape["req"]
+    split_mesh = jax.sharding.Mesh(
+        mesh.devices.reshape(OUTER, req_size // OUTER // 2, 2, mesh.shape["tp"]),
+        REQ + ("tp",),
+    )
     return jax.shard_map(
         on_device,
-        mesh=mesh,
+        mesh=split_mesh,
         in_specs=(
-            P("req", None, "tp"),
-            P("req"),
+            P(REQ, None, "tp"),
+            P(REQ),
             P(),
-            P("req"),
-            P("req", None),
-            P("req", None, None, "tp"),
-            P("req", "tp"),
+            P(REQ),
+            P(REQ, None),
+            P(REQ, None, None, "tp"),
+            P(REQ, "tp"),
             P("tp", None),
             P("tp"),
         ),
-        out_specs=(P("req", "tp"), P("req", "tp")),
+        out_specs=(P(REQ, "tp"), P(REQ, "tp")),
         check_vma=False,
     )

time: 221 us -> 257 us (1.16)
  blocking collectives: 9.07 us -> 71.6 us
  starting transfers between devices: 27.4 us -> 14.5 us
  other arithmetic: 34.2 us -> 25.4 us
  local copies, waits for them, and re-layouts: 41.5 us -> 36.8 us
    all_to_all x0 -> x2, blocking collectives: none -> 62.6 us  [two_stage_all_to_all(): x = lax.all_to_all(x, 'ry', split_axis=0, concat_axis=0, tiled=True)]
    all_to_all x2, starting transfers between devices: 27.4 us -> 14.4 us  [two_stage_all_to_all(): x = lax.all_to_all(x, ('rz', 'rc'), split_axis=1, concat_axis=1, tiled=True)]
    all_to_all x2 -> x0, other arithmetic: 8.12 us -> none  [on_device(): lax.all_to_all(result.reshape(devices, slot_cap * head_cols), 'req', spli...]
    unnamed x22 -> x20, local copies, waits for them, and re-layouts: 6.69 us -> 1.83 us
    all_to_all x2, waiting for transfers between devices: 44.4 us -> 40.8 us  [two_stage_all_to_all(): x = lax.all_to_all(x, ('rz', 'rc'), split_axis=1, concat_axis=1, tiled=True)]
    reduce_scatter x1, waiting for transfers between devices: 25.3 us -> 28 us  [on_device(): lax.psum_scatter(partial_sum.astype(jnp.bfloat16), 'tp', scatter_dimensio...]
where the time goes in v2:
time: 257 us; the launch traced here: 255 us
  blocking collectives  71.6 us (28%)
  waiting for transfers between devices  68.7 us (27%)
  local copies, waits for them, and re-layouts  36.8 us (14%)
  other arithmetic  25.4 us (10%)
  matrix products  22.9 us (9%)
  between operations  15 us (6%)
  starting transfers between devices  14.5 us (6%)
    all_to_all x2, blocking collectives, two_stage_all_to_all(): x = lax.all_to_all(x, 'ry', split_axis=0, concat_axis=0, tiled=True)  62.6 us
    all_to_all x2, waiting for transfers between devices, two_stage_all_to_all(): x = lax.all_to_all(x, ('rz', 'rc'), split_axis=1, concat_axis=1, tiled=True)  40.8 us
    reduce_scatter x1, waiting for transfers between devices, on_device(): lax.psum_scatter(partial_sum.astype(jnp.bfloat16), 'tp', scatter_dimensio...  28 us
    all_to_all x2, starting transfers between devices, two_stage_all_to_all(): x = lax.all_to_all(x, ('rz', 'rc'), split_axis=1, concat_axis=1, tiled=True)  14.4 us
    dot_general x4, matrix products, one_head(): jnp.einsum('mk,kd->md', softmax_weights, head_values, preferred_element_t...  10.6 us
    psum x1, blocking collectives, on_device(): square_sum = lax.psum(jnp.sum(hidden * hidden, axis=1), 'tp')  9.07 us
    dot_general x4, matrix products, one_head(): jnp.einsum('md,kd->mk', head_query, head_keys, preferred_element_type=jnp...  8.57 us
  transfers between devices with their start and end apart: 3, of which 3 were waited for; matrix products, arithmetic and copies ran while one was open for 5% of the time, Pallas kernels for 0%

profile of v2, /device:TPU:56, one launch (start us, length us, event | category | flops | bytes accessed | tf_op | source)
XLA Modules:
  0.0 254.9 jit_solution(9583415751893050044)
XLA Ops:
  8.0 1.9 gather_fusion
  10.3 1.7 convolution_convert_fusion.1
  11.9 2.0 copy.62
  14.3 2.0 pad_maximum_fusion
  16.2 41.6 %all_to_all.20 = bf16[8,16,16,384]{3,2,1,0:T(8,128)(2,1)S(1)} all-to-all(bf16[8,16,16,384]{3,2,1,0:T(8,128)(2,1)S(1)} %pad_maximum_fusion), channel_id=1, replica_groups=mesh['ry'=8,'rz'=8,'rc'=2,'tp'=4] {'ry'}, dimensions={0} | all-to-all | bytes 3145728 | tf_op jit(solution)/shard_map/all_to_all | solution.py:71
  57.8 1.4 copy.63
  59.2 10.6 %all-to-all-start.1 = ((bf16[8,16,16,384]{3,2,0,1:T(8,128)(2,1)}), bf16[8,16,16,384]{3,2,0,1:T(8,128)(2,1)}, u32[]{:S(2)}, u32[]{:S(2)}) async-start(bf16[8,16,16,384]{3,2,0,1:T(8,128)(2,1)} %copy.63), calls=%async_computation.1 | async-start | bytes 3145728 | tf_op jit(solution)/shard_map/all_to_all | solution.py:72
  70.5 3.3 %gather_fusion.1 = bf16[8,2,128,384]{3,2,1,0:T(8,128)(2,1)} fusion(bf16[8,2,128,384]{3,2,1,0:T(8,128)(2,1)} %param.16, s32[1024]{0:T(1024)S(1)} %pad_clamp_fusion.1), kind=kCustom, calls=%fused_computation.1 | custom fusion | bytes 3145760 | tf_op jit(solution)/shard_map/gather | solution.py:118
  73.8 2.8 %fusion.31 = (bf16[8,1,128,384]{3,2,1,0:T(8,128)(2,1)}, bf16[8,1,128,384]{3,2,1,0:T(8,128)(2,1)}) fusion(bf16[8,2,128,384]{3,2,1,0:T(8,128)(2,1)} %gather_fusion.1), kind=kLoop, calls=%fused_computation.78 | loop fusion | bytes 3145728 | tf_op jit(solution)/shard_map/slice | solution.py:121
  76.6 1.6 copy.66
  78.2 1.2 reshape_squeeze.6
  79.5 1.6 copy.68
  81.1 1.2 reshape_squeeze.7
  82.3 25.4 %all-to-all-done.1 = bf16[8,16,16,384]{3,2,0,1:T(8,128)(2,1)} async-done(((bf16[8,16,16,384]{3,2,0,1:T(8,128)(2,1)}), bf16[8,16,16,384]{3,2,0,1:T(8,128)(2,1)}, u32[]{:S(2)}, u32[]{:S(2)}) %all-to-all-start.1) | async-done | bytes 1572896 | tf_op jit(solution)/shard_map/all_to_all | solution.py:72
  107.7 1.6 copy.64
  109.3 1.1 copy-done.2
  110.5 2.4 fusion.27
  113.8 4.9 %reshape.231 = bf16[640,3,4,96]{3,2,1,0:T(4,128)(2,1)} reshape(bf16[128,15,384]{2,1,0:T(8,128)(2,1)} %bitcast.88) | data formatting | bytes 2949120 | tf_op jit(solution)/shard_map/reshape | solution.py:133
  118.7 2.7 %slice_bitcast_fusion = (bf16[640,4,96]{2,1,0:T(4,128)(2,1)}, f32[640,4,96]{2,1,0:T(4,128)S(1)}, f32[640,4,96]{2,1,0:T(4,128)S(1)}) fusion(bf16[640,3,4,96]{3,2,1,0:T(4,128)(2,1)} %reshape.231), kind=kLoop, calls=%fused_computation.38 | loop fusion | flops 491520 | bytes 3932160 | tf_op jit(solution)/shard_map/squeeze | solution.py:40
  121.5 1.2 multiply_cosine_fusion
  122.9 1.5 slice_negate_fusion
  124.5 2.7 %fusion.16 = (bf16[640,4,96]{2,1,0:T(4,128)(2,1)S(1)}, bf16[4,640,96]{2,0,1:T(4,128)(2,1)}) fusion(f32[640,4,48]{2,1,0:T(4,128)S(1)} %get-tuple-element.89, f32[640,4,48]{2,1,0:T(4,128)S(1)} %get-tuple-element.88, f32[640,96]{1,0:T(8,128)S(1)} %get-tuple-element.101, f32[640,96]{1,0:T(8,128)S(1)} %get-tuple-element.100, ...), kind=kLoop, calls=%fused_computation.31 | loop fusion | flops 2949120 | bytes 4423680 | tf_op jit(solution)/shard_map/convert_element_type | solution.py:38
  127.1 1.4 copy.67
  128.6 2.1 copy.70
  130.7 1.1 compare_and_fusion
  131.8 2.1 copy.69
  133.9 2.3 maximum_bitcast_fusion
  136.6 1.2 maximum_bitcast_fusion.1
  137.8 22.0 %while.10 = (s32[]{:T(128)}, bf16[4,640,96]{1,2,0:T(8,128)(2,1)}, bf16[4,640,96]{2,1,0:T(8,128)(2,1)}, bf16[4,1664,96]{1,2,0:T(8,128)(2,1)}, pred[640,1664]{1,0:...) while((s32[]{:T(128)}, bf16[4,640,96]{1,2,0:T(8,128)(2,1)}, bf16[4,640,96]{2,1,0:T(8,128)(2,1)}, ...), condition=%wide.region_7.8_spmd, body=%wide.region_4.7_spmd.sunk | while | flops 417524480 | bytes 14785101 | solution.py:56
  137.8 2.1 fusion.39
  140.6 2.6 %fusion.41 = bf16[4,640,96]{1,2,0:T(8,128)(2,1)} fusion(bf16[4,640,96]{1,2,0:T(8,128)(2,1)} %get-tuple-element.151, s32[]{:T(128)} %get-tuple-element.150, f32[640,1664]{1,0:T(8,128)S(1)} %get-tuple-element.141, f32[640]{0:T(1024)S(1)} %fusion.40, f32[640]{0:T(1024)S(1)} %get-tuple-element.142, bf16[4,1664,96]{1,2,0:T(8,128)(2,1)} %get-tuple-element.162), kind=kOutput, calls=%fused_computation.10.clone.1 | convolution fusion | flops 207728640 | bytes 4708352 | tf_op jit(solution)/shard_map/while/body/eval_jaxpr/mk,kd->md/dot_general | solution.py:52
  143.3 2.1 fusion.39
  146.1 2.6 %fusion.41 = bf16[4,640,96]{1,2,0:T(8,128)(2,1)} fusion(bf16[4,640,96]{1,2,0:T(8,128)(2,1)} %get-tuple-element.151, s32[]{:T(128)} %get-tuple-element.150, f32[640,1664]{1,0:T(8,128)S(1)} %get-tuple-element.141, f32[640]{0:T(1024)S(1)} %fusion.40, f32[640]{0:T(1024)S(1)} %get-tuple-element.142, bf16[4,1664,96]{1,2,0:T(8,128)(2,1)} %get-tuple-element.162), kind=kOutput, calls=%fused_computation.10.clone.1 | convolution fusion | flops 207728640 | bytes 4708352 | tf_op jit(solution)/shard_map/while/body/eval_jaxpr/mk,kd->md/dot_general | solution.py:52
  148.8 2.1 fusion.39
  151.6 2.6 %fusion.41 = bf16[4,640,96]{1,2,0:T(8,128)(2,1)} fusion(bf16[4,640,96]{1,2,0:T(8,128)(2,1)} %get-tuple-element.151, s32[]{:T(128)} %get-tuple-element.150, f32[640,1664]{1,0:T(8,128)S(1)} %get-tuple-element.141, f32[640]{0:T(1024)S(1)} %fusion.40, f32[640]{0:T(1024)S(1)} %get-tuple-element.142, bf16[4,1664,96]{1,2,0:T(8,128)(2,1)} %get-tuple-element.162), kind=kOutput, calls=%fused_computation.10.clone.1 | convolution fusion | flops 207728640 | bytes 4708352 | tf_op jit(solution)/shard_map/while/body/eval_jaxpr/mk,kd->md/dot_general | solution.py:52
  154.3 2.1 fusion.39
  157.2 2.6 %fusion.41 = bf16[4,640,96]{1,2,0:T(8,128)(2,1)} fusion(bf16[4,640,96]{1,2,0:T(8,128)(2,1)} %get-tuple-element.151, s32[]{:T(128)} %get-tuple-element.150, f32[640,1664]{1,0:T(8,128)S(1)} %get-tuple-element.141, f32[640]{0:T(1024)S(1)} %fusion.40, f32[640]{0:T(1024)S(1)} %get-tuple-element.142, bf16[4,1664,96]{1,2,0:T(8,128)(2,1)} %get-tuple-element.162), kind=kOutput, calls=%fused_computation.10.clone.1 | convolution fusion | flops 207728640 | bytes 4708352 | tf_op jit(solution)/shard_map/while/body/eval_jaxpr/mk,kd->md/dot_general | solution.py:52
  159.8 1.7 copy.73
  162.2 21.0 %all_to_all.21 = bf16[8,16,15,128]{3,1,2,0:T(8,128)(2,1)S(1)} all-to-all(bf16[8,16,15,128]{3,1,2,0:T(8,128)(2,1)S(1)} %copy.74), channel_id=1, replica_groups=mesh['ry'=8,'rz'=8,'rc'=2,'tp'=4] {'ry'}, dimensions={0} | all-to-all | bytes 983040 | tf_op jit(solution)/shard_map/all_to_all | solution.py:71
  183.2 0.9 copy.75
  184.1 3.8 %all-to-all-start.3 = ((bf16[8,16,15,128]{3,0,2,1:T(8,128)(2,1)}), bf16[8,16,15,128]{3,0,2,1:T(8,128)(2,1)S(1)}, u32[]{:S(2)}, u32[]{:S(2)}) async-start(bf16[8,16,15,128]{3,0,2,1:T(8,128)(2,1)} %copy.75), calls=%async_computation.3 | async-start | bytes 983040 | tf_op jit(solution)/shard_map/all_to_all | solution.py:72
  188.0 15.4 %all-to-all-done.3 = bf16[8,16,15,128]{3,0,2,1:T(8,128)(2,1)S(1)} async-done(((bf16[8,16,15,128]{3,0,2,1:T(8,128)(2,1)}), bf16[8,16,15,128]{3,0,2,1:T(8,128)(2,1)S(1)}, u32[]{:S(2)}, u32[]{:S(2)}) %all-to-all-start.3) | async-done | bytes 491552 | tf_op jit(solution)/shard_map/all_to_all | solution.py:72
  203.8 1.2 gather_fusion.2
  204.9 2.1 convolution_convert_fusion
  207.8 28.0 %reduce-scatter.2.cloned.1.call-done = bf16[256,768]{1,0:T(8,128)(2,1)} async-done(((bf16[256,3072]{1,0:T(8,128)(2,1)}), bf16[256,768]{1,0:T(8,128)(2,1)}) %reduce-scatter.2.cloned.1.call-update) | async-done | bytes 393232 | tf_op jit(solution)/shard_map/reduce_scatter | solution.py:139
  235.7 1.2 multiply_reduce_fusion
  236.9 9.1 %psum.7 = f32[256]{0:T(256)S(1)} all-reduce(f32[256]{0:T(256)S(1)} %multiply_reduce_fusion), channel_id=1, replica_groups=mesh['ry'=8,'rz'=8,'rc'=2,'tp'=4] {'tp'}, use_global_device_ids=true, to_apply=%region_10.11 | all-reduce | flops 256 | bytes 2048 | tf_op jit(solution)/shard_map/psum | solution.py:143
  246.0 2.0 multiply_convert_fusion
  (59 shorter events, 8.0 us)
Async XLA Ops:
  7.2 197.8 %copy-start = (bf16[384,3072]{1,0:T(8,128)(2,1)S(1)}, bf16[384,3072]{1,0:T(8,128)(2,1)}, u32[]{:S(2)}) copy-start(bf16[384,3072]{1,0:T(8,128)(2,1)} %param.18) | copy-start | bytes 7077892
  59.2 11.3 %copy-start.9 = (s32[1,8]{1,0:T(1,128)S(1)}, s32[1,8]{1,0:T(1,128)}, u32[]{:S(2)}) copy-start(s32[1,8]{1,0:T(1,128)} %param.15) | copy-start | bytes 100
  59.2 48.5 %all-to-all-start.1 = ((bf16[8,16,16,384]{3,2,0,1:T(8,128)(2,1)}), bf16[8,16,16,384]{3,2,0,1:T(8,128)(2,1)}, u32[]{:S(2)}, u32[]{:S(2)}) async-start(bf16[8,16,16,384]{3,2,0,1:T(8,128)(2,1)} %copy.63), calls=%async_computation.1 | async-start | bytes 3145728 | tf_op jit(solution)/shard_map/all_to_all | solution.py:72
  109.3 1.1 copy-start.2
  122.9 1.5 copy-start.1
  128.6 5.3 %copy-start.4 = (bf16[1024,4,96]{0,2,1:T(8,128)(2,1)S(1)}, bf16[1024,4,96]{0,2,1:T(8,128)(2,1)}, u32[]{:S(2)}) copy-start(bf16[1024,4,96]{0,2,1:T(8,128)(2,1)} %reshape_squeeze.6) | copy-start | bytes 2359300
  133.9 2.3 copy-start.6
  133.9 2.7 %copy-start.3 = (bf16[1024,4,96]{0,2,1:T(8,128)(2,1)S(1)}, bf16[1024,4,96]{0,2,1:T(8,128)(2,1)}, u32[]{:S(2)}) copy-start(bf16[1024,4,96]{0,2,1:T(8,128)(2,1)} %reshape_squeeze.7) | copy-start | bytes 2359300
  133.9 2.7 %copy-start.5 = (bf16[640,4,96]{0,2,1:T(8,128)(2,1)S(1)}, bf16[640,4,96]{0,2,1:T(8,128)(2,1)}, u32[]{:S(2)}) copy-start(bf16[640,4,96]{0,2,1:T(8,128)(2,1)} %copy.69) | copy-start | bytes 1474564
  184.1 19.3 %all-to-all-start.3 = ((bf16[8,16,15,128]{3,0,2,1:T(8,128)(2,1)}), bf16[8,16,15,128]{3,0,2,1:T(8,128)(2,1)S(1)}, u32[]{:S(2)}, u32[]{:S(2)}) async-start(bf16[8,16,15,128]{3,0,2,1:T(8,128)(2,1)} %copy.75), calls=%async_computation.3 | async-start | bytes 983040 | tf_op jit(solution)/shard_map/all_to_all | solution.py:72
  187.9 47.8 %reduce-scatter.2.cloned.1.call-start = ((), (), s32[]{:S(2)}) async-start(), calls=%async_computation.5 | async-start | bytes 1966080 | tf_op jit(solution)/shard_map/reduce_scatter | solution.py:139
  207.1 0.7 copy-start.8
  207.1 28.6 %copy-start.7 = (bf16[256,768]{1,0:T(8,128)(2,1)S(1)}, bf16[256,768]{1,0:T(8,128)(2,1)}, u32[]{:S(2)}) copy-start(bf16[256,768]{1,0:T(8,128)(2,1)} %param.17) | copy-start | bytes 1179652
Sparse Core Ops, SparseCore 0:
  207.2 28.4 reduce-scatter.1

commit v3 on v1

--- a/solution.py
+++ b/solution.py
@@ -28,38 +28,48 @@
     return field * cosine[:, None, :] + turned * sine_tab[:, None, :]
 
 
-def attend_heads(grouped, cache_keys, cache_values, cosine, sine_tab, visible):
+def turn_matrix(cols):
+    halves = HEAD_SIZE // 2
+    c_in = jnp.arange(cols, dtype=jnp.int32)[:, None]
+    c_out = jnp.arange(cols, dtype=jnp.int32)[None, :]
+    local = c_out % HEAD_SIZE
+    same_head = (c_in // HEAD_SIZE) == (c_out // HEAD_SIZE)
+    low = same_head & (local < halves) & (c_in % HEAD_SIZE == local + halves)
+    high = same_head & (local >= halves) & (c_in % HEAD_SIZE == local - halves)
+    return jnp.where(low, -1.0, jnp.where(high, 1.0, 0.0)).astype(jnp.bfloat16)
+
+
+def rotate_flat(field, cosine, sine_tab, turn):
+    heads = field.shape[1] // HEAD_SIZE
+    turned = jnp.dot(field, turn, preferred_element_type=jnp.float32)
+    cos_all = jnp.tile(cosine, (1, heads))
+    sin_all = jnp.tile(sine_tab, (1, heads))
+    return (field.astype(jnp.float32) * cos_all + turned * sin_all).astype(jnp.bfloat16)
+
+
+def attend_flat(query, keys, values, visible):
     score_scale = 1.0 / math.sqrt(HEAD_SIZE)
-    query_rows_block = rotate(grouped[:, 0].astype(jnp.float32), cosine, sine_tab).astype(
-        jnp.bfloat16
-    )
-    fresh_keys = rotate(grouped[:, 1].astype(jnp.float32), cosine, sine_tab).astype(jnp.bfloat16)
-    gathered_keys = jnp.concatenate([cache_keys, fresh_keys], axis=0)
-    gathered_values = jnp.concatenate([cache_values, grouped[:, 2]], axis=0)
+    cols = query.shape[1]
+    col_head = jnp.arange(cols, dtype=jnp.int32) // HEAD_SIZE
 
-    def one_head(head_parts):
-        head_query, head_keys, head_values = head_parts
+    def one_head(head):
+        chosen = (col_head == head)[None, :]
+        head_query = jnp.where(chosen, query, jnp.zeros_like(query))
         logit_scores = (
-            jnp.einsum("md,kd->mk", head_query, head_keys, preferred_element_type=jnp.float32)
+            jnp.einsum("mc,kc->mk", head_query, keys, preferred_element_type=jnp.float32)
             * score_scale
         )
         logit_scores = jnp.where(visible, logit_scores, -1e30)
         top_score = jnp.max(logit_scores, axis=1, keepdims=True)
         weight = jnp.exp(logit_scores - top_score)
         softmax_weights = (weight / jnp.sum(weight, axis=1, keepdims=True)).astype(jnp.bfloat16)
-        return jnp.einsum(
-            "mk,kd->md", softmax_weights, head_values, preferred_element_type=jnp.float32
+        head_out = jnp.einsum(
+            "mk,kc->mc", softmax_weights, values, preferred_element_type=jnp.float32
         ).astype(jnp.bfloat16)
+        return jnp.where(chosen, head_out, jnp.zeros_like(head_out))
 
-    heads_out = lax.map(
-        one_head,
-        (
-            query_rows_block.transpose(1, 0, 2),
-            gathered_keys.transpose(1, 0, 2),
-            gathered_values.transpose(1, 0, 2),
-        ),
-    )
-    return heads_out.transpose(1, 0, 2)
+    outs = lax.map(one_head, jnp.arange(cols // HEAD_SIZE, dtype=jnp.int32))
+    return jnp.sum(outs, axis=0, dtype=jnp.float32).astype(jnp.bfloat16)
 
 
 def on_device(
@@ -94,7 +104,7 @@
         & (slot_in[None, :, None] == jnp.arange(slot_cap, dtype=jnp.int32)[:, None, None])
     ).astype(jnp.bfloat16)
     slots = jnp.einsum(
-        "jid,ipc->djpc", pick, qkv_rows, preferred_element_type=jnp.float32
+        "jid,ipc->dpjc", pick, qkv_rows, preferred_element_type=jnp.float32
     ).astype(jnp.bfloat16)
     count_row = jnp.broadcast_to(counts.astype(jnp.bfloat16)[:, None, None], (devices, 1, head_cols))
     outgoing = jnp.concatenate(
@@ -106,8 +116,8 @@
     length = cached_len[0]
     pool_pages = kv_pages[page_table[0]]
     cache_span = pool_pages.shape[0] * pool_pages.shape[2]
-    cache_keys = pool_pages[:, 0].reshape(cache_span, heads_here, HEAD_SIZE)
-    cache_values = pool_pages[:, 1].reshape(cache_span, heads_here, HEAD_SIZE)
+    cache_keys = pool_pages[:, 0].reshape(cache_span, head_cols)
+    cache_values = pool_pages[:, 1].reshape(cache_span, head_cols)
     live_slot = (jnp.arange(slot_cap, dtype=jnp.int32)[None, :] < arrived_counts[:, None]).reshape(
         buffer_len
     )
@@ -119,10 +129,22 @@
     )
     new_ok = live_slot[None, :] & (new_rank[None, :] <= new_rank[:, None])
     visible = jnp.concatenate([cache_ok, new_ok], axis=1)
-    grouped = arrived[:, : slot_cap * parts].reshape(buffer_len, parts, heads_here, HEAD_SIZE)
-    result = attend_heads(grouped, cache_keys, cache_values, cosine, sine_tab, visible)
+    part_rows = [
+        arrived[:, p * slot_cap : (p + 1) * slot_cap].reshape(buffer_len, head_cols)
+        for p in range(parts)
+    ]
+    turn = turn_matrix(head_cols)
+    query = rotate_flat(part_rows[0], cosine, sine_tab, turn)
+    fresh_keys = rotate_flat(part_rows[1], cosine, sine_tab, turn)
+    keys = jnp.concatenate([cache_keys, fresh_keys], axis=0)
+    values = jnp.concatenate([cache_values, part_rows[2]], axis=0)
+    result = attend_flat(query, keys, values, visible)
     returned = lax.all_to_all(
-        result.reshape(devices, slot_cap * head_cols), "req", split_axis=0, concat_axis=0, tiled=True
+        result.reshape(devices, slot_cap * parts, head_cols // parts),
+        "req",
+        split_axis=0,
+        concat_axis=0,
+        tiled=True,
     )
     target = owner_dev * slot_cap + slot_in
     attn_rows = returned.reshape(buffer_len, head_cols)[target]

time: 221 us -> 214 us (0.968)
  other arithmetic: 34.2 us -> 23.3 us
  local copies, waits for them, and re-layouts: 41.5 us -> 32.6 us
  matrix products: 21.9 us -> 30.4 us
  waiting for transfers between devices: 69.7 us -> 75.1 us
    dot_general x9 -> x11, matrix products: 19.7 us -> 28.3 us  [the longest x4 12.7 us: one_head(): jnp.einsum('mc,kc->mk', head_query, keys, preferred_element_type=jnp.floa...]
    all_to_all x2 -> x0, other arithmetic: 8.12 us -> none  [on_device(): lax.all_to_all(result.reshape(devices, slot_cap * head_cols), 'req', spli...]
    unnamed x22 -> x36, local copies, waits for them, and re-layouts: 6.69 us -> 1.62 us
    all_to_all x1, waiting for transfers between devices: 26.9 us -> 31.9 us  [on_device(): lax.all_to_all(outgoing, 'req', split_axis=0, concat_axis=0, tiled=True)]
    all_to_all x2 -> x0, local copies, waits for them, and re-layouts: 4.27 us -> none  [on_device(): lax.all_to_all(result.reshape(devices, slot_cap * head_cols), 'req', spli...]
    concatenate x0 -> x2, other arithmetic: none -> 3.76 us  [the longest x1 2.57 us: on_device(): keys = jnp.concatenate([cache_keys, fresh_keys], axis=0)]
    transpose x2 -> x0, other arithmetic: 3.46 us -> none  [the longest x1 2.29 us: attend_heads(): gathered_keys.transpose(1, 0, 2)]
    squeeze x1 -> x0, other arithmetic: 2.67 us -> none  [attend_heads(): gathered_values = jnp.concatenate([cache_values, grouped[:, 2]], axis=0)]
  transfers between devices with their start and end apart: 3 -> 3, of which waited for: 3 -> 3; matrix products, arithmetic and copies ran while one was open for 5% -> 3% of each run, Pallas kernels for 0% -> 0%
where the time goes in v3:
time: 214 us; the launch traced here: 213 us
  waiting for transfers between devices  75.1 us (35%)
  local copies, waits for them, and re-layouts  32.6 us (15%)
  matrix products  30.4 us (14%)
  starting transfers between devices  27.2 us (13%)
  other arithmetic  23.3 us (11%)
  between operations  15 us (7%)
  blocking collectives  9.04 us (4%)
    all_to_all x1, waiting for transfers between devices, on_device(): lax.all_to_all(outgoing, 'req', split_axis=0, concat_axis=0, tiled=True)  31.9 us
    reduce_scatter x1, waiting for transfers between devices, on_device(): lax.psum_scatter(partial_sum.astype(jnp.bfloat16), 'tp', scatter_dimensio...  25.2 us
    all_to_all x1, waiting for transfers between devices, on_device(): lax.all_to_all(result.reshape(devices, slot_cap * parts, head_cols // par...  17.9 us
    all_to_all x1, starting transfers between devices, on_device(): lax.all_to_all(outgoing, 'req', split_axis=0, concat_axis=0, tiled=True)  17.9 us
    dot_general x4, matrix products, one_head(): jnp.einsum('mc,kc->mk', head_query, keys, preferred_element_type=jnp.floa...  12.7 us
    all_to_all x1, starting transfers between devices, on_device(): lax.all_to_all(result.reshape(devices, slot_cap * parts, head_cols // par...  9.28 us
    psum x1, blocking collectives, on_device(): square_sum = lax.psum(jnp.sum(hidden * hidden, axis=1), 'tp')  9.04 us
    dot_general x4, matrix products, one_head(): jnp.einsum('mk,kc->mc', softmax_weights, values, preferred_element_type=j...  8.89 us
  transfers between devices with their start and end apart: 3, of which 3 were waited for; matrix products, arithmetic and copies ran while one was open for 3% of the time, Pallas kernels for 0%

profile of v3, /device:TPU:56, one launch (start us, length us, event | category | flops | bytes accessed | tf_op | source)
XLA Modules:
  0.0 212.7 jit_solution(9554539306171958829)
XLA Ops:
  7.2 0.8 compare_select_fusion.1
  8.0 1.9 gather_fusion
  10.7 1.7 fusion.16
  12.9 2.1 copy.37
  15.0 17.9 %all-to-all-start = ((bf16[128,16,384]{2,1,0:T(8,128)(2,1)}), bf16[128,16,384]{2,1,0:T(8,128)(2,1)}, u32[]{:S(2)}, u32[]{:S(2)}) async-start(bf16[128,16,384]{2,1,0:T(8,128)(2,1)} %copy.37), calls=%async_computation | async-start | bytes 3145728 | tf_op jit(solution)/shard_map/all_to_all | solution.py:113
  33.5 3.4 %gather_fusion.1 = bf16[8,2,128,384]{3,2,1,0:T(8,128)(2,1)} fusion(bf16[8,2,128,384]{3,2,1,0:T(8,128)(2,1)} %param.16, s32[1024]{0:T(1024)S(1)} %pad_clamp_fusion.1), kind=kCustom, calls=%fused_computation.1 | custom fusion | bytes 3145760 | tf_op jit(solution)/shard_map/gather | solution.py:117
  37.6 2.7 %fusion.47 = (bf16[8,1,128,384]{3,2,1,0:T(8,128)(2,1)}, bf16[8,1,128,384]{3,2,1,0:T(8,128)(2,1)}) fusion(bf16[8,2,128,384]{3,2,1,0:T(8,128)(2,1)} %gather_fusion.1), kind=kLoop, calls=%fused_computation.103 | loop fusion | bytes 3145728 | tf_op jit(solution)/shard_map/slice | solution.py:120
  40.3 31.9 %all-to-all-done = bf16[128,16,384]{2,1,0:T(8,128)(2,1)} async-done(((bf16[128,16,384]{2,1,0:T(8,128)(2,1)}), bf16[128,16,384]{2,1,0:T(8,128)(2,1)}, u32[]{:S(2)}, u32[]{:S(2)}) %all-to-all-start) | async-done | bytes 1572896 | tf_op jit(solution)/shard_map/all_to_all | solution.py:113
  72.2 3.3 %fusion.30 = s32[128]{0:T(128)S(1)} fusion(bf16[128,16,384]{2,1,0:T(8,128)(2,1)} %all-to-all-done), kind=kLoop, calls=%fused_computation.63 | loop fusion | flops 128 | bytes 768 | tf_op jit(solution)/shard_map/convert_element_type | solution.py:114
  76.6 0.7 add_convert_fusion
  77.7 0.7 pad_maximum_fusion.3
  78.5 1.3 copy.38
  79.8 1.0 tile.10
  80.8 1.3 copy.39
  82.1 3.4 %fusion.48 = (bf16[128,5,384]{2,1,0:T(8,128)(2,1)S(1)}, bf16[128,5,384]{2,1,0:T(8,128)(2,1)}, bf16[128,5,384]{2,1,0:T(8,128)(2,1)}) fusion(bf16[128,16,384]{2,1,0:T(8,128)(2,1)} %all-to-all-done), kind=kLoop, calls=%fused_computation.104 | loop fusion | bytes 2949120 | tf_op jit(solution)/shard_map/slice | solution.py:133
  85.5 2.1 reshape.322
  87.6 2.1 reshape.320
  89.7 3.5 %fusion.20 = bf16[640,384]{1,0:T(8,128)(2,1)} fusion(f32[640,384]{1,0:T(8,128)} %copy.39, bf16[640,384]{1,0:T(8,128)(2,1)} %reshape.322, f32[640,384]{1,0:T(8,128)} %copy.38, s32[384]{0:T(512)S(1)} %get-tuple-element.94, s32[384]{0:T(512)S(1)} %get-tuple-element.95, s32[384]{0:T(512)S(1)} %get-tuple-element.93, s32[384]{0:T(512)S(1)} %get-tuple-element.92, ...), kind=kOutput, calls=%fused_computation.36 | convolution fusion | flops 191447040 | bytes 2956032 | tf_op jit(solution)/shard_map/dot_general | solution.py:44
  93.2 1.6 fusion.19
  95.1 1.0 reshape.323
  96.1 2.6 %pad_maximum_fusion.1 = bf16[1664,384]{1,0:T(8,128)(2,1)} fusion(bf16[640,384]{1,0:T(8,128)(2,1)} %fusion.20, bf16[1024,384]{1,0:T(8,128)(2,1)} %bitcast.50), kind=kLoop, calls=%fused_computation.37 | loop fusion | flops 2555904 | bytes 2555904 | tf_op jit(solution)/shard_map/concatenate | solution.py:139
  98.7 1.4 pad_add_fusion
  100.1 1.2 pad_maximum_fusion.2
  101.7 31.8 %while.11 = (s32[]{:T(128)}, bf16[4,640,384]{2,1,0:T(8,128)(2,1)}, s32[4]{0:T(128)S(1)}, bf16[640,384]{1,0:T(8,128)(2,1)}, bf16[1664,384]{1,0:T(8,128)(2,1)}, /*...) while((s32[]{:T(128)}, bf16[4,640,384]{2,1,0:T(8,128)(2,1)}, ...), condition=%wide.region_7.8_spmd.clone, body=%wide.region_4.7_spmd.clone.sunk | while | flops 1645037696 | bytes 22509824 | solution.py:71
  102.3 0.7 fusion.63
  103.0 3.2 %fusion.64 = (f32[640]{0:T(1024)S(1)}, f32[640,1664]{1,0:T(8,128)S(1)}) fusion(pred[640,1664]{1,0:T(32,128)(4,1)S(1)} %get-tuple-element.166, bf16[1664,384]{1,0:T(8,128)(2,1)} %get-tuple-element.165, bf16[640,384]{1,0:T(8,128)(2,1)} %get-tuple-element.164, pred[384]{0:T(512)(128)(4,1)S(1)} %fusion.63), kind=kOutput, calls=%fused_computation.102.clone.1 | convolution fusion | flops 821329280 | bytes 7097216 | tf_op jit(solution)/shard_map/while/body/eval_jaxpr/mc,kc->mk/dot_general | solution.py:59
  106.2 0.7 fusion.65
  107.5 2.2 %fusion.66 = bf16[4,640,384]{2,1,0:T(8,128)(2,1)} fusion(bf16[4,640,384]{2,1,0:T(8,128)(2,1)} %get-tuple-element.154, s32[]{:T(128)} %get-tuple-element.153, bf16[1664,384]{1,0:T(8,128)(2,1)S(1)} %copy-done.4, f32[640,1664]{1,0:T(8,128)S(1)} %get-tuple-element.143, f32[640]{0:T(1024)S(1)} %fusion.65, f32[640]{0:T(1024)S(1)} %get-tuple-element.144, ...), kind=kOutput, calls=%fused_computation.12.clone.1 | convolution fusion | flops 821575680 | bytes 6035328 | tf_op jit(solution)/shard_map/while/body/eval_jaxpr/mk,kc->mc/dot_general | solution.py:66
  110.9 3.2 %fusion.64 = (f32[640]{0:T(1024)S(1)}, f32[640,1664]{1,0:T(8,128)S(1)}) fusion(pred[640,1664]{1,0:T(32,128)(4,1)S(1)} %get-tuple-element.166, bf16[1664,384]{1,0:T(8,128)(2,1)} %get-tuple-element.165, bf16[640,384]{1,0:T(8,128)(2,1)} %get-tuple-element.164, pred[384]{0:T(512)(128)(4,1)S(1)} %fusion.63), kind=kOutput, calls=%fused_computation.102.clone.1 | convolution fusion | flops 821329280 | bytes 7097216 | tf_op jit(solution)/shard_map/while/body/eval_jaxpr/mc,kc->mk/dot_general | solution.py:59
  114.1 0.7 fusion.65
  115.4 2.2 %fusion.66 = bf16[4,640,384]{2,1,0:T(8,128)(2,1)} fusion(bf16[4,640,384]{2,1,0:T(8,128)(2,1)} %get-tuple-element.154, s32[]{:T(128)} %get-tuple-element.153, bf16[1664,384]{1,0:T(8,128)(2,1)S(1)} %copy-done.4, f32[640,1664]{1,0:T(8,128)S(1)} %get-tuple-element.143, f32[640]{0:T(1024)S(1)} %fusion.65, f32[640]{0:T(1024)S(1)} %get-tuple-element.144, ...), kind=kOutput, calls=%fused_computation.12.clone.1 | convolution fusion | flops 821575680 | bytes 6035328 | tf_op jit(solution)/shard_map/while/body/eval_jaxpr/mk,kc->mc/dot_general | solution.py:66
  118.2 0.7 fusion.63
  118.9 3.2 %fusion.64 = (f32[640]{0:T(1024)S(1)}, f32[640,1664]{1,0:T(8,128)S(1)}) fusion(pred[640,1664]{1,0:T(32,128)(4,1)S(1)} %get-tuple-element.166, bf16[1664,384]{1,0:T(8,128)(2,1)} %get-tuple-element.165, bf16[640,384]{1,0:T(8,128)(2,1)} %get-tuple-element.164, pred[384]{0:T(512)(128)(4,1)S(1)} %fusion.63), kind=kOutput, calls=%fused_computation.102.clone.1 | convolution fusion | flops 821329280 | bytes 7097216 | tf_op jit(solution)/shard_map/while/body/eval_jaxpr/mc,kc->mk/dot_general | solution.py:59
  122.0 0.7 fusion.65
  123.3 2.2 %fusion.66 = bf16[4,640,384]{2,1,0:T(8,128)(2,1)} fusion(bf16[4,640,384]{2,1,0:T(8,128)(2,1)} %get-tuple-element.154, s32[]{:T(128)} %get-tuple-element.153, bf16[1664,384]{1,0:T(8,128)(2,1)S(1)} %copy-done.4, f32[640,1664]{1,0:T(8,128)S(1)} %get-tuple-element.143, f32[640]{0:T(1024)S(1)} %fusion.65, f32[640]{0:T(1024)S(1)} %get-tuple-element.144, ...), kind=kOutput, calls=%fused_computation.12.clone.1 | convolution fusion | flops 821575680 | bytes 6035328 | tf_op jit(solution)/shard_map/while/body/eval_jaxpr/mk,kc->mc/dot_general | solution.py:66
  126.8 3.2 %fusion.64 = (f32[640]{0:T(1024)S(1)}, f32[640,1664]{1,0:T(8,128)S(1)}) fusion(pred[640,1664]{1,0:T(32,128)(4,1)S(1)} %get-tuple-element.166, bf16[1664,384]{1,0:T(8,128)(2,1)} %get-tuple-element.165, bf16[640,384]{1,0:T(8,128)(2,1)} %get-tuple-element.164, pred[384]{0:T(512)(128)(4,1)S(1)} %fusion.63), kind=kOutput, calls=%fused_computation.102.clone.1 | convolution fusion | flops 821329280 | bytes 7097216 | tf_op jit(solution)/shard_map/while/body/eval_jaxpr/mc,kc->mk/dot_general | solution.py:59
  130.0 0.7 fusion.65
  131.3 2.2 %fusion.66 = bf16[4,640,384]{2,1,0:T(8,128)(2,1)} fusion(bf16[4,640,384]{2,1,0:T(8,128)(2,1)} %get-tuple-element.154, s32[]{:T(128)} %get-tuple-element.153, bf16[1664,384]{1,0:T(8,128)(2,1)S(1)} %copy-done.4, f32[640,1664]{1,0:T(8,128)S(1)} %get-tuple-element.143, f32[640]{0:T(1024)S(1)} %fusion.65, f32[640]{0:T(1024)S(1)} %get-tuple-element.144, ...), kind=kOutput, calls=%fused_computation.12.clone.1 | convolution fusion | flops 821575680 | bytes 6035328 | tf_op jit(solution)/shard_map/while/body/eval_jaxpr/mk,kc->mc/dot_general | solution.py:66
  133.5 2.1 reduce_sum.50
  135.6 1.1 reshape.324
  136.7 9.3 %all-to-all-start.1 = ((bf16[128,15,128]{2,1,0:T(8,128)(2,1)}), bf16[128,15,128]{2,1,0:T(8,128)(2,1)S(1)}, u32[]{:S(2)}, u32[]{:S(2)}) async-start(bf16[128,15,128]{2,1,0:T(8,128)(2,1)} %reshape.324), calls=%async_computation.1 | async-start | bytes 1048576 | tf_op jit(solution)/shard_map/all_to_all | solution.py:142
  146.1 17.9 %all-to-all-done.1 = bf16[128,15,128]{2,1,0:T(8,128)(2,1)S(1)} async-done(((bf16[128,15,128]{2,1,0:T(8,128)(2,1)}), bf16[128,15,128]{2,1,0:T(8,128)(2,1)S(1)}, u32[]{:S(2)}, u32[]{:S(2)}) %all-to-all-start.1) | async-done | bytes 491552 | tf_op jit(solution)/shard_map/all_to_all | solution.py:142
  164.3 1.2 gather_fusion.2
  165.4 2.2 %convolution_convert_fusion = bf16[256,3072]{1,0:T(8,128)(2,1)} fusion(bf16[256,384]{1,0:T(8,128)(2,1)S(1)} %gather_fusion.2, bf16[384,3072]{1,0:T(8,128)(2,1)S(1)} %copy-done), kind=kOutput, calls=%fused_computation.26 | convolution fusion | flops 604766208 | bytes 4128768 | tf_op jit(solution)/shard_map/dot_general | solution.py:151
  168.3 25.2 %reduce-scatter.2.cloned.1.call-done = bf16[256,768]{1,0:T(8,128)(2,1)} async-done(((bf16[256,3072]{1,0:T(8,128)(2,1)}), bf16[256,768]{1,0:T(8,128)(2,1)}) %reduce-scatter.2.cloned.1.call-update) | async-done | bytes 393232 | tf_op jit(solution)/shard_map/reduce_scatter | solution.py:152
  193.5 1.2 multiply_reduce_fusion
  194.7 9.0 %psum.7 = f32[256]{0:T(256)S(1)} all-reduce(f32[256]{0:T(256)S(1)} %multiply_reduce_fusion), channel_id=1, replica_groups=mesh['req'=128,'tp'=4] {'tp'}, use_global_device_ids=true, to_apply=%region_11.12 | all-reduce | flops 256 | bytes 2048 | tf_op jit(solution)/shard_map/psum | solution.py:156
  203.8 2.0 multiply_convert_fusion
  (87 shorter events, 11.3 us)
Async XLA Ops:
  7.2 158.3 %copy-start = (bf16[384,3072]{1,0:T(8,128)(2,1)S(1)}, bf16[384,3072]{1,0:T(8,128)(2,1)}, u32[]{:S(2)}) copy-start(bf16[384,3072]{1,0:T(8,128)(2,1)} %param.18) | copy-start | bytes 7077892
  9.9 2.7 %copy-start.10 = (s32[256]{0:T(256)}, s32[256]{0:T(256)S(1)}, u32[]{:S(2)}) copy-start(s32[256]{0:T(256)S(1)} %gather_fusion) | copy-start | bytes 3076
  10.1 0.6 copy-start.14
  15.0 18.5 %copy-start.18 = (s32[1,8]{1,0:T(1,128)S(1)}, s32[1,8]{1,0:T(1,128)}, u32[]{:S(2)}) copy-start(s32[1,8]{1,0:T(1,128)} %param.15) | copy-start | bytes 100
  15.0 57.3 %all-to-all-start = ((bf16[128,16,384]{2,1,0:T(8,128)(2,1)}), bf16[128,16,384]{2,1,0:T(8,128)(2,1)}, u32[]{:S(2)}, u32[]{:S(2)}) async-start(bf16[128,16,384]{2,1,0:T(8,128)(2,1)} %copy.37), calls=%async_computation | async-start | bytes 3145728 | tf_op jit(solution)/shard_map/all_to_all | solution.py:113
  76.6 1.9 copy-start.12
  89.7 3.5 %copy-start.6 = (f32[640,384]{1,0:T(8,128)S(1)}, f32[640,384]{1,0:T(8,128)}, u32[]{:S(2)}) copy-start(f32[640,384]{1,0:T(8,128)} %copy.38) | copy-start | bytes 2949124
  89.7 3.5 %copy-start.7 = (f32[640,384]{1,0:T(8,128)S(1)}, f32[640,384]{1,0:T(8,128)}, u32[]{:S(2)}) copy-start(f32[640,384]{1,0:T(8,128)} %copy.39) | copy-start | bytes 2949124
  89.7 3.5 %copy-start.8 = (bf16[640,384]{1,0:T(8,128)(2,1)S(1)}, bf16[640,384]{1,0:T(8,128)(2,1)}, u32[]{:S(2)}) copy-start(bf16[640,384]{1,0:T(8,128)(2,1)} %reshape.320) | copy-start | bytes 1474564
  93.2 1.6 copy-start.9
  93.2 1.6 copy-start.13
  96.1 2.6 %copy-start.16 = (pred[1664]{0:T(1024)(128)(4,1)S(1)}, pred[1664]{0:T(1024)(128)(4,1)}, u32[]{:S(2)}) copy-start(pred[1664]{0:T(1024)(128)(4,1)} %pad.2.clone) | copy-start | bytes 4996
  96.1 4.0 %copy-start.1 = (bf16[8,1,128,384]{3,2,1,0:T(8,128)(2,1)S(1)}, bf16[8,1,128,384]{3,2,1,0:T(8,128)(2,1)}, u32[]{:S(2)}) copy-start(bf16[8,1,128,384]{3,2,1,0:T(8,128)(2,1)} %get-tuple-element.79) | copy-start | bytes 2359300
  96.1 4.0 %copy-start.2 = (bf16[640,384]{1,0:T(8,128)(2,1)S(1)}, bf16[640,384]{1,0:T(8,128)(2,1)}, u32[]{:S(2)}) copy-start(bf16[640,384]{1,0:T(8,128)(2,1)} %reshape.323) | copy-start | bytes 1474564
  100.1 1.7 copy-start.5
  106.1 1.3 copy-start.4
  114.1 1.3 copy-start.4
  122.0 1.3 copy-start.4
  130.0 1.3 copy-start.4
  135.6 10.4 %copy-start.11 = (s32[256]{0:T(256)S(1)}, s32[256]{0:T(256)}, u32[]{:S(2)}) copy-start(s32[256]{0:T(256)} %copy-done.10) | copy-start | bytes 3076
  135.6 10.4 %copy-start.15 = (s32[256]{0:T(256)S(1)}, s32[256]{0:T(256)}, u32[]{:S(2)}) copy-start(s32[256]{0:T(256)} %copy-done.14) | copy-start | bytes 3076
  136.7 27.3 %all-to-all-start.1 = ((bf16[128,15,128]{2,1,0:T(8,128)(2,1)}), bf16[128,15,128]{2,1,0:T(8,128)(2,1)S(1)}, u32[]{:S(2)}, u32[]{:S(2)}) async-start(bf16[128,15,128]{2,1,0:T(8,128)(2,1)} %reshape.324), calls=%async_computation.1 | async-start | bytes 1048576 | tf_op jit(solution)/shard_map/all_to_all | solution.py:142
  146.0 47.5 %reduce-scatter.2.cloned.1.call-start = ((), (), s32[]{:S(2)}) async-start(), calls=%async_computation.3 | async-start | bytes 1966080 | tf_op jit(solution)/shard_map/reduce_scatter | solution.py:152
  167.6 0.7 copy-start.17
  167.6 25.9 %copy-start.3 = (bf16[256,768]{1,0:T(8,128)(2,1)S(1)}, bf16[256,768]{1,0:T(8,128)(2,1)}, u32[]{:S(2)}) copy-start(bf16[256,768]{1,0:T(8,128)(2,1)} %param.17) | copy-start | bytes 1179652
Sparse Core Ops, SparseCore 0:
  167.7 25.7 reduce-scatter.1

commit v4 on v3

--- a/solution.py
+++ b/solution.py
@@ -3,6 +3,8 @@
 import jax
 import jax.numpy as jnp
 from jax import lax
+from jax.experimental import pallas as pl
+from jax.experimental.pallas import tpu as pltpu
 from jax.sharding import PartitionSpec as P
 
 D = 3072
@@ -47,29 +49,66 @@
     return (field.astype(jnp.float32) * cos_all + turned * sin_all).astype(jnp.bfloat16)
 
 
-def attend_flat(query, keys, values, visible):
+ROW_BLOCK = 128
+
+
+def attend_kernel(q_ref, kc_ref, vc_ref, kn_ref, vn_ref, qrank_ref, cache_ok_ref, krank_ref, o_ref):
     score_scale = 1.0 / math.sqrt(HEAD_SIZE)
+    query = q_ref[...]
     cols = query.shape[1]
-    col_head = jnp.arange(cols, dtype=jnp.int32) // HEAD_SIZE
-
-    def one_head(head):
-        chosen = (col_head == head)[None, :]
+    col_head = lax.broadcasted_iota(jnp.int32, (1, cols), 1) // HEAD_SIZE
+    cache_ok = cache_ok_ref[...] > 0
+    new_ok = krank_ref[...] <= qrank_ref[...]
+    contract = (((1,), (1,)), ((), ()))
+    total = jnp.zeros(o_ref.shape, jnp.float32)
+    for head in range(cols // HEAD_SIZE):
+        chosen = col_head == head
         head_query = jnp.where(chosen, query, jnp.zeros_like(query))
-        logit_scores = (
-            jnp.einsum("mc,kc->mk", head_query, keys, preferred_element_type=jnp.float32)
-            * score_scale
+        score_c = lax.dot_general(
+            head_query, kc_ref[...], contract, preferred_element_type=jnp.float32
+        ) * score_scale
+        score_n = lax.dot_general(
+            head_query, kn_ref[...], contract, preferred_element_type=jnp.float32
+        ) * score_scale
+        score_c = jnp.where(cache_ok, score_c, -1e30)
+        score_n = jnp.where(new_ok, score_n, -1e30)
+        top = jnp.maximum(
+            jnp.max(score_c, axis=1, keepdims=True), jnp.max(score_n, axis=1, keepdims=True)
         )
-        logit_scores = jnp.where(visible, logit_scores, -1e30)
-        top_score = jnp.max(logit_scores, axis=1, keepdims=True)
-        weight = jnp.exp(logit_scores - top_score)
-        softmax_weights = (weight / jnp.sum(weight, axis=1, keepdims=True)).astype(jnp.bfloat16)
-        head_out = jnp.einsum(
-            "mk,kc->mc", softmax_weights, values, preferred_element_type=jnp.float32
-        ).astype(jnp.bfloat16)
-        return jnp.where(chosen, head_out, jnp.zeros_like(head_out))
-
-    outs = lax.map(one_head, jnp.arange(cols // HEAD_SIZE, dtype=jnp.int32))
-    return jnp.sum(outs, axis=0, dtype=jnp.float32).astype(jnp.bfloat16)
+        weight_c = jnp.exp(score_c - top)
+        weight_n = jnp.exp(score_n - top)
+        whole = jnp.sum(weight_c, axis=1, keepdims=True) + jnp.sum(weight_n, axis=1, keepdims=True)
+        prob_c = (weight_c / whole).astype(jnp.bfloat16)
+        prob_n = (weight_n / whole).astype(jnp.bfloat16)
+        head_out = jnp.dot(prob_c, vc_ref[...], preferred_element_type=jnp.float32) + jnp.dot(
+            prob_n, vn_ref[...], preferred_element_type=jnp.float32
+        )
+        head_out = head_out.astype(jnp.bfloat16).astype(jnp.float32)
+        total = total + jnp.where(chosen, head_out, 0.0)
+    o_ref[...] = total.astype(o_ref.dtype)
+
+
+def attend_flat(query, cache_keys, cache_values, fresh_keys, fresh_values, q_rank, cache_ok, k_rank):
+    rows, cols = query.shape
+    span = cache_keys.shape[0]
+    whole = lambda i: (0, 0)
+    block = ROW_BLOCK if rows % ROW_BLOCK == 0 else rows
+    return pl.pallas_call(
+        attend_kernel,
+        out_shape=jax.ShapeDtypeStruct((rows, cols), jnp.bfloat16),
+        grid=(rows // block,),
+        in_specs=[
+            pl.BlockSpec((block, cols), lambda i: (i, 0)),
+            pl.BlockSpec((span, cols), whole),
+            pl.BlockSpec((span, cols), whole),
+            pl.BlockSpec((rows, cols), whole),
+            pl.BlockSpec((rows, cols), whole),
+            pl.BlockSpec((block, 1), lambda i: (i, 0)),
+            pl.BlockSpec((1, span), whole),
+            pl.BlockSpec((1, rows), whole),
+        ],
+        out_specs=pl.BlockSpec((block, cols), lambda i: (i, 0)),
+    )(query, cache_keys, cache_values, fresh_keys, fresh_values, q_rank, cache_ok, k_rank)
 
 
 def on_device(
@@ -124,11 +163,9 @@
     live_int = live_slot.astype(jnp.int32)
     new_rank = jnp.cumsum(live_int) - live_int
     cosine, sine_tab = rope_tables(length + new_rank)
-    cache_ok = jnp.broadcast_to(
-        (jnp.arange(cache_span, dtype=jnp.int32) < length)[None, :], (buffer_len, cache_span)
-    )
-    new_ok = live_slot[None, :] & (new_rank[None, :] <= new_rank[:, None])
-    visible = jnp.concatenate([cache_ok, new_ok], axis=1)
+    cache_ok = (jnp.arange(cache_span, dtype=jnp.int32) < length).astype(jnp.int32)[None, :]
+    k_rank = jnp.where(live_slot, new_rank, jnp.int32(2**30))[None, :]
+    q_rank = new_rank[:, None]
     part_rows = [
         arrived[:, p * slot_cap : (p + 1) * slot_cap].reshape(buffer_len, head_cols)
         for p in range(parts)
@@ -136,9 +173,9 @@
     turn = turn_matrix(head_cols)
     query = rotate_flat(part_rows[0], cosine, sine_tab, turn)
     fresh_keys = rotate_flat(part_rows[1], cosine, sine_tab, turn)
-    keys = jnp.concatenate([cache_keys, fresh_keys], axis=0)
-    values = jnp.concatenate([cache_values, part_rows[2]], axis=0)
-    result = attend_flat(query, keys, values, visible)
+    result = attend_flat(
+        query, cache_keys, cache_values, fresh_keys, part_rows[2], q_rank, cache_ok, k_rank
+    )
     returned = lax.all_to_all(
         result.reshape(devices, slot_cap * parts, head_cols // parts),
         "req",

time: 214 us -> 199 us (0.930)
  Pallas kernels: 0 us -> 23.1 us
  matrix products: 30.4 us -> 8.86 us
  other arithmetic: 23.3 us -> 11 us
  local copies, waits for them, and re-layouts: 32.6 us -> 28.7 us
    pallas_call x0 -> x1, Pallas kernels: none -> 23.1 us  [attend_flat(): pl.pallas_call(attend_kernel, out_shape=jax.ShapeDtypeStruct((rows, cols)...]
    dot_general x8 -> x0, matrix products: 21.5 us -> none  [the longest x4 12.7 us: one_head(): jnp.einsum('mc,kc->mk', head_query, keys, preferred_element_type=jnp.floa...]
    concatenate x3 -> x0, other arithmetic: 5.12 us -> none  [the longest x1 2.57 us: on_device(): keys = jnp.concatenate([cache_keys, fresh_keys], axis=0)]
    reduce_sum x5 -> x0, other arithmetic: 4.94 us -> none  [the longest x4 2.86 us: one_head(): jnp.sum(weight, axis=1, keepdims=True)]
    eq x4 -> x0, other arithmetic: 2.63 us -> none  [one_head(): chosen = (col_head == head)[None, :]]
    while x8 -> x0, local copies, waits for them, and re-layouts: 2.34 us -> none
    dynamic_slice x4 -> x0, local copies, waits for them, and re-layouts: 2.33 us -> none  [attend_flat(): outs = lax.map(one_head, jnp.arange(cols // HEAD_SIZE, dtype=jnp.int32))]
where the time goes in v4:
time: 199 us; the launch traced here: 198 us
  waiting for transfers between devices  75.1 us (38%)
  local copies, waits for them, and re-layouts  28.7 us (14%)
  starting transfers between devices  27 us (14%)
  Pallas kernels  23.1 us (12%)
  between operations  14.9 us (7%)
  other arithmetic  11 us (6%)
  blocking collectives  9.06 us (5%)
  matrix products  8.86 us (4%)
    all_to_all x1, waiting for transfers between devices, on_device(): lax.all_to_all(outgoing, 'req', split_axis=0, concat_axis=0, tiled=True)  32 us
    reduce_scatter x1, waiting for transfers between devices, on_device(): lax.psum_scatter(partial_sum.astype(jnp.bfloat16), 'tp', scatter_dimensio...  25.2 us
    pallas_call x1, Pallas kernels, attend_flat(): pl.pallas_call(attend_kernel, out_shape=jax.ShapeDtypeStruct((rows, cols)...  23.1 us
    all_to_all x1, waiting for transfers between devices, on_device(): lax.all_to_all(result.reshape(devices, slot_cap * parts, head_cols // par...  17.9 us
    all_to_all x1, starting transfers between devices, on_device(): lax.all_to_all(outgoing, 'req', split_axis=0, concat_axis=0, tiled=True)  17.9 us
    psum x1, blocking collectives, on_device(): square_sum = lax.psum(jnp.sum(hidden * hidden, axis=1), 'tp')  9.06 us
    all_to_all x1, starting transfers between devices, on_device(): lax.all_to_all(result.reshape(devices, slot_cap * parts, head_cols // par...  9.04 us
    reshape x3, local copies, waits for them, and re-layouts, on_device(): arrived[:, p * slot_cap:(p + 1) * slot_cap].reshape(buffer_len, head_cols)  5.11 us
  transfers between devices with their start and end apart: 3, of which 3 were waited for; matrix products, arithmetic and copies ran while one was open for 3% of the time, Pallas kernels for 0%

profile of v4, /device:TPU:56, one launch (start us, length us, event | category | flops | bytes accessed | tf_op | source)
XLA Modules:
  0.0 197.6 jit_solution(9546850972373486306)
XLA Ops:
  7.2 0.8 compare_select_fusion.1
  8.0 1.9 gather_fusion
  9.9 0.1 convert_reduce_fusion.1
  10.0 0.2 convert_reduce_fusion
  10.3 1.7 fusion
  11.9 0.2 copy.50
  12.2 0.1 broadcast_in_dim.17
  12.2 0.2 pad_maximum_fusion
  12.4 2.1 %copy.51 = bf16[128,16,384]{2,1,0:T(8,128)(2,1)} copy(bf16[128,16,384]{2,0,1:T(8,128)(2,1)S(1)} %pad_maximum_fusion) | data formatting | bytes 3145728 | tf_op jit(solution)/shard_map/concatenate | solution.py:149
  14.5 17.9 %all-to-all-start = ((bf16[128,16,384]{2,1,0:T(8,128)(2,1)}), bf16[128,16,384]{2,1,0:T(8,128)(2,1)}, u32[]{:S(2)}, u32[]{:S(2)}) async-start(bf16[128,16,384]{2,1,0:T(8,128)(2,1)} %copy.51), calls=%async_computation | async-start | bytes 3145728 | tf_op jit(solution)/shard_map/all_to_all | solution.py:152
  33.1 3.3 %gather_fusion.1 = bf16[8,2,128,384]{3,2,1,0:T(8,128)(2,1)} fusion(bf16[8,2,128,384]{3,2,1,0:T(8,128)(2,1)} %param.14, s32[1024]{0:T(1024)S(1)} %pad_clamp_fusion.1), kind=kCustom, calls=%fused_computation.1 | custom fusion | bytes 3145760 | tf_op jit(solution)/shard_map/gather | solution.py:156
  36.4 0.6 compare_convert_fusion.cache_ok_ref
  37.0 2.8 %fusion.34 = (bf16[8,1,128,384]{3,2,1,0:T(8,128)(2,1)}, bf16[8,1,128,384]{3,2,1,0:T(8,128)(2,1)}) fusion(bf16[8,2,128,384]{3,2,1,0:T(8,128)(2,1)} %gather_fusion.1), kind=kLoop, calls=%fused_computation.82 | loop fusion | bytes 3145728 | tf_op jit(solution)/shard_map/slice | solution.py:159
  39.8 32.0 %all-to-all-done = bf16[128,16,384]{2,1,0:T(8,128)(2,1)} async-done(((bf16[128,16,384]{2,1,0:T(8,128)(2,1)}), bf16[128,16,384]{2,1,0:T(8,128)(2,1)}, u32[]{:S(2)}, u32[]{:S(2)}) %all-to-all-start) | async-done | bytes 1572896 | tf_op jit(solution)/shard_map/all_to_all | solution.py:152
  71.8 3.3 %fusion.14 = s32[128]{0:T(128)S(1)} fusion(bf16[128,16,384]{2,1,0:T(8,128)(2,1)} %all-to-all-done), kind=kLoop, calls=%fused_computation.37 | loop fusion | flops 128 | bytes 768 | tf_op jit(solution)/shard_map/convert_element_type | solution.py:153
  75.1 0.1 iota_compare_fusion.2
  75.2 0.2 reshape.371
  75.4 0.2 reshape.370
  75.6 0.2 reshape.369
  75.8 0.2 lt.123
  76.0 0.3 reduce-window.9
  76.3 0.1 slice.27
  76.4 0.1 slice_reduce_fusion
  76.6 0.6 fusion.21.krank_ref
  77.2 0.9 copy.56.qrank_ref
  78.2 0.5 multiply_cosine_fusion
  78.7 0.7 pad_maximum_fusion.1
  79.5 1.3 copy.52
  80.7 3.5 %fusion.33 = (bf16[128,5,384]{2,1,0:T(8,128)(2,1)}, bf16[128,5,384]{2,1,0:T(8,128)(2,1)}, bf16[128,5,384]{2,1,0:T(8,128)(2,1)S(1)}) fusion(bf16[128,16,384]{2,1,0:T(8,128)(2,1)} %all-to-all-done), kind=kLoop, calls=%fused_computation.81 | loop fusion | bytes 2949120 | tf_op jit(solution)/shard_map/slice | solution.py:170
  84.2 2.1 %reshape.365.vn_ref = bf16[640,384]{1,0:T(8,128)(2,1)} reshape(bf16[128,5,384]{2,1,0:T(8,128)(2,1)} %get-tuple-element.2) | data formatting | bytes 983040 | tf_op jit(solution)/shard_map/reshape | solution.py:170
  86.3 2.1 %reshape.364 = bf16[640,384]{1,0:T(8,128)(2,1)} reshape(bf16[128,5,384]{2,1,0:T(8,128)(2,1)} %get-tuple-element.3) | data formatting | bytes 983040 | tf_op jit(solution)/shard_map/reshape | solution.py:170
  88.3 1.0 reshape.362
  89.3 1.0 tile.10
  90.3 1.3 copy.53
  91.6 3.5 %fusion.4.kn_ref = bf16[640,384]{1,0:T(8,128)(2,1)} fusion(f32[640,384]{1,0:T(8,128)} %copy.53, bf16[640,384]{1,0:T(8,128)(2,1)} %reshape.364, f32[640,384]{1,0:T(8,128)} %copy.52, s32[384]{0:T(512)S(1)} %get-tuple-element.17, s32[384]{0:T(512)S(1)} %get-tuple-element.18, s32[384]{0:T(512)S(1)} %get-tuple-element.16, s32[384]{0:T(512)S(1)} %get-tuple-element.15, ...), kind=kOutput, calls=%fused_computation.12 | convolution fusion | flops 191447040 | bytes 2956032 | tf_op jit(solution)/shard_map/dot_general | solution.py:46
  95.1 1.6 fusion.3.q_ref
  96.7 23.1 %shard_map.104 = bf16[640,384]{1,0:T(8,128)(2,1)} custom-call(bf16[640,384]{1,0:T(8,128)(2,1)} %fusion.3.q_ref, bf16[1024,384]{1,0:T(8,128)(2,1)} %bitcast.50, bf16[1024,384]{1,0:T(8,128)(2,1)} %bitcast.49, bf16[640,384]{1,0:T(8,128)(2,1)} %fusion.4.kn_ref, bf16[640,384]{1,0:T(8,128)(2,1)} %reshape.365.vn_ref, s32[640,1]{1,0:T(8,128)} %copy.56.qrank_ref, ...), custom_call_target="tpu_custom_call" | custom-call | tf_op jit(solution)/shard_map/pallas_call | solution.py:96
  119.8 2.1 %reshape.366 = bf16[128,15,128]{2,1,0:T(8,128)(2,1)} reshape(bf16[640,384]{1,0:T(8,128)(2,1)} %shard_map.104) | data formatting | bytes 983040 | tf_op jit(solution)/shard_map/reshape | solution.py:180
  121.9 9.0 %all-to-all-start.1 = ((bf16[128,15,128]{2,1,0:T(8,128)(2,1)}), bf16[128,15,128]{2,1,0:T(8,128)(2,1)S(1)}, u32[]{:S(2)}, u32[]{:S(2)}) async-start(bf16[128,15,128]{2,1,0:T(8,128)(2,1)} %reshape.366), calls=%async_computation.1 | async-start | bytes 1048576 | tf_op jit(solution)/shard_map/all_to_all | solution.py:179
  131.0 17.9 %all-to-all-done.1 = bf16[128,15,128]{2,1,0:T(8,128)(2,1)S(1)} async-done(((bf16[128,15,128]{2,1,0:T(8,128)(2,1)}), bf16[128,15,128]{2,1,0:T(8,128)(2,1)S(1)}, u32[]{:S(2)}, u32[]{:S(2)}) %all-to-all-start.1) | async-done | bytes 491552 | tf_op jit(solution)/shard_map/all_to_all | solution.py:179
  148.9 0.3 reshape.367
  149.2 1.2 gather_fusion.2
  150.4 2.1 %convolution_convert_fusion = bf16[256,3072]{1,0:T(8,128)(2,1)} fusion(bf16[256,384]{1,0:T(8,128)(2,1)S(1)} %gather_fusion.2, bf16[384,3072]{1,0:T(8,128)(2,1)S(1)} %copy-done), kind=kOutput, calls=%fused_computation.3 | convolution fusion | flops 604766208 | bytes 4128768 | tf_op jit(solution)/shard_map/dot_general | solution.py:188
  152.6 0.7 copy-done.5
  153.2 25.2 %reduce-scatter.2.cloned.1.call-done = bf16[256,768]{1,0:T(8,128)(2,1)} async-done(((bf16[256,3072]{1,0:T(8,128)(2,1)}), bf16[256,768]{1,0:T(8,128)(2,1)}) %reduce-scatter.2.cloned.1.call-update) | async-done | bytes 393232 | tf_op jit(solution)/shard_map/reduce_scatter | solution.py:189
  178.5 1.2 multiply_reduce_fusion
  179.7 9.1 %psum.7 = f32[256]{0:T(256)S(1)} all-reduce(f32[256]{0:T(256)S(1)} %multiply_reduce_fusion), channel_id=1, replica_groups=mesh['req'=128,'tp'=4] {'tp'}, use_global_device_ids=true, to_apply=%region_6.7 | all-reduce | flops 256 | bytes 2048 | tf_op jit(solution)/shard_map/psum | solution.py:193
  188.7 2.0 %multiply_convert_fusion = (bf16[256,768]{1,0:T(8,128)(2,1)}, bf16[256,768]{1,0:T(8,128)(2,1)}) fusion(bf16[256,768]{1,0:T(8,128)(2,1)} %reduce-scatter.2.cloned.1.call-done, bf16[256,768]{1,0:T(8,128)(2,1)S(1)} %copy-done.1, f32[768]{0:T(1024)S(1)} %convert_element_type.143, f32[256]{0:T(256)S(1)} %add_rsqrt_fusion), kind=kLoop, calls=%fused_computation.13 | loop fusion | flops 1376256 | bytes 1576960 | tf_op jit(solution)/shard_map/convert_element_type | solution.py:196
  (35 shorter events, 0.5 us)
Async XLA Ops:
  7.2 143.2 %copy-start = (bf16[384,3072]{1,0:T(8,128)(2,1)S(1)}, bf16[384,3072]{1,0:T(8,128)(2,1)}, u32[]{:S(2)}) copy-start(bf16[384,3072]{1,0:T(8,128)(2,1)} %param.16) | copy-start | bytes 7077892
  14.5 18.5 %copy-start.6 = (s32[1,8]{1,0:T(1,128)S(1)}, s32[1,8]{1,0:T(1,128)}, u32[]{:S(2)}) copy-start(s32[1,8]{1,0:T(1,128)} %param.13) | copy-start | bytes 100
  14.5 57.3 %all-to-all-start = ((bf16[128,16,384]{2,1,0:T(8,128)(2,1)}), bf16[128,16,384]{2,1,0:T(8,128)(2,1)}, u32[]{:S(2)}, u32[]{:S(2)}) async-start(bf16[128,16,384]{2,1,0:T(8,128)(2,1)} %copy.51), calls=%async_computation | async-start | bytes 3145728 | tf_op jit(solution)/shard_map/all_to_all | solution.py:152
  91.6 3.5 %copy-start.2 = (f32[640,384]{1,0:T(8,128)S(1)}, f32[640,384]{1,0:T(8,128)}, u32[]{:S(2)}) copy-start(f32[640,384]{1,0:T(8,128)} %copy.52) | copy-start | bytes 2949124
  91.6 3.5 %copy-start.3 = (f32[640,384]{1,0:T(8,128)S(1)}, f32[640,384]{1,0:T(8,128)}, u32[]{:S(2)}) copy-start(f32[640,384]{1,0:T(8,128)} %copy.53) | copy-start | bytes 2949124
  91.6 3.5 %copy-start.4 = (bf16[640,384]{1,0:T(8,128)(2,1)S(1)}, bf16[640,384]{1,0:T(8,128)(2,1)}, u32[]{:S(2)}) copy-start(bf16[640,384]{1,0:T(8,128)(2,1)} %reshape.362) | copy-start | bytes 1474564
  121.9 27.0 %all-to-all-start.1 = ((bf16[128,15,128]{2,1,0:T(8,128)(2,1)}), bf16[128,15,128]{2,1,0:T(8,128)(2,1)S(1)}, u32[]{:S(2)}, u32[]{:S(2)}) async-start(bf16[128,15,128]{2,1,0:T(8,128)(2,1)} %reshape.366), calls=%async_computation.1 | async-start | bytes 1048576 | tf_op jit(solution)/shard_map/all_to_all | solution.py:179
  130.9 47.5 %reduce-scatter.2.cloned.1.call-start = ((), (), s32[]{:S(2)}) async-start(), calls=%async_computation.3 | async-start | bytes 1966080 | tf_op jit(solution)/shard_map/reduce_scatter | solution.py:189
  152.5 0.7 copy-start.5
  152.5 25.9 %copy-start.1 = (bf16[256,768]{1,0:T(8,128)(2,1)S(1)}, bf16[256,768]{1,0:T(8,128)(2,1)}, u32[]{:S(2)}) copy-start(bf16[256,768]{1,0:T(8,128)(2,1)} %param.15) | copy-start | bytes 1179652
Sparse Core Ops, SparseCore 0:
  152.7 25.7 reduce-scatter.1

commit v5 on v4

--- a/solution.py
+++ b/solution.py
@@ -49,12 +49,25 @@
     return (field.astype(jnp.float32) * cos_all + turned * sin_all).astype(jnp.bfloat16)
 
 
-ROW_BLOCK = 128
-
-
-def attend_kernel(q_ref, kc_ref, vc_ref, kn_ref, vn_ref, qrank_ref, cache_ok_ref, krank_ref, o_ref):
+def turn_rows(field, cos_rows, sin_rows, turn):
+    turned = jnp.dot(field, turn, preferred_element_type=jnp.float32)
+    return (field.astype(jnp.float32) * cos_rows + turned * sin_rows).astype(jnp.bfloat16)
+
+
+def attend_kernel(
+    q_ref, kn_ref, vn_ref, kc_ref, vc_ref, cos_ref, sin_ref, turn_ref, qrank_ref, cache_ok_ref,
+    krank_ref, o_ref, keys_ref,
+):
+    step = pl.program_id(0)
+    block = q_ref.shape[0]
+
+    @pl.when(step == 0)
+    def _():
+        keys_ref[...] = turn_rows(kn_ref[...], cos_ref[...], sin_ref[...], turn_ref[...])
+
+    here = pl.ds(pl.multiple_of(step * block, block), block)
+    query = turn_rows(q_ref[...], cos_ref[here, :], sin_ref[here, :], turn_ref[...])
     score_scale = 1.0 / math.sqrt(HEAD_SIZE)
-    query = q_ref[...]
     cols = query.shape[1]
     col_head = lax.broadcasted_iota(jnp.int32, (1, cols), 1) // HEAD_SIZE
     cache_ok = cache_ok_ref[...] > 0
@@ -68,7 +81,7 @@
             head_query, kc_ref[...], contract, preferred_element_type=jnp.float32
         ) * score_scale
         score_n = lax.dot_general(
-            head_query, kn_ref[...], contract, preferred_element_type=jnp.float32
+            head_query, keys_ref[...], contract, preferred_element_type=jnp.float32
         ) * score_scale
         score_c = jnp.where(cache_ok, score_c, -1e30)
         score_n = jnp.where(new_ok, score_n, -1e30)
@@ -88,27 +101,34 @@
     o_ref[...] = total.astype(o_ref.dtype)
 
 
-def attend_flat(query, cache_keys, cache_values, fresh_keys, fresh_values, q_rank, cache_ok, k_rank):
+def attend_slots(query, fresh_keys, fresh_values, cache_keys, cache_values, cos_all, sin_all, turn,
+                 q_rank, cache_ok, k_rank, slot_cap):
     rows, cols = query.shape
+    block = rows // slot_cap
     span = cache_keys.shape[0]
     whole = lambda i: (0, 0)
-    block = ROW_BLOCK if rows % ROW_BLOCK == 0 else rows
     return pl.pallas_call(
         attend_kernel,
-        out_shape=jax.ShapeDtypeStruct((rows, cols), jnp.bfloat16),
-        grid=(rows // block,),
+        out_shape=jax.ShapeDtypeStruct((block, slot_cap * cols), jnp.bfloat16),
+        grid=(slot_cap,),
         in_specs=[
             pl.BlockSpec((block, cols), lambda i: (i, 0)),
+            pl.BlockSpec((rows, cols), whole),
+            pl.BlockSpec((rows, cols), whole),
             pl.BlockSpec((span, cols), whole),
             pl.BlockSpec((span, cols), whole),
             pl.BlockSpec((rows, cols), whole),
             pl.BlockSpec((rows, cols), whole),
+            pl.BlockSpec((cols, cols), whole),
             pl.BlockSpec((block, 1), lambda i: (i, 0)),
             pl.BlockSpec((1, span), whole),
             pl.BlockSpec((1, rows), whole),
         ],
-        out_specs=pl.BlockSpec((block, cols), lambda i: (i, 0)),
-    )(query, cache_keys, cache_values, fresh_keys, fresh_values, q_rank, cache_ok, k_rank)
+        out_specs=pl.BlockSpec((block, cols), lambda i: (0, i)),
+        scratch_shapes=[pltpu.VMEM((rows, cols), jnp.bfloat16)],
+        compiler_params=pltpu.CompilerParams(dimension_semantics=("arbitrary",)),
+    )(query, fresh_keys, fresh_values, cache_keys, cache_values, cos_all, sin_all, turn, q_rank,
+      cache_ok, k_rank)
 
 
 def on_device(
@@ -150,31 +170,31 @@
         [slots.reshape(devices, slot_cap * parts, head_cols), count_row], axis=1
     )
     arrived = lax.all_to_all(outgoing, "req", split_axis=0, concat_axis=0, tiled=True)
-    arrived_counts = arrived[:, slot_cap * parts, 0].astype(jnp.int32)
+    planes = arrived.transpose(1, 0, 2)
+    arrived_counts = planes[slot_cap * parts, :, 0].astype(jnp.int32)
 
     length = cached_len[0]
     pool_pages = kv_pages[page_table[0]]
     cache_span = pool_pages.shape[0] * pool_pages.shape[2]
     cache_keys = pool_pages[:, 0].reshape(cache_span, head_cols)
     cache_values = pool_pages[:, 1].reshape(cache_span, head_cols)
-    live_slot = (jnp.arange(slot_cap, dtype=jnp.int32)[None, :] < arrived_counts[:, None]).reshape(
-        buffer_len
-    )
-    live_int = live_slot.astype(jnp.int32)
-    new_rank = jnp.cumsum(live_int) - live_int
+    slot_of = jnp.arange(slot_cap, dtype=jnp.int32)[:, None]
+    before = jnp.cumsum(arrived_counts) - arrived_counts
+    live_slot = (slot_of < arrived_counts[None, :]).reshape(buffer_len)
+    new_rank = (before[None, :] + slot_of).reshape(buffer_len)
     cosine, sine_tab = rope_tables(length + new_rank)
+    cos_all = jnp.tile(cosine, (1, heads_here))
+    sin_all = jnp.tile(sine_tab, (1, heads_here))
     cache_ok = (jnp.arange(cache_span, dtype=jnp.int32) < length).astype(jnp.int32)[None, :]
     k_rank = jnp.where(live_slot, new_rank, jnp.int32(2**30))[None, :]
     q_rank = new_rank[:, None]
     part_rows = [
-        arrived[:, p * slot_cap : (p + 1) * slot_cap].reshape(buffer_len, head_cols)
+        planes[p * slot_cap : (p + 1) * slot_cap].reshape(buffer_len, head_cols)
         for p in range(parts)
     ]
-    turn = turn_matrix(head_cols)
-    query = rotate_flat(part_rows[0], cosine, sine_tab, turn)
-    fresh_keys = rotate_flat(part_rows[1], cosine, sine_tab, turn)
-    result = attend_flat(
-        query, cache_keys, cache_values, fresh_keys, part_rows[2], q_rank, cache_ok, k_rank
+    result = attend_slots(
+        part_rows[0], part_rows[1], part_rows[2], cache_keys, cache_values, cos_all, sin_all,
+        turn_matrix(head_cols), q_rank, cache_ok, k_rank, slot_cap,
     )
     returned = lax.all_to_all(
         result.reshape(devices, slot_cap * parts, head_cols // parts),

time: 199 us -> 192 us (0.965)
  matrix products: 8.86 us -> 3.8 us
  local copies, waits for them, and re-layouts: 28.7 us -> 25 us
    reshape x3 -> x0, local copies, waits for them, and re-layouts: 5.11 us -> none  [on_device(): arrived[:, p * slot_cap:(p + 1) * slot_cap].reshape(buffer_len, head_cols)]
    dot_general x2 -> x0, matrix products: 5.06 us -> none  [rotate_flat(): turned = jnp.dot(field, turn, preferred_element_type=jnp.float32)]
    convert_element_type x2 -> x3, other arithmetic: 3.38 us -> 5.44 us  [the longest x2 4.38 us: on_device(): arrived_counts = planes[slot_cap * parts, :, 0].astype(jnp.int32)]
    slice x2 -> x4, local copies, waits for them, and re-layouts: 3.53 us -> 4.91 us  [on_device(): planes[p * slot_cap:(p + 1) * slot_cap].reshape(buffer_len, head_cols)]
  transfers between devices with their start and end apart: 3 -> 3, of which waited for: 3 -> 3; matrix products, arithmetic and copies ran while one was open for 3% -> 4% of each run, Pallas kernels for 0% -> 0%
where the time goes in v5:
time: 192 us; the launch traced here: 191 us
  waiting for transfers between devices  74.1 us (39%)
  starting transfers between devices  27 us (14%)
  local copies, waits for them, and re-layouts  25 us (13%)
  Pallas kernels  25 us (13%)
  between operations  14.9 us (8%)
  other arithmetic  12.2 us (6%)
  blocking collectives  9.04 us (5%)
  matrix products  3.8 us (2%)
    all_to_all x1, waiting for transfers between devices, on_device(): lax.all_to_all(outgoing, 'req', split_axis=0, concat_axis=0, tiled=True)  30.9 us
    reduce_scatter x1, waiting for transfers between devices, on_device(): lax.psum_scatter(partial_sum.astype(jnp.bfloat16), 'tp', scatter_dimensio...  25.3 us
    pallas_call x1, Pallas kernels, attend_slots(): pl.pallas_call(attend_kernel, out_shape=jax.ShapeDtypeStruct((block, slot...  25 us
    all_to_all x1, waiting for transfers between devices, on_device(): lax.all_to_all(result.reshape(devices, slot_cap * parts, head_cols // par...  17.9 us
    all_to_all x1, starting transfers between devices, on_device(): lax.all_to_all(outgoing, 'req', split_axis=0, concat_axis=0, tiled=True)  17.9 us
    psum x1, blocking collectives, on_device(): square_sum = lax.psum(jnp.sum(hidden * hidden, axis=1), 'tp')  9.04 us
    all_to_all x1, starting transfers between devices, on_device(): lax.all_to_all(result.reshape(devices, slot_cap * parts, head_cols // par...  9.04 us
    slice x4, local copies, waits for them, and re-layouts, on_device(): planes[p * slot_cap:(p + 1) * slot_cap].reshape(buffer_len, head_cols)  4.91 us
  transfers between devices with their start and end apart: 3, of which 3 were waited for; matrix products, arithmetic and copies ran while one was open for 4% of the time, Pallas kernels for 0%

profile of v5, /device:TPU:56, one launch (start us, length us, event | category | flops | bytes accessed | tf_op | source)
XLA Modules:
  0.0 191.0 jit_solution(11275446255978124303)
XLA Ops:
  7.2 0.0 copy-start
  7.2 0.8 compare_select_fusion.1
  8.0 1.9 gather_fusion
  9.9 0.1 convert_reduce_fusion.1
  10.0 0.2 convert_reduce_fusion
  10.3 1.7 fusion
  11.9 0.2 copy.40
  12.2 0.1 broadcast_in_dim.17
  12.2 0.2 pad_maximum_fusion
  12.4 2.1 %copy.41 = bf16[128,16,384]{2,1,0:T(8,128)(2,1)} copy(bf16[128,16,384]{2,0,1:T(8,128)(2,1)S(1)} %pad_maximum_fusion) | data formatting | bytes 3145728 | tf_op jit(solution)/shard_map/concatenate | solution.py:169
  14.5 17.9 %all-to-all-start = ((bf16[128,16,384]{2,1,0:T(8,128)(2,1)}), bf16[128,16,384]{2,1,0:T(8,128)(2,1)}, u32[]{:S(2)}, u32[]{:S(2)}) async-start(bf16[128,16,384]{2,1,0:T(8,128)(2,1)} %copy.41), calls=%async_computation | async-start | bytes 3145728 | tf_op jit(solution)/shard_map/all_to_all | solution.py:172
  33.0 0.0 copy-done.3
  33.1 3.3 %gather_fusion.1 = bf16[8,2,128,384]{3,2,1,0:T(8,128)(2,1)} fusion(bf16[8,2,128,384]{3,2,1,0:T(8,128)(2,1)} %param.14, s32[1024]{0:T(1024)S(1)} %pad_clamp_fusion.1), kind=kCustom, calls=%fused_computation.1 | custom fusion | bytes 3145760 | tf_op jit(solution)/shard_map/gather | solution.py:177
  36.4 0.6 compare_convert_fusion.cache_ok_ref
  37.0 1.1 select_convert_fusion.turn_ref
  38.1 2.8 %fusion.20 = (bf16[8,1,128,384]{3,2,1,0:T(8,128)(2,1)}, bf16[8,1,128,384]{3,2,1,0:T(8,128)(2,1)}) fusion(bf16[8,2,128,384]{3,2,1,0:T(8,128)(2,1)} %gather_fusion.1), kind=kLoop, calls=%fused_computation.66 | loop fusion | bytes 3145728 | tf_op jit(solution)/shard_map/slice | solution.py:180
  40.9 30.9 %all-to-all-done = bf16[128,16,384]{2,1,0:T(8,128)(2,1)} async-done(((bf16[128,16,384]{2,1,0:T(8,128)(2,1)}), bf16[128,16,384]{2,1,0:T(8,128)(2,1)}, u32[]{:S(2)}, u32[]{:S(2)}) %all-to-all-start) | async-done | bytes 1572896 | tf_op jit(solution)/shard_map/all_to_all | solution.py:172
  71.8 2.3 %fusion.21 = (bf16[5,128,384]{2,0,1:T(8,128)(2,1)S(1)}, bf16[5,128,384]{2,0,1:T(8,128)(2,1)S(1)}, bf16[5,128,384]{2,0,1:T(8,128)(2,1)S(1)}) fusion(bf16[16,128,384]{2,0,1:T(8,128)(2,1)} %bitcast.5), kind=kLoop, calls=%fused_computation.67 | loop fusion | bytes 2949120 | tf_op jit(solution)/shard_map/slice | solution.py:192
  74.1 3.3 %fusion.19 = s32[128]{0:T(128)S(1)} fusion(bf16[16,128,384]{2,0,1:T(8,128)(2,1)} %bitcast.5), kind=kLoop, calls=%fused_computation.65 | loop fusion | flops 128 | bytes 768 | tf_op jit(solution)/shard_map/convert_element_type | solution.py:174
  77.4 1.1 slice_convert_fusion
  78.5 0.9 copy.42
  79.4 0.8 copy.43
  80.2 0.9 copy.44
  81.1 0.2 reduce-window.8
  81.2 0.1 reduce
  81.4 0.5 multiply_sine_fusion
  81.9 0.7 pad_maximum_fusion.1
  82.6 0.1 tile.8
  82.7 1.3 copy.46.cos_ref
  84.0 1.0 tile.20
  85.0 1.3 copy.47.sin_ref
  86.3 0.6 copy_bitcast_fusion
  86.9 0.9 copy.53
  87.8 25.0 %shard_map.104 = bf16[128,1920]{1,0:T(8,128)(2,1)} custom-call(bf16[640,384]{1,0:T(8,128)(2,1)} %bitcast.50, bf16[640,384]{1,0:T(8,128)(2,1)} %bitcast.51, bf16[640,384]{1,0:T(8,128)(2,1)} %bitcast.52, bf16[1024,384]{1,0:T(8,128)(2,1)} %bitcast.49, bf16[1024,384]{1,0:T(8,128)(2,1)} %bitcast.48, f32[640,384]{1,0:T(8,128)} %copy.46.cos_ref, ...), custom_call_target="tpu_custom_call" | custom-call | tf_op jit(solution)/shard_map/pallas_call | solution.py:110
  112.8 1.3 copy.49
  114.1 1.2 copy.50
  115.2 9.0 %all-to-all-start.1 = ((bf16[128,15,128]{2,1,0:T(8,128)(2,1)}), bf16[128,15,128]{2,1,0:T(8,128)(2,1)S(1)}, u32[]{:S(2)}, u32[]{:S(2)}) async-start(bf16[128,15,128]{2,1,0:T(8,128)(2,1)} %copy.50), calls=%async_computation.1 | async-start | bytes 1048576 | tf_op jit(solution)/shard_map/all_to_all | solution.py:199
  124.3 0.0 reduce-scatter.2.cloned.1.call-start
  124.4 17.9 %all-to-all-done.1 = bf16[128,15,128]{2,1,0:T(8,128)(2,1)S(1)} async-done(((bf16[128,15,128]{2,1,0:T(8,128)(2,1)}), bf16[128,15,128]{2,1,0:T(8,128)(2,1)S(1)}, u32[]{:S(2)}, u32[]{:S(2)}) %all-to-all-start.1) | async-done | bytes 491552 | tf_op jit(solution)/shard_map/all_to_all | solution.py:199
  142.3 0.3 reshape.360
  142.6 1.2 gather_fusion.2
  143.8 2.1 %convolution_convert_fusion = bf16[256,3072]{1,0:T(8,128)(2,1)} fusion(bf16[256,384]{1,0:T(8,128)(2,1)S(1)} %gather_fusion.2, bf16[384,3072]{1,0:T(8,128)(2,1)S(1)} %copy-done), kind=kOutput, calls=%fused_computation.3 | convolution fusion | flops 604766208 | bytes 4128768 | tf_op jit(solution)/shard_map/dot_general | solution.py:208
  145.9 0.0 reduce-scatter.2.cloned.1.call-update
  145.9 0.7 copy-done.2
  146.6 25.3 %reduce-scatter.2.cloned.1.call-done = bf16[256,768]{1,0:T(8,128)(2,1)} async-done(((bf16[256,3072]{1,0:T(8,128)(2,1)}), bf16[256,768]{1,0:T(8,128)(2,1)}) %reduce-scatter.2.cloned.1.call-update) | async-done | bytes 393232 | tf_op jit(solution)/shard_map/reduce_scatter | solution.py:209
  171.9 1.2 multiply_reduce_fusion
  173.1 9.0 %psum.7 = f32[256]{0:T(256)S(1)} all-reduce(f32[256]{0:T(256)S(1)} %multiply_reduce_fusion), channel_id=1, replica_groups=mesh['req'=128,'tp'=4] {'tp'}, use_global_device_ids=true, to_apply=%region_5.6 | all-reduce | flops 256 | bytes 2048 | tf_op jit(solution)/shard_map/psum | solution.py:213
  182.1 2.0 %multiply_convert_fusion = (bf16[256,768]{1,0:T(8,128)(2,1)}, bf16[256,768]{1,0:T(8,128)(2,1)}) fusion(bf16[256,768]{1,0:T(8,128)(2,1)} %reduce-scatter.2.cloned.1.call-done, bf16[256,768]{1,0:T(8,128)(2,1)S(1)} %copy-done.1, f32[768]{0:T(1024)S(1)} %convert_element_type.105, f32[256]{0:T(256)S(1)} %add_rsqrt_fusion), kind=kLoop, calls=%fused_computation.7 | loop fusion | flops 1376256 | bytes 1576960 | tf_op jit(solution)/shard_map/convert_element_type | solution.py:216
  (22 shorter events, 0.1 us)
Async XLA Ops:
  7.2 136.6 %copy-start = (bf16[384,3072]{1,0:T(8,128)(2,1)S(1)}, bf16[384,3072]{1,0:T(8,128)(2,1)}, u32[]{:S(2)}) copy-start(bf16[384,3072]{1,0:T(8,128)(2,1)} %param.16) | copy-start | bytes 7077892
  14.5 18.5 %copy-start.3 = (s32[1,8]{1,0:T(1,128)S(1)}, s32[1,8]{1,0:T(1,128)}, u32[]{:S(2)}) copy-start(s32[1,8]{1,0:T(1,128)} %param.13) | copy-start | bytes 100
  14.5 57.3 %all-to-all-start = ((bf16[128,16,384]{2,1,0:T(8,128)(2,1)}), bf16[128,16,384]{2,1,0:T(8,128)(2,1)}, u32[]{:S(2)}, u32[]{:S(2)}) async-start(bf16[128,16,384]{2,1,0:T(8,128)(2,1)} %copy.41), calls=%async_computation | async-start | bytes 3145728 | tf_op jit(solution)/shard_map/all_to_all | solution.py:172
  115.2 27.0 %all-to-all-start.1 = ((bf16[128,15,128]{2,1,0:T(8,128)(2,1)}), bf16[128,15,128]{2,1,0:T(8,128)(2,1)S(1)}, u32[]{:S(2)}, u32[]{:S(2)}) async-start(bf16[128,15,128]{2,1,0:T(8,128)(2,1)} %copy.50), calls=%async_computation.1 | async-start | bytes 1048576 | tf_op jit(solution)/shard_map/all_to_all | solution.py:199
  124.3 47.6 %reduce-scatter.2.cloned.1.call-start = ((), (), s32[]{:S(2)}) async-start(), calls=%async_computation.3 | async-start | bytes 1966080 | tf_op jit(solution)/shard_map/reduce_scatter | solution.py:209
  145.9 0.7 copy-start.2
  145.9 26.0 %copy-start.1 = (bf16[256,768]{1,0:T(8,128)(2,1)S(1)}, bf16[256,768]{1,0:T(8,128)(2,1)}, u32[]{:S(2)}) copy-start(bf16[256,768]{1,0:T(8,128)(2,1)} %param.15) | copy-start | bytes 1179652
Sparse Core Ops, SparseCore 0:
  146.0 25.7 reduce-scatter.1

commit v6 on v5

--- a/solution.py
+++ b/solution.py
@@ -152,6 +152,7 @@
     device_ids = jnp.arange(devices, dtype=jnp.int32)
     row_ids = jnp.arange(row_count, dtype=jnp.int32)
 
+    weight_cols = lax.all_to_all(out_weight, "tp", split_axis=1, concat_axis=0, tiled=True)
     owner_dev = request_owner[row_request]
     same_owner = owner_dev[:, None] == owner_dev[None, :]
     slot_in = jnp.sum((same_owner & (row_ids[None, :] < row_ids[:, None])).astype(jnp.int32), axis=1)
@@ -205,10 +206,8 @@
     )
     target = owner_dev * slot_cap + slot_in
     attn_rows = returned.reshape(buffer_len, head_cols)[target]
-    partial_sum = jnp.dot(attn_rows, out_weight, preferred_element_type=jnp.float32)
-    mixed_cols = lax.psum_scatter(
-        partial_sum.astype(jnp.bfloat16), "tp", scatter_dimension=1, tiled=True
-    ).astype(jnp.float32)
+    attn_all = lax.all_gather(attn_rows, "tp", axis=1, tiled=True)
+    mixed_cols = jnp.dot(attn_all, weight_cols, preferred_element_type=jnp.float32)
     hidden = residual.astype(jnp.float32) + mixed_cols
     square_sum = lax.psum(jnp.sum(hidden * hidden, axis=1), "tp")
     inv_rms = lax.rsqrt(square_sum / D + EPS)

time: 192 us -> 171 us (0.89)
  waiting for transfers between devices: 74.1 us -> 44.7 us
  blocking collectives: 9.04 us -> 25.6 us
  between operations: 14.9 us -> 1.51 us
  other arithmetic: 12.2 us -> 7.39 us
  starting transfers between devices: 27 us -> 31 us
  local copies, waits for them, and re-layouts: 25 us -> 28.8 us
    reduce_scatter x1 -> x0, waiting for transfers between devices: 25.3 us -> none  [on_device(): lax.psum_scatter(partial_sum.astype(jnp.bfloat16), 'tp', scatter_dimensio...]
    all_gather x0 -> x1, blocking collectives: none -> 15.6 us  [on_device(): attn_all = lax.all_gather(attn_rows, 'tp', axis=1, tiled=True)]
    all_to_all x0 -> x1, starting transfers between devices: none -> 4.68 us  [on_device(): lax.all_to_all(out_weight, 'tp', split_axis=1, concat_axis=0, tiled=True)]
    all_to_all x0 -> x1, local copies, waits for them, and re-layouts: none -> 4.29 us  [on_device(): lax.all_to_all(out_weight, 'tp', split_axis=1, concat_axis=0, tiled=True)]
    all_to_all x1, waiting for transfers between devices: 17.9 us -> 13.6 us  [on_device(): lax.all_to_all(result.reshape(devices, slot_cap * parts, head_cols // par...]
    unnamed x9 -> x10, local copies, waits for them, and re-layouts: 1.58 us -> 5.23 us
  transfers between devices with their start and end apart: 3 -> 3, of which waited for: 3 -> 2; matrix products, arithmetic and copies ran while one was open for 4% -> 17% of each run, Pallas kernels for 0% -> 15%
where the time goes in v6:
time: 171 us; the launch traced here: 168 us
  waiting for transfers between devices  44.7 us (26%)
  starting transfers between devices  31 us (18%)
  local copies, waits for them, and re-layouts  28.8 us (17%)
  blocking collectives  25.6 us (15%)
  Pallas kernels  25 us (15%)
  other arithmetic  7.39 us (4%)
  matrix products  4.19 us (2%)
    all_to_all x1, waiting for transfers between devices, on_device(): lax.all_to_all(outgoing, 'req', split_axis=0, concat_axis=0, tiled=True)  31.1 us
    pallas_call x1, Pallas kernels, attend_slots(): pl.pallas_call(attend_kernel, out_shape=jax.ShapeDtypeStruct((block, slot...  25 us
    all_to_all x1, starting transfers between devices, on_device(): lax.all_to_all(outgoing, 'req', split_axis=0, concat_axis=0, tiled=True)  17.3 us
    all_gather x1, blocking collectives, on_device(): attn_all = lax.all_gather(attn_rows, 'tp', axis=1, tiled=True)  15.6 us
    all_to_all x1, waiting for transfers between devices, on_device(): lax.all_to_all(result.reshape(devices, slot_cap * parts, head_cols // par...  13.6 us
    psum x1, blocking collectives, on_device(): square_sum = lax.psum(jnp.sum(hidden * hidden, axis=1), 'tp')  10 us
    all_to_all x1, starting transfers between devices, on_device(): lax.all_to_all(result.reshape(devices, slot_cap * parts, head_cols // par...  9.05 us
    unnamed x10, local copies, waits for them, and re-layouts  5.23 us
  transfers between devices with their start and end apart: 3, of which 2 were waited for; matrix products, arithmetic and copies ran while one was open for 17% of the time, Pallas kernels for 15%

profile of v6, /device:TPU:56, one launch (start us, length us, event | category | flops | bytes accessed | tf_op | source)
XLA Modules:
  0.0 168.2 jit_solution(6228989299307943351)
XLA Ops:
  0.6 0.0 copy-start
  0.6 0.8 compare_select_fusion.1
  1.5 1.9 %gather_fusion = s32[256]{0:T(256)S(1)} fusion(s32[128]{0:T(128)} %param.11, s32[1024]{0:T(1024)S(1)} %pad_clamp_fusion.2), kind=kCustom, calls=%fused_computation | custom fusion | bytes 3072 | tf_op jit(solution)/shard_map/gather | solution.py:156
  3.3 0.1 convert_reduce_fusion.1
  3.5 0.2 convert_reduce_fusion
  3.7 1.7 fusion
  5.4 0.2 copy.44
  5.6 0.1 broadcast_in_dim.17
  5.7 0.2 pad_maximum_fusion
  5.9 2.1 %copy.45 = bf16[128,16,384]{2,1,0:T(8,128)(2,1)} copy(bf16[128,16,384]{2,0,1:T(8,128)(2,1)S(1)} %pad_maximum_fusion) | data formatting | bytes 3145728 | tf_op jit(solution)/shard_map/concatenate | solution.py:170
  7.9 17.3 %all-to-all-start = ((bf16[128,16,384]{2,1,0:T(8,128)(2,1)}), bf16[128,16,384]{2,1,0:T(8,128)(2,1)S(1)}, u32[]{:S(2)}, u32[]{:S(2)}) async-start(bf16[128,16,384]{2,1,0:T(8,128)(2,1)} %copy.45), calls=%async_computation | async-start | bytes 3145728 | tf_op jit(solution)/shard_map/all_to_all | solution.py:173
  25.9 0.0 copy-start.3
  25.9 4.3 %copy.55 = bf16[384,3072]{0,1:T(8,128)(2,1)} copy(bf16[384,3072]{1,0:T(8,128)(2,1)} %param.16) | data formatting | bytes 4718592 | tf_op args[7]
  30.3 1.9 %gather_fusion.1 = bf16[8,2,128,384]{3,2,1,0:T(8,128)(2,1)} fusion(bf16[8,2,128,384]{3,2,1,0:T(8,128)(2,1)S(1)} %copy-done, s32[1024]{0:T(1024)S(1)} %pad_clamp_fusion.1), kind=kCustom, calls=%fused_computation.1 | custom fusion | bytes 3145760 | tf_op jit(solution)/shard_map/gather | solution.py:178
  32.2 0.6 compare_convert_fusion.cache_ok_ref
  32.8 1.1 select_convert_fusion.turn_ref
  33.9 31.1 %all-to-all-done = bf16[128,16,384]{2,1,0:T(8,128)(2,1)S(1)} async-done(((bf16[128,16,384]{2,1,0:T(8,128)(2,1)}), bf16[128,16,384]{2,1,0:T(8,128)(2,1)S(1)}, u32[]{:S(2)}, u32[]{:S(2)}) %all-to-all-start) | async-done | bytes 1572896 | tf_op jit(solution)/shard_map/all_to_all | solution.py:173
  65.0 4.7 %all-to-all-start.2 = ((bf16[384,4,768]{0,2,1:T(8,128)(2,1)}), bf16[384,4,768]{0,2,1:T(8,128)(2,1)}, u32[]{:S(2)}, u32[]{:S(2)}) async-start(bf16[384,4,768]{0,2,1:T(8,128)(2,1)} %bitcast.51), calls=%async_computation.2 | async-start | bytes 4718592 | tf_op jit(solution)/shard_map/all_to_all | solution.py:155
  69.7 2.7 %fusion.19 = (bf16[8,1,128,384]{3,2,1,0:T(8,128)(2,1)}, bf16[8,1,128,384]{3,2,1,0:T(8,128)(2,1)}) fusion(bf16[8,2,128,384]{3,2,1,0:T(8,128)(2,1)} %gather_fusion.1), kind=kLoop, calls=%fused_computation.64 | loop fusion | bytes 3145728 | tf_op jit(solution)/shard_map/slice | solution.py:181
  72.4 0.4 fusion.20
  72.8 0.9 copy.46
  73.7 0.9 copy.47
  74.6 0.9 copy.48
  75.5 0.1 slice_convert_fusion
  75.6 0.2 reduce-window.8
  75.8 0.1 reduce
  75.9 2.4 %fusion.18 = s32[128]{0:T(128)S(1)} fusion(bf16[16,128,384]{2,0,1:T(8,128)(2,1)S(1)} %bitcast.50), kind=kLoop, calls=%fused_computation.63 | loop fusion | flops 128 | bytes 768 | tf_op jit(solution)/shard_map/convert_element_type | solution.py:175
  78.3 0.5 multiply_sine_fusion
  78.8 0.1 tile.8
  78.9 1.3 copy.50.cos_ref
  80.2 0.1 tile.20
  80.3 1.3 copy.51.sin_ref
  81.6 0.6 copy_bitcast_fusion
  82.2 0.9 copy.59
  83.1 25.0 %shard_map.104 = bf16[128,1920]{1,0:T(8,128)(2,1)} custom-call(bf16[640,384]{1,0:T(8,128)(2,1)} %bitcast.58, bf16[640,384]{1,0:T(8,128)(2,1)} %bitcast.59, bf16[640,384]{1,0:T(8,128)(2,1)} %bitcast.60, bf16[1024,384]{1,0:T(8,128)(2,1)} %bitcast.56, bf16[1024,384]{1,0:T(8,128)(2,1)} %bitcast.55, f32[640,384]{1,0:T(8,128)} %copy.50.cos_ref, ...), custom_call_target="tpu_custom_call" | custom-call | tf_op jit(solution)/shard_map/pallas_call | solution.py:110
  108.0 1.3 copy.53
  109.3 1.2 copy.54
  110.6 0.0 all-to-all-done.2
  110.6 9.0 %all-to-all-start.1 = ((bf16[128,15,128]{2,1,0:T(8,128)(2,1)}), bf16[128,15,128]{2,1,0:T(8,128)(2,1)S(1)}, u32[]{:S(2)}, u32[]{:S(2)}) async-start(bf16[128,15,128]{2,1,0:T(8,128)(2,1)} %copy.54), calls=%async_computation.1 | async-start | bytes 1048576 | tf_op jit(solution)/shard_map/all_to_all | solution.py:200
  119.7 4.3 %copy.56 = bf16[4,384,768]{2,1,0:T(8,128)(2,1)} copy(bf16[4,384,768]{1,2,0:T(8,128)(2,1)} %bitcast.22) | data formatting | bytes 4718592 | tf_op jit(solution)/shard_map/all_to_all | solution.py:155
  124.0 13.6 %all-to-all-done.1 = bf16[128,15,128]{2,1,0:T(8,128)(2,1)S(1)} async-done(((bf16[128,15,128]{2,1,0:T(8,128)(2,1)}), bf16[128,15,128]{2,1,0:T(8,128)(2,1)S(1)}, u32[]{:S(2)}, u32[]{:S(2)}) %all-to-all-start.1) | async-done | bytes 491552 | tf_op jit(solution)/shard_map/all_to_all | solution.py:200
  137.6 0.3 reshape.363
  137.9 0.0 copy-start.2
  137.9 1.2 gather_fusion.2
  139.1 15.6 %all-gather = bf16[256,1536]{1,0:T(8,128)(2,1)S(1)} all-gather(bf16[256,384]{1,0:T(8,128)(2,1)S(1)} %gather_fusion.2), channel_id=2, replica_groups=mesh['req'=128,'tp'=4] {'tp'}, dimensions={1}, use_global_device_ids=true | all-gather | bytes 983040 | tf_op jit(solution)/shard_map/all_gather | solution.py:209
  154.7 2.5 %multiply_reduce_fusion = (f32[256]{0:T(256)S(1)}, f32[256,768]{1,0:T(8,128)S(1)}) fusion(bf16[256,1536]{1,0:T(8,128)(2,1)S(1)} %all-gather, bf16[1536,768]{1,0:T(8,128)(2,1)} %bitcast.57, bf16[256,768]{1,0:T(8,128)(2,1)S(1)} %copy-done.2), kind=kOutput, calls=%fused_computation.8 | convolution fusion | flops 604765952 | bytes 4326400 | tf_op jit(solution)/shard_map/dot_general | solution.py:210
  157.2 10.0 %psum.7 = f32[256]{0:T(256)S(1)} all-reduce(f32[256]{0:T(256)S(1)} %get-tuple-element.14), channel_id=1, replica_groups=mesh['req'=128,'tp'=4] {'tp'}, use_global_device_ids=true, to_apply=%region_4.5 | all-reduce | flops 256 | bytes 2048 | tf_op jit(solution)/shard_map/psum | solution.py:212
  167.2 1.0 multiply_convert_fusion
  (23 shorter events, 0.2 us)
Async XLA Ops:
  0.6 29.6 %copy-start = (bf16[8,2,128,384]{3,2,1,0:T(8,128)(2,1)S(1)}, bf16[8,2,128,384]{3,2,1,0:T(8,128)(2,1)}, u32[]{:S(2)}) copy-start(bf16[8,2,128,384]{3,2,1,0:T(8,128)(2,1)} %param.14) | copy-start | bytes 4718596
  7.9 57.0 %all-to-all-start = ((bf16[128,16,384]{2,1,0:T(8,128)(2,1)}), bf16[128,16,384]{2,1,0:T(8,128)(2,1)S(1)}, u32[]{:S(2)}, u32[]{:S(2)}) async-start(bf16[128,16,384]{2,1,0:T(8,128)(2,1)} %copy.45), calls=%async_computation | async-start | bytes 3145728 | tf_op jit(solution)/shard_map/all_to_all | solution.py:173
  25.9 4.3 %copy-start.3 = (s32[1,8]{1,0:T(1,128)S(1)}, s32[1,8]{1,0:T(1,128)}, u32[]{:S(2)}) copy-start(s32[1,8]{1,0:T(1,128)} %param.13) | copy-start | bytes 100
  65.0 45.6 %all-to-all-start.2 = ((bf16[384,4,768]{0,2,1:T(8,128)(2,1)}), bf16[384,4,768]{0,2,1:T(8,128)(2,1)}, u32[]{:S(2)}, u32[]{:S(2)}) async-start(bf16[384,4,768]{0,2,1:T(8,128)(2,1)} %bitcast.51), calls=%async_computation.2 | async-start | bytes 4718592 | tf_op jit(solution)/shard_map/all_to_all | solution.py:155
  108.0 11.6 %copy-start.1 = (bf16[768]{0:T(1024)(128)(2,1)S(1)}, bf16[768]{0:T(1024)(128)(2,1)}, u32[]{:S(2)}) copy-start(bf16[768]{0:T(1024)(128)(2,1)} %param.17) | copy-start | bytes 4612
  110.6 27.0 %all-to-all-start.1 = ((bf16[128,15,128]{2,1,0:T(8,128)(2,1)}), bf16[128,15,128]{2,1,0:T(8,128)(2,1)S(1)}, u32[]{:S(2)}, u32[]{:S(2)}) async-start(bf16[128,15,128]{2,1,0:T(8,128)(2,1)} %copy.54), calls=%async_computation.1 | async-start | bytes 1048576 | tf_op jit(solution)/shard_map/all_to_all | solution.py:200
  137.9 16.8 %copy-start.2 = (bf16[256,768]{1,0:T(8,128)(2,1)S(1)}, bf16[256,768]{1,0:T(8,128)(2,1)}, u32[]{:S(2)}) copy-start(bf16[256,768]{1,0:T(8,128)(2,1)} %param.15) | copy-start | bytes 1179652

commit v7 on v6

--- a/solution.py
+++ b/solution.py
@@ -206,10 +206,24 @@
     )
     target = owner_dev * slot_cap + slot_in
     attn_rows = returned.reshape(buffer_len, head_cols)[target]
-    attn_all = lax.all_gather(attn_rows, "tp", axis=1, tiled=True)
-    mixed_cols = jnp.dot(attn_all, weight_cols, preferred_element_type=jnp.float32)
+    tp_size = lax.axis_size("tp")
+    attn_all = lax.all_to_all(
+        jnp.broadcast_to(attn_rows[None], (tp_size,) + attn_rows.shape), "tp", 0, 0, tiled=True
+    )
+    mixed_cols = jnp.einsum(
+        "tmc,tcn->mn",
+        attn_all,
+        weight_cols.reshape(attn_all.shape[0], head_cols, -1),
+        preferred_element_type=jnp.float32,
+    )
     hidden = residual.astype(jnp.float32) + mixed_cols
-    square_sum = lax.psum(jnp.sum(hidden * hidden, axis=1), "tp")
+    square_part = jnp.sum(hidden * hidden, axis=1)
+    square_sum = jnp.sum(
+        lax.all_to_all(
+            jnp.broadcast_to(square_part[None], (tp_size,) + square_part.shape), "tp", 0, 0, tiled=True
+        ),
+        axis=0,
+    )
     inv_rms = lax.rsqrt(square_sum / D + EPS)
     normed = hidden * inv_rms[:, None] * norm_gain.astype(jnp.float32)[None, :]
     return (hidden.astype(jnp.bfloat16), normed.astype(jnp.bfloat16))

time: 171 us -> 194 us (1.13)
  waiting for transfers between devices: 44.7 us -> 76.2 us
  blocking collectives: 25.6 us -> 15.1 us
  starting transfers between devices: 31 us -> 34.3 us
    all_to_all x1, waiting for transfers between devices: 0.01 us -> 28.9 us  [on_device(): lax.all_to_all(out_weight, 'tp', split_axis=1, concat_axis=0, tiled=True)]
    all_gather x1 -> x0, blocking collectives: 15.6 us -> none  [on_device(): attn_all = lax.all_gather(attn_rows, 'tp', axis=1, tiled=True)]
    all_to_all x0 -> x1, blocking collectives: none -> 15.1 us  [on_device(): lax.all_to_all(jnp.broadcast_to(attn_rows[None], (tp_size,) + attn_rows.s...]
    psum x1 -> x0, blocking collectives: 10 us -> none  [on_device(): square_sum = lax.psum(jnp.sum(hidden * hidden, axis=1), 'tp')]
    all_to_all x0 -> x1, waiting for transfers between devices: none -> 5.23 us  [on_device(): lax.all_to_all(jnp.broadcast_to(square_part[None], (tp_size,) + square_pa...]
    all_to_all x1, waiting for transfers between devices: 13.6 us -> 9.43 us  [on_device(): lax.all_to_all(result.reshape(devices, slot_cap * parts, head_cols // par...]
    all_to_all x0 -> x1, starting transfers between devices: none -> 3.25 us  [on_device(): lax.all_to_all(jnp.broadcast_to(square_part[None], (tp_size,) + square_pa...]
  transfers between devices with their start and end apart: 3 -> 4, of which waited for: 2 -> 4; matrix products, arithmetic and copies ran while one was open for 17% -> 9% of each run, Pallas kernels for 15% -> 0%
where the time goes in v7:
time: 194 us; the launch traced here: 193 us
  waiting for transfers between devices  76.2 us (39%)
  starting transfers between devices  34.3 us (18%)
  local copies, waits for them, and re-layouts  29.3 us (15%)
  Pallas kernels  25 us (13%)
  blocking collectives  15.1 us (8%)
  other arithmetic  7.41 us (4%)
  matrix products  4.2 us (2%)
    all_to_all x1, waiting for transfers between devices, on_device(): lax.all_to_all(outgoing, 'req', split_axis=0, concat_axis=0, tiled=True)  32.6 us
    all_to_all x1, waiting for transfers between devices, on_device(): lax.all_to_all(out_weight, 'tp', split_axis=1, concat_axis=0, tiled=True)  28.9 us
    pallas_call x1, Pallas kernels, attend_slots(): pl.pallas_call(attend_kernel, out_shape=jax.ShapeDtypeStruct((block, slot...  25 us
    all_to_all x1, starting transfers between devices, on_device(): lax.all_to_all(outgoing, 'req', split_axis=0, concat_axis=0, tiled=True)  17.5 us
    all_to_all x1, blocking collectives, on_device(): lax.all_to_all(jnp.broadcast_to(attn_rows[None], (tp_size,) + attn_rows.s...  15.1 us
    all_to_all x1, waiting for transfers between devices, on_device(): lax.all_to_all(result.reshape(devices, slot_cap * parts, head_cols // par...  9.43 us
    all_to_all x1, starting transfers between devices, on_device(): lax.all_to_all(result.reshape(devices, slot_cap * parts, head_cols // par...  9.06 us
    all_to_all x1, waiting for transfers between devices, on_device(): lax.all_to_all(jnp.broadcast_to(square_part[None], (tp_size,) + square_pa...  5.23 us
  transfers between devices with their start and end apart: 4, of which 4 were waited for; matrix products, arithmetic and copies ran while one was open for 9% of the time, Pallas kernels for 0%

profile of v7, /device:TPU:56, one launch (start us, length us, event | category | flops | bytes accessed | tf_op | source)
XLA Modules:
  0.0 193.0 jit_solution(15331907507017358356)
XLA Ops:
  0.6 0.8 compare_select_fusion.1
  1.5 1.9 gather_fusion
  3.3 0.1 convert_reduce_fusion.1
  3.5 0.2 convert_reduce_fusion
  3.7 1.7 fusion.2
  5.4 0.2 copy.59
  5.6 0.1 broadcast_in_dim.21
  5.7 0.2 pad_maximum_fusion
  5.9 2.1 %copy.60 = bf16[128,16,384]{2,1,0:T(8,128)(2,1)} copy(bf16[128,16,384]{2,0,1:T(8,128)(2,1)S(1)} %pad_maximum_fusion) | data formatting | bytes 3145728 | tf_op jit(solution)/shard_map/concatenate | solution.py:170
  7.9 17.5 %all-to-all-start = ((bf16[128,16,384]{2,1,0:T(8,128)(2,1)}), bf16[128,16,384]{2,1,0:T(8,128)(2,1)S(1)}, u32[]{:S(2)}, u32[]{:S(2)}) async-start(bf16[128,16,384]{2,1,0:T(8,128)(2,1)} %copy.60), calls=%async_computation | async-start | bytes 3145728 | tf_op jit(solution)/shard_map/all_to_all | solution.py:173
  26.1 1.9 gather_fusion.1
  28.1 0.6 compare_convert_fusion.cache_ok_ref
  28.7 1.1 select_convert_fusion.turn_ref
  29.7 2.8 %fusion.27 = (bf16[8,1,128,384]{3,2,1,0:T(8,128)(2,1)}, bf16[8,1,128,384]{3,2,1,0:T(8,128)(2,1)}) fusion(bf16[8,2,128,384]{3,2,1,0:T(8,128)(2,1)} %gather_fusion.1), kind=kLoop, calls=%fused_computation.67 | loop fusion | bytes 3145728 | tf_op jit(solution)/shard_map/slice | solution.py:181
  32.5 32.6 %all-to-all-done = bf16[128,16,384]{2,1,0:T(8,128)(2,1)S(1)} async-done(((bf16[128,16,384]{2,1,0:T(8,128)(2,1)}), bf16[128,16,384]{2,1,0:T(8,128)(2,1)S(1)}, u32[]{:S(2)}, u32[]{:S(2)}) %all-to-all-start) | async-done | bytes 1572896 | tf_op jit(solution)/shard_map/all_to_all | solution.py:173
  65.1 0.4 fusion.28
  65.6 2.4 %fusion.26 = s32[128]{0:T(128)S(1)} fusion(bf16[16,128,384]{2,0,1:T(8,128)(2,1)S(1)} %bitcast.59), kind=kLoop, calls=%fused_computation.66 | loop fusion | flops 128 | bytes 768 | tf_op jit(solution)/shard_map/convert_element_type | solution.py:175
  67.9 0.1 slice_convert_fusion
  68.0 0.8 copy.61
  68.9 0.8 copy.62
  69.7 0.8 copy.63
  70.6 0.2 reduce-window.8
  70.7 0.1 reduce.1
  70.9 0.5 multiply_sine_fusion
  71.4 0.1 tile.8
  71.5 1.3 copy.65.cos_ref
  72.8 0.1 tile.20
  72.9 1.3 copy.66.sin_ref
  74.2 0.6 copy_bitcast_fusion
  74.8 0.9 copy.76
  75.7 25.0 %shard_map.104 = bf16[128,1920]{1,0:T(8,128)(2,1)} custom-call(bf16[640,384]{1,0:T(8,128)(2,1)} %bitcast.67, bf16[640,384]{1,0:T(8,128)(2,1)} %bitcast.68, bf16[640,384]{1,0:T(8,128)(2,1)} %bitcast.69, bf16[1024,384]{1,0:T(8,128)(2,1)} %bitcast.66, bf16[1024,384]{1,0:T(8,128)(2,1)} %bitcast.65, f32[640,384]{1,0:T(8,128)} %copy.65.cos_ref, ...), custom_call_target="tpu_custom_call" | custom-call | tf_op jit(solution)/shard_map/pallas_call | solution.py:110
  100.6 1.3 copy.68
  101.9 1.2 copy.69
  103.1 9.1 %all-to-all-start.1 = ((bf16[128,15,128]{2,1,0:T(8,128)(2,1)}), bf16[128,15,128]{2,1,0:T(8,128)(2,1)S(1)}, u32[]{:S(2)}, u32[]{:S(2)}) async-start(bf16[128,15,128]{2,1,0:T(8,128)(2,1)} %copy.69), calls=%async_computation.1 | async-start | bytes 1048576 | tf_op jit(solution)/shard_map/all_to_all | solution.py:200
  112.2 4.3 %copy.70 = bf16[384,3072]{0,1:T(8,128)(2,1)} copy(bf16[384,3072]{1,0:T(8,128)(2,1)} %param.16) | data formatting | bytes 4718592 | tf_op args[7]
  116.5 4.3 %copy.71 = bf16[384,4,768]{2,0,1:T(8,128)(2,1)} copy(bf16[384,4,768]{0,2,1:T(8,128)(2,1)} %bitcast.61) | data formatting | bytes 4718592 | tf_op jit(solution)/shard_map/all_to_all | solution.py:155
  120.8 9.4 %all-to-all-done.1 = bf16[128,15,128]{2,1,0:T(8,128)(2,1)S(1)} async-done(((bf16[128,15,128]{2,1,0:T(8,128)(2,1)}), bf16[128,15,128]{2,1,0:T(8,128)(2,1)S(1)}, u32[]{:S(2)}, u32[]{:S(2)}) %all-to-all-start.1) | async-done | bytes 491552 | tf_op jit(solution)/shard_map/all_to_all | solution.py:200
  130.2 4.5 %all-to-all-start.3 = ((bf16[384,4,768]{2,0,1:T(8,128)(2,1)}), bf16[384,4,768]{2,0,1:T(8,128)(2,1)}, u32[]{:S(2)}, u32[]{:S(2)}) async-start(bf16[384,4,768]{2,0,1:T(8,128)(2,1)} %copy.71), calls=%async_computation.3 | async-start | bytes 4718592 | tf_op jit(solution)/shard_map/all_to_all | solution.py:155
  134.7 0.3 reshape.376
  135.0 1.2 gather_fusion.2
  136.2 28.9 %all-to-all-done.3 = bf16[384,4,768]{2,0,1:T(8,128)(2,1)} async-done(((bf16[384,4,768]{2,0,1:T(8,128)(2,1)}), bf16[384,4,768]{2,0,1:T(8,128)(2,1)}, u32[]{:S(2)}, u32[]{:S(2)}) %all-to-all-start.3) | async-done | bytes 2359328 | tf_op jit(solution)/shard_map/all_to_all | solution.py:155
  165.1 0.1 broadcast_in_dim.27
  165.2 15.1 %all_to_all.37 = bf16[4,256,384]{2,1,0:T(8,128)(2,1)S(1)} all-to-all(bf16[4,256,384]{2,1,0:T(8,128)(2,1)S(1)} %broadcast_in_dim.27), channel_id=1, replica_groups=mesh['req'=128,'tp'=4] {'tp'}, dimensions={0} | all-to-all | bytes 1572864 | tf_op jit(solution)/shard_map/all_to_all | solution.py:210
  180.3 2.5 %multiply_reduce_fusion = (f32[256]{0:T(256)S(1)}, f32[256,768]{1,0:T(8,128)S(1)}) fusion(bf16[4,256,384]{2,1,0:T(8,128)(2,1)S(1)} %all_to_all.37, bf16[384,4,768]{2,0,1:T(8,128)(2,1)} %all-to-all-done.3, bf16[256,768]{1,0:T(8,128)(2,1)S(1)} %copy-done.2), kind=kOutput, calls=%fused_computation.11 | convolution fusion | flops 604765952 | bytes 4326400 | tf_op jit(solution)/shard_map/tmc,tcn->mn/dot_general | solution.py:213
  182.8 0.6 broadcast_in_dim.30
  183.4 3.2 %all-to-all-start.4 = ((f32[4,1,256]{2,1,0:T(1,128)}), f32[4,1,256]{2,1,0:T(1,128)S(1)}, u32[]{:S(2)}, u32[]{:S(2)}) async-start(f32[4,1,256]{2,1,0:T(1,128)} %broadcast_in_dim.30), calls=%async_computation.4 | async-start | bytes 8192 | tf_op jit(solution)/shard_map/all_to_all | solution.py:222
  186.7 5.2 %all-to-all-done.4 = f32[4,1,256]{2,1,0:T(1,128)S(1)} async-done(((f32[4,1,256]{2,1,0:T(1,128)}), f32[4,1,256]{2,1,0:T(1,128)S(1)}, u32[]{:S(2)}, u32[]{:S(2)}) %all-to-all-start.4) | async-done | bytes 4128 | tf_op jit(solution)/shard_map/all_to_all | solution.py:222
  192.0 1.0 multiply_convert_fusion
  (27 shorter events, 0.2 us)
Async XLA Ops:
  0.6 25.5 %copy-start = (bf16[8,2,128,384]{3,2,1,0:T(8,128)(2,1)S(1)}, bf16[8,2,128,384]{3,2,1,0:T(8,128)(2,1)}, u32[]{:S(2)}) copy-start(bf16[8,2,128,384]{3,2,1,0:T(8,128)(2,1)} %param.14) | copy-start | bytes 4718596
  7.9 18.1 %copy-start.3 = (s32[1,8]{1,0:T(1,128)S(1)}, s32[1,8]{1,0:T(1,128)}, u32[]{:S(2)}) copy-start(s32[1,8]{1,0:T(1,128)} %param.13) | copy-start | bytes 100
  7.9 57.2 %all-to-all-start = ((bf16[128,16,384]{2,1,0:T(8,128)(2,1)}), bf16[128,16,384]{2,1,0:T(8,128)(2,1)S(1)}, u32[]{:S(2)}, u32[]{:S(2)}) async-start(bf16[128,16,384]{2,1,0:T(8,128)(2,1)} %copy.60), calls=%async_computation | async-start | bytes 3145728 | tf_op jit(solution)/shard_map/all_to_all | solution.py:173
  103.1 27.1 %all-to-all-start.1 = ((bf16[128,15,128]{2,1,0:T(8,128)(2,1)}), bf16[128,15,128]{2,1,0:T(8,128)(2,1)S(1)}, u32[]{:S(2)}, u32[]{:S(2)}) async-start(bf16[128,15,128]{2,1,0:T(8,128)(2,1)} %copy.69), calls=%async_computation.1 | async-start | bytes 1048576 | tf_op jit(solution)/shard_map/all_to_all | solution.py:200
  130.2 34.9 %all-to-all-start.3 = ((bf16[384,4,768]{2,0,1:T(8,128)(2,1)}), bf16[384,4,768]{2,0,1:T(8,128)(2,1)}, u32[]{:S(2)}, u32[]{:S(2)}) async-start(bf16[384,4,768]{2,0,1:T(8,128)(2,1)} %copy.71), calls=%async_computation.3 | async-start | bytes 4718592 | tf_op jit(solution)/shard_map/all_to_all | solution.py:155
  136.2 44.1 %copy-start.2 = (bf16[256,768]{1,0:T(8,128)(2,1)S(1)}, bf16[256,768]{1,0:T(8,128)(2,1)}, u32[]{:S(2)}) copy-start(bf16[256,768]{1,0:T(8,128)(2,1)} %param.15) | copy-start | bytes 1179652
  180.3 6.4 %copy-start.1 = (bf16[768]{0:T(1024)(128)(2,1)S(1)}, bf16[768]{0:T(1024)(128)(2,1)}, u32[]{:S(2)}) copy-start(bf16[768]{0:T(1024)(128)(2,1)} %param.17) | copy-start | bytes 4612
  183.4 8.5 %all-to-all-start.4 = ((f32[4,1,256]{2,1,0:T(1,128)}), f32[4,1,256]{2,1,0:T(1,128)S(1)}, u32[]{:S(2)}, u32[]{:S(2)}) async-start(f32[4,1,256]{2,1,0:T(1,128)} %broadcast_in_dim.30), calls=%async_computation.4 | async-start | bytes 8192 | tf_op jit(solution)/shard_map/all_to_all | solution.py:222

commit v8 on v6

--- a/solution.py
+++ b/solution.py
@@ -131,6 +131,10 @@
       cache_ok, k_rank)
 
 
+def tp_shift(x, k, tp_size):
+    return lax.ppermute(x, "tp", perm=[(i, (i + k) % tp_size) for i in range(tp_size)])
+
+
 def on_device(
     qkv_rows,
     row_request,
@@ -206,10 +210,23 @@
     )
     target = owner_dev * slot_cap + slot_in
     attn_rows = returned.reshape(buffer_len, head_cols)[target]
-    attn_all = lax.all_gather(attn_rows, "tp", axis=1, tiled=True)
-    mixed_cols = jnp.dot(attn_all, weight_cols, preferred_element_type=jnp.float32)
+    tp_size = lax.axis_size("tp")
+    tp_here = lax.axis_index("tp")
+    from_dev = (tp_here - jnp.arange(tp_size, dtype=jnp.int32)) % tp_size
+    weight_blocks = jnp.take(weight_cols.reshape(tp_size, head_cols, -1), from_dev, axis=0)
+    attn_all = jnp.stack([attn_rows] + [tp_shift(attn_rows, k, tp_size) for k in range(1, tp_size)])
+    mixed_cols = jnp.einsum(
+        "kmc,kcn->mn", attn_all, weight_blocks, preferred_element_type=jnp.float32
+    )
     hidden = residual.astype(jnp.float32) + mixed_cols
-    square_sum = lax.psum(jnp.sum(hidden * hidden, axis=1), "tp")
+    square_part = jnp.sum(hidden * hidden, axis=1)
+    shifted = jnp.stack(
+        [square_part] + [tp_shift(square_part, k, tp_size) for k in range(1, tp_size)]
+    )
+    by_source = jnp.take(shifted, (tp_here - jnp.arange(tp_size, dtype=jnp.int32)) % tp_size, axis=0)
+    square_sum = by_source[0]
+    for k in range(1, tp_size):
+        square_sum = square_sum + by_source[k]
     inv_rms = lax.rsqrt(square_sum / D + EPS)
     normed = hidden * inv_rms[:, None] * norm_gain.astype(jnp.float32)[None, :]
     return (hidden.astype(jnp.bfloat16), normed.astype(jnp.bfloat16))

time: 171 us -> 194 us (1.13)
  blocking collectives: 25.6 us -> 0 us
  starting transfers between devices: 31 us -> 52.4 us
  waiting for transfers between devices: 44.7 us -> 65.4 us
  local copies, waits for them, and re-layouts: 28.8 us -> 35.4 us
    ppermute x0 -> x6, starting transfers between devices: none -> 21.1 us  [tp_shift(): lax.ppermute(x, 'tp', perm=[(i, (i + k) % tp_size) for i in range(tp_size)])]
    all_to_all x1, waiting for transfers between devices: 0.01 us -> 17.3 us  [on_device(): lax.all_to_all(out_weight, 'tp', split_axis=1, concat_axis=0, tiled=True)]
    all_gather x1 -> x0, blocking collectives: 15.6 us -> none  [on_device(): attn_all = lax.all_gather(attn_rows, 'tp', axis=1, tiled=True)]
    psum x1 -> x0, blocking collectives: 10 us -> none  [on_device(): square_sum = lax.psum(jnp.sum(hidden * hidden, axis=1), 'tp')]
    ppermute x0 -> x6, waiting for transfers between devices: none -> 6.09 us  [tp_shift(): lax.ppermute(x, 'tp', perm=[(i, (i + k) % tp_size) for i in range(tp_size)])]
    gather x0 -> x2, local copies, waits for them, and re-layouts: none -> 4.38 us  [the longest x1 3.82 us: on_device(): jnp.take(weight_cols.reshape(tp_size, head_cols, -1), from_dev, axis=0)]
    all_to_all x1, waiting for transfers between devices: 13.6 us -> 9.45 us  [on_device(): lax.all_to_all(result.reshape(devices, slot_cap * parts, head_cols // par...]
    slice x4, local copies, waits for them, and re-layouts: 3.09 us -> 5.35 us  [on_device(): planes[p * slot_cap:(p + 1) * slot_cap].reshape(buffer_len, head_cols)]
  transfers between devices with their start and end apart: 3 -> 9, of which waited for: 2 -> 5; matrix products, arithmetic and copies ran while one was open for 17% -> 11% of each run, Pallas kernels for 15% -> 0%
where the time goes in v8:
time: 194 us; the launch traced here: 192 us
  waiting for transfers between devices  65.4 us (34%)
  starting transfers between devices  52.4 us (27%)
  local copies, waits for them, and re-layouts  35.4 us (18%)
  Pallas kernels  25 us (13%)
  other arithmetic  7.51 us (4%)
  matrix products  4.3 us (2%)
    all_to_all x1, waiting for transfers between devices, on_device(): lax.all_to_all(outgoing, 'req', split_axis=0, concat_axis=0, tiled=True)  32.6 us
    pallas_call x1, Pallas kernels, attend_slots(): pl.pallas_call(attend_kernel, out_shape=jax.ShapeDtypeStruct((block, slot...  25 us
    ppermute x6, starting transfers between devices, tp_shift(): lax.ppermute(x, 'tp', perm=[(i, (i + k) % tp_size) for i in range(tp_size)])  21.1 us
    all_to_all x1, starting transfers between devices, on_device(): lax.all_to_all(outgoing, 'req', split_axis=0, concat_axis=0, tiled=True)  17.5 us
    all_to_all x1, waiting for transfers between devices, on_device(): lax.all_to_all(out_weight, 'tp', split_axis=1, concat_axis=0, tiled=True)  17.3 us
    all_to_all x1, waiting for transfers between devices, on_device(): lax.all_to_all(result.reshape(devices, slot_cap * parts, head_cols // par...  9.45 us
    all_to_all x1, starting transfers between devices, on_device(): lax.all_to_all(result.reshape(devices, slot_cap * parts, head_cols // par...  9.04 us
    ppermute x6, waiting for transfers between devices, tp_shift(): lax.ppermute(x, 'tp', perm=[(i, (i + k) % tp_size) for i in range(tp_size)])  6.09 us
  transfers between devices with their start and end apart: 9, of which 5 were waited for; matrix products, arithmetic and copies ran while one was open for 11% of the time, Pallas kernels for 0%

profile of v8, /device:TPU:56, one launch (start us, length us, event | category | flops | bytes accessed | tf_op | source)
XLA Modules:
  0.0 191.6 jit_solution(3877867275806203551)
XLA Ops:
  0.6 0.8 compare_select_fusion.1
  1.5 1.9 gather_fusion
  3.3 0.2 convert_reduce_fusion
  3.7 1.7 fusion.3
  5.4 0.2 copy.44
  5.7 0.2 pad_maximum_fusion
  5.9 2.1 %copy.45 = bf16[128,16,384]{2,1,0:T(8,128)(2,1)} copy(bf16[128,16,384]{2,0,1:T(8,128)(2,1)S(1)} %pad_maximum_fusion) | data formatting | bytes 3145728 | tf_op jit(solution)/shard_map/concatenate | solution.py:174
  7.9 17.5 %all-to-all-start = ((bf16[128,16,384]{2,1,0:T(8,128)(2,1)}), bf16[128,16,384]{2,1,0:T(8,128)(2,1)S(1)}, u32[]{:S(2)}, u32[]{:S(2)}) async-start(bf16[128,16,384]{2,1,0:T(8,128)(2,1)} %copy.45), calls=%async_computation | async-start | bytes 3145728 | tf_op jit(solution)/shard_map/all_to_all | solution.py:177
  26.1 1.9 %gather_fusion.1 = bf16[8,2,128,384]{3,2,1,0:T(8,128)(2,1)} fusion(bf16[8,2,128,384]{3,2,1,0:T(8,128)(2,1)S(1)} %copy-done, s32[1024]{0:T(1024)S(1)} %pad_clamp_fusion.2), kind=kCustom, calls=%fused_computation.1 | custom fusion | bytes 3145760 | tf_op jit(solution)/shard_map/gather | solution.py:182
  28.1 0.6 compare_convert_fusion.cache_ok_ref
  28.7 1.1 select_convert_fusion.turn_ref
  29.7 2.7 %fusion.42 = (bf16[8,1,128,384]{3,2,1,0:T(8,128)(2,1)}, bf16[8,1,128,384]{3,2,1,0:T(8,128)(2,1)}) fusion(bf16[8,2,128,384]{3,2,1,0:T(8,128)(2,1)} %gather_fusion.1), kind=kLoop, calls=%fused_computation.99 | loop fusion | bytes 3145728 | tf_op jit(solution)/shard_map/slice | solution.py:185
  32.5 32.6 %all-to-all-done = bf16[128,16,384]{2,1,0:T(8,128)(2,1)S(1)} async-done(((bf16[128,16,384]{2,1,0:T(8,128)(2,1)}), bf16[128,16,384]{2,1,0:T(8,128)(2,1)S(1)}, u32[]{:S(2)}, u32[]{:S(2)}) %all-to-all-start) | async-done | bytes 1572896 | tf_op jit(solution)/shard_map/all_to_all | solution.py:177
  65.1 2.4 %fusion.41 = s32[128]{0:T(128)S(1)} fusion(bf16[16,128,384]{2,0,1:T(8,128)(2,1)S(1)} %bitcast.60), kind=kLoop, calls=%fused_computation.98 | loop fusion | flops 128 | bytes 768 | tf_op jit(solution)/shard_map/convert_element_type | solution.py:179
  67.4 0.1 slice_convert_fusion
  67.6 1.6 fusion.43
  69.2 0.2 reduce-window.8
  69.5 0.5 multiply_sine_fusion
  70.1 1.3 copy.50.cos_ref
  71.5 1.3 copy.51.sin_ref
  72.8 0.6 copy_bitcast_fusion
  73.4 0.9 copy.59
  74.3 2.0 %copy.46 = bf16[5,128,384]{2,1,0:T(8,128)(2,1)} copy(bf16[5,128,384]{2,0,1:T(8,128)(2,1)} %get-tuple-element.6) | data formatting | bytes 983040 | tf_op jit(solution)/shard_map/slice | solution.py:197
  76.3 0.8 copy.47
  77.2 0.9 copy.48
  78.0 25.0 %shard_map.104 = bf16[128,1920]{1,0:T(8,128)(2,1)} custom-call(bf16[640,384]{1,0:T(8,128)(2,1)} %bitcast.69, bf16[640,384]{1,0:T(8,128)(2,1)} %bitcast.70, bf16[640,384]{1,0:T(8,128)(2,1)} %bitcast.71, bf16[1024,384]{1,0:T(8,128)(2,1)} %bitcast.68, bf16[1024,384]{1,0:T(8,128)(2,1)} %bitcast.67, f32[640,384]{1,0:T(8,128)} %copy.50.cos_ref, ...), custom_call_target="tpu_custom_call" | custom-call | tf_op jit(solution)/shard_map/pallas_call | solution.py:110
  103.0 1.3 copy.53
  104.3 1.2 copy.54
  105.5 9.0 %all-to-all-start.1 = ((bf16[128,15,128]{2,1,0:T(8,128)(2,1)}), bf16[128,15,128]{2,1,0:T(8,128)(2,1)S(1)}, u32[]{:S(2)}, u32[]{:S(2)}) async-start(bf16[128,15,128]{2,1,0:T(8,128)(2,1)} %copy.54), calls=%async_computation.1 | async-start | bytes 1048576 | tf_op jit(solution)/shard_map/all_to_all | solution.py:204
  114.6 4.3 %copy.55 = bf16[384,3072]{0,1:T(8,128)(2,1)} copy(bf16[384,3072]{1,0:T(8,128)(2,1)} %param.16) | data formatting | bytes 4718592 | tf_op args[7]
  118.8 4.3 %copy.56 = bf16[384,4,768]{2,0,1:T(8,128)(2,1)} copy(bf16[384,4,768]{0,2,1:T(8,128)(2,1)} %bitcast.63) | data formatting | bytes 4718592 | tf_op jit(solution)/shard_map/all_to_all | solution.py:159
  123.1 9.5 %all-to-all-done.1 = bf16[128,15,128]{2,1,0:T(8,128)(2,1)S(1)} async-done(((bf16[128,15,128]{2,1,0:T(8,128)(2,1)}), bf16[128,15,128]{2,1,0:T(8,128)(2,1)S(1)}, u32[]{:S(2)}, u32[]{:S(2)}) %all-to-all-start.1) | async-done | bytes 491552 | tf_op jit(solution)/shard_map/all_to_all | solution.py:204
  132.6 4.7 %all-to-all-start.2 = ((bf16[384,4,768]{2,0,1:T(8,128)(2,1)}), bf16[384,4,768]{2,0,1:T(8,128)(2,1)}, u32[]{:S(2)}, u32[]{:S(2)}) async-start(bf16[384,4,768]{2,0,1:T(8,128)(2,1)} %copy.56), calls=%async_computation.2 | async-start | bytes 4718592 | tf_op jit(solution)/shard_map/all_to_all | solution.py:159
  137.4 0.3 reshape.445
  137.7 1.2 gather_fusion.2
  138.8 3.6 %collective-permute-start = (bf16[256,384]{1,0:T(8,128)(2,1)S(1)}, bf16[256,384]{1,0:T(8,128)(2,1)S(1)}, u32[]{:S(2)}, u32[]{:S(2)}) collective-permute-start(bf16[256,384]{1,0:T(8,128)(2,1)S(1)} %gather_fusion.2), channel_id=1, source_target_pairs={{0,1},{1,2},{2,3},{3,0},{4,5},{5,6},{6,7},{7,4},{8,9},{9,10},{10,1... | collective-permute-start | bytes 589832 | tf_op jit(solution)/shard_map/ppermute | solution.py:135
  142.5 4.6 %collective-permute-start.1 = (bf16[256,384]{1,0:T(8,128)(2,1)S(1)}, bf16[256,384]{1,0:T(8,128)(2,1)S(1)}, u32[]{:S(2)}, u32[]{:S(2)}) collective-permute-start(bf16[256,384]{1,0:T(8,128)(2,1)S(1)} %gather_fusion.2), channel_id=1, source_target_pairs={{0,2},{1,3},{2,0},{3,1},{4,6},{5,7},{6,4},{7,5},{8,10},{9,11},{10,... | collective-permute-start | bytes 589832 | tf_op jit(solution)/shard_map/ppermute | solution.py:135
  147.1 3.4 %collective-permute-start.2 = (bf16[256,384]{1,0:T(8,128)(2,1)S(1)}, bf16[256,384]{1,0:T(8,128)(2,1)S(1)}, u32[]{:S(2)}, u32[]{:S(2)}) collective-permute-start(bf16[256,384]{1,0:T(8,128)(2,1)S(1)} %gather_fusion.2), channel_id=1, source_target_pairs={{0,3},{1,0},{2,1},{3,2},{4,7},{5,4},{6,5},{7,6},{8,11},{9,8},{10,9... | collective-permute-start | bytes 589832 | tf_op jit(solution)/shard_map/ppermute | solution.py:135
  150.5 17.3 %all-to-all-done.2 = bf16[384,4,768]{2,0,1:T(8,128)(2,1)} async-done(((bf16[384,4,768]{2,0,1:T(8,128)(2,1)}), bf16[384,4,768]{2,0,1:T(8,128)(2,1)}, u32[]{:S(2)}, u32[]{:S(2)}) %all-to-all-start.2) | async-done | bytes 2359328 | tf_op jit(solution)/shard_map/all_to_all | solution.py:159
  167.7 3.8 %gather_fusion.3 = bf16[4,384,768]{2,1,0:T(8,128)(2,1)} fusion(bf16[4,384,768]{2,1,0:T(8,128)(2,1)} %bitcast.26, s32[1024]{0:T(1024)S(1)} %pad_clamp_fusion), kind=kCustom, calls=%fused_computation.3 | custom fusion | bytes 4718608 | tf_op jit(solution)/shard_map/jit(_take)/gather | solution.py:216
  171.6 4.3 %collective-permute-done.1 = bf16[256,384]{1,0:T(8,128)(2,1)S(1)} collective-permute-done((bf16[256,384]{1,0:T(8,128)(2,1)S(1)}, bf16[256,384]{1,0:T(8,128)(2,1)S(1)}, u32[]{:S(2)}, u32[]{:S(2)}) %collective-permute-start.1) | collective-permute-done | bytes 196640 | tf_op jit(solution)/shard_map/ppermute | solution.py:135
  175.9 2.6 %multiply_reduce_fusion = (f32[256]{0:T(256)S(1)}, f32[256,768]{1,0:T(8,128)S(1)}) fusion(bf16[4,384,768]{2,1,0:T(8,128)(2,1)} %gather_fusion.3, pred[4]{0:T(512)(128)(4,1)S(1)} %compare_and_fusion.2, bf16[1,256,384]{2,1,0:T(8,128)(2,1)S(1)} %bitcast.85, bf16[1,256,384]{2,1,0:T(8,128)(2,1)S(1)} %bitcast.84, bf16[1,256,384]{2,1,0:T(8,128)(2,1)S(1)} %bitcast.83, ...), kind=kOutput, calls=%fused_computation.22 | convolution fusion | flops 607125248 | bytes 4326404 | tf_op jit(solution)/shard_map/kmc,kcn->mn/dot_general | solution.py:218
  178.5 1.9 %collective-permute-start.3 = (f32[256]{0:T(256)S(1)}, f32[256]{0:T(256)S(1)}, u32[]{:S(2)}, u32[]{:S(2)}) collective-permute-start(f32[256]{0:T(256)S(1)} %get-tuple-element.14), channel_id=1, source_target_pairs={{0,1},{1,2},{2,3},{3,0},{4,5},{5,6},{6,7},{7,4},{8,9},{9,10},{10,1... | collective-permute-start | bytes 3080 | tf_op jit(solution)/shard_map/ppermute | solution.py:135
  180.5 3.4 %collective-permute-start.4 = (f32[256]{0:T(256)S(1)}, f32[256]{0:T(256)S(1)}, u32[]{:S(2)}, u32[]{:S(2)}) collective-permute-start(f32[256]{0:T(256)S(1)} %get-tuple-element.14), channel_id=1, source_target_pairs={{0,2},{1,3},{2,0},{3,1},{4,6},{5,7},{6,4},{7,5},{8,10},{9,11},{10,... | collective-permute-start | bytes 3080 | tf_op jit(solution)/shard_map/ppermute | solution.py:135
  183.9 4.2 %collective-permute-start.5 = (f32[256]{0:T(256)S(1)}, f32[256]{0:T(256)S(1)}, u32[]{:S(2)}, u32[]{:S(2)}) collective-permute-start(f32[256]{0:T(256)S(1)} %get-tuple-element.14), channel_id=1, source_target_pairs={{0,3},{1,0},{2,1},{3,2},{4,7},{5,4},{6,5},{7,6},{8,11},{9,8},{10,9... | collective-permute-start | bytes 3080 | tf_op jit(solution)/shard_map/ppermute | solution.py:135
  188.2 1.8 collective-permute-done.5
  189.9 0.6 gather_fusion.4
  190.6 1.0 multiply_convert_fusion
  (44 shorter events, 0.8 us)
Async XLA Ops:
  0.6 25.5 %copy-start = (bf16[8,2,128,384]{3,2,1,0:T(8,128)(2,1)S(1)}, bf16[8,2,128,384]{3,2,1,0:T(8,128)(2,1)}, u32[]{:S(2)}) copy-start(bf16[8,2,128,384]{3,2,1,0:T(8,128)(2,1)} %param.14) | copy-start | bytes 4718596
  7.9 18.1 %copy-start.5 = (s32[1,8]{1,0:T(1,128)S(1)}, s32[1,8]{1,0:T(1,128)}, u32[]{:S(2)}) copy-start(s32[1,8]{1,0:T(1,128)} %param.13) | copy-start | bytes 100
  7.9 57.2 %all-to-all-start = ((bf16[128,16,384]{2,1,0:T(8,128)(2,1)}), bf16[128,16,384]{2,1,0:T(8,128)(2,1)S(1)}, u32[]{:S(2)}, u32[]{:S(2)}) async-start(bf16[128,16,384]{2,1,0:T(8,128)(2,1)} %copy.45), calls=%async_computation | async-start | bytes 3145728 | tf_op jit(solution)/shard_map/all_to_all | solution.py:177
  71.5 4.8 %copy-start.2 = (bf16[5,128,384]{2,0,1:T(8,128)(2,1)S(1)}, bf16[5,128,384]{2,0,1:T(8,128)(2,1)}, u32[]{:S(2)}) copy-start(bf16[5,128,384]{2,0,1:T(8,128)(2,1)} %get-tuple-element.5) | copy-start | bytes 1474564
  72.8 4.3 %copy-start.1 = (bf16[5,128,384]{2,0,1:T(8,128)(2,1)S(1)}, bf16[5,128,384]{2,0,1:T(8,128)(2,1)}, u32[]{:S(2)}) copy-start(bf16[5,128,384]{2,0,1:T(8,128)(2,1)} %get-tuple-element.4) | copy-start | bytes 1474564
  105.5 27.0 %all-to-all-start.1 = ((bf16[128,15,128]{2,1,0:T(8,128)(2,1)}), bf16[128,15,128]{2,1,0:T(8,128)(2,1)S(1)}, u32[]{:S(2)}, u32[]{:S(2)}) async-start(bf16[128,15,128]{2,1,0:T(8,128)(2,1)} %copy.54), calls=%async_computation.1 | async-start | bytes 1048576 | tf_op jit(solution)/shard_map/all_to_all | solution.py:204
  132.6 35.2 %all-to-all-start.2 = ((bf16[384,4,768]{2,0,1:T(8,128)(2,1)}), bf16[384,4,768]{2,0,1:T(8,128)(2,1)}, u32[]{:S(2)}, u32[]{:S(2)}) async-start(bf16[384,4,768]{2,0,1:T(8,128)(2,1)} %copy.56), calls=%async_computation.2 | async-start | bytes 4718592 | tf_op jit(solution)/shard_map/all_to_all | solution.py:159
  138.8 32.7 %collective-permute-start = (bf16[256,384]{1,0:T(8,128)(2,1)S(1)}, bf16[256,384]{1,0:T(8,128)(2,1)S(1)}, u32[]{:S(2)}, u32[]{:S(2)}) collective-permute-start(bf16[256,384]{1,0:T(8,128)(2,1)S(1)} %gather_fusion.2), channel_id=1, source_target_pairs={{0,1},{1,2},{2,3},{3,0},{4,5},{5,6},{6,7},{7,4},{8,9},{9,10},{10,1... | collective-permute-start | bytes 589832 | tf_op jit(solution)/shard_map/ppermute | solution.py:135
  142.5 33.4 %collective-permute-start.1 = (bf16[256,384]{1,0:T(8,128)(2,1)S(1)}, bf16[256,384]{1,0:T(8,128)(2,1)S(1)}, u32[]{:S(2)}, u32[]{:S(2)}) collective-permute-start(bf16[256,384]{1,0:T(8,128)(2,1)S(1)} %gather_fusion.2), channel_id=1, source_target_pairs={{0,2},{1,3},{2,0},{3,1},{4,6},{5,7},{6,4},{7,5},{8,10},{9,11},{10,... | collective-permute-start | bytes 589832 | tf_op jit(solution)/shard_map/ppermute | solution.py:135
  147.1 28.8 %collective-permute-start.2 = (bf16[256,384]{1,0:T(8,128)(2,1)S(1)}, bf16[256,384]{1,0:T(8,128)(2,1)S(1)}, u32[]{:S(2)}, u32[]{:S(2)}) collective-permute-start(bf16[256,384]{1,0:T(8,128)(2,1)S(1)} %gather_fusion.2), channel_id=1, source_target_pairs={{0,3},{1,0},{2,1},{3,2},{4,7},{5,4},{6,5},{7,6},{8,11},{9,8},{10,9... | collective-permute-start | bytes 589832 | tf_op jit(solution)/shard_map/ppermute | solution.py:135
  167.7 8.2 %copy-start.4 = (bf16[256,768]{1,0:T(8,128)(2,1)S(1)}, bf16[256,768]{1,0:T(8,128)(2,1)}, u32[]{:S(2)}) copy-start(bf16[256,768]{1,0:T(8,128)(2,1)} %param.15) | copy-start | bytes 1179652
  175.9 12.2 %copy-start.3 = (bf16[768]{0:T(1024)(128)(2,1)S(1)}, bf16[768]{0:T(1024)(128)(2,1)}, u32[]{:S(2)}) copy-start(bf16[768]{0:T(1024)(128)(2,1)} %param.17) | copy-start | bytes 4612
  178.5 9.6 %collective-permute-start.3 = (f32[256]{0:T(256)S(1)}, f32[256]{0:T(256)S(1)}, u32[]{:S(2)}, u32[]{:S(2)}) collective-permute-start(f32[256]{0:T(256)S(1)} %get-tuple-element.14), channel_id=1, source_target_pairs={{0,1},{1,2},{2,3},{3,0},{4,5},{5,6},{6,7},{7,4},{8,9},{9,10},{10,1... | collective-permute-start | bytes 3080 | tf_op jit(solution)/shard_map/ppermute | solution.py:135
  180.5 7.7 %collective-permute-start.4 = (f32[256]{0:T(256)S(1)}, f32[256]{0:T(256)S(1)}, u32[]{:S(2)}, u32[]{:S(2)}) collective-permute-start(f32[256]{0:T(256)S(1)} %get-tuple-element.14), channel_id=1, source_target_pairs={{0,2},{1,3},{2,0},{3,1},{4,6},{5,7},{6,4},{7,5},{8,10},{9,11},{10,... | collective-permute-start | bytes 3080 | tf_op jit(solution)/shard_map/ppermute | solution.py:135
  183.9 6.0 %collective-permute-start.5 = (f32[256]{0:T(256)S(1)}, f32[256]{0:T(256)S(1)}, u32[]{:S(2)}, u32[]{:S(2)}) collective-permute-start(f32[256]{0:T(256)S(1)} %get-tuple-element.14), channel_id=1, source_target_pairs={{0,3},{1,0},{2,1},{3,2},{4,7},{5,4},{6,5},{7,6},{8,11},{9,8},{10,9... | collective-permute-start | bytes 3080 | tf_op jit(solution)/shard_map/ppermute | solution.py:135

commit v9 on v6

--- a/solution.py
+++ b/solution.py
@@ -49,13 +49,16 @@
     return (field.astype(jnp.float32) * cos_all + turned * sin_all).astype(jnp.bfloat16)
 
 
-def turn_rows(field, cos_rows, sin_rows, turn):
+def turn_rows(field, positions, inverse, turn):
+    angles = positions.astype(jnp.float32) * inverse
     turned = jnp.dot(field, turn, preferred_element_type=jnp.float32)
-    return (field.astype(jnp.float32) * cos_rows + turned * sin_rows).astype(jnp.bfloat16)
+    return (field.astype(jnp.float32) * jnp.cos(angles) + turned * jnp.sin(angles)).astype(
+        jnp.bfloat16
+    )
 
 
 def attend_kernel(
-    q_ref, kn_ref, vn_ref, kc_ref, vc_ref, cos_ref, sin_ref, turn_ref, qrank_ref, cache_ok_ref,
+    q_ref, kn_ref, vn_ref, kc_ref, vc_ref, pos_ref, inv_ref, turn_ref, qrank_ref, cache_ok_ref,
     krank_ref, o_ref, keys_ref,
 ):
     step = pl.program_id(0)
@@ -63,10 +66,10 @@
 
     @pl.when(step == 0)
     def _():
-        keys_ref[...] = turn_rows(kn_ref[...], cos_ref[...], sin_ref[...], turn_ref[...])
+        keys_ref[...] = turn_rows(kn_ref[...], pos_ref[...], inv_ref[...], turn_ref[...])
 
     here = pl.ds(pl.multiple_of(step * block, block), block)
-    query = turn_rows(q_ref[...], cos_ref[here, :], sin_ref[here, :], turn_ref[...])
+    query = turn_rows(q_ref[...], pos_ref[here, :], inv_ref[...], turn_ref[...])
     score_scale = 1.0 / math.sqrt(HEAD_SIZE)
     cols = query.shape[1]
     col_head = lax.broadcasted_iota(jnp.int32, (1, cols), 1) // HEAD_SIZE
@@ -101,7 +104,7 @@
     o_ref[...] = total.astype(o_ref.dtype)
 
 
-def attend_slots(query, fresh_keys, fresh_values, cache_keys, cache_values, cos_all, sin_all, turn,
+def attend_slots(query, fresh_keys, fresh_values, cache_keys, cache_values, positions, inverse, turn,
                  q_rank, cache_ok, k_rank, slot_cap):
     rows, cols = query.shape
     block = rows // slot_cap
@@ -117,8 +120,8 @@
             pl.BlockSpec((rows, cols), whole),
             pl.BlockSpec((span, cols), whole),
             pl.BlockSpec((span, cols), whole),
-            pl.BlockSpec((rows, cols), whole),
-            pl.BlockSpec((rows, cols), whole),
+            pl.BlockSpec((rows, 1), whole),
+            pl.BlockSpec((1, cols), whole),
             pl.BlockSpec((cols, cols), whole),
             pl.BlockSpec((block, 1), lambda i: (i, 0)),
             pl.BlockSpec((1, span), whole),
@@ -127,7 +130,7 @@
         out_specs=pl.BlockSpec((block, cols), lambda i: (0, i)),
         scratch_shapes=[pltpu.VMEM((rows, cols), jnp.bfloat16)],
         compiler_params=pltpu.CompilerParams(dimension_semantics=("arbitrary",)),
-    )(query, fresh_keys, fresh_values, cache_keys, cache_values, cos_all, sin_all, turn, q_rank,
+    )(query, fresh_keys, fresh_values, cache_keys, cache_values, positions, inverse, turn, q_rank,
       cache_ok, k_rank)
 
 
@@ -183,9 +186,10 @@
     before = jnp.cumsum(arrived_counts) - arrived_counts
     live_slot = (slot_of < arrived_counts[None, :]).reshape(buffer_len)
     new_rank = (before[None, :] + slot_of).reshape(buffer_len)
-    cosine, sine_tab = rope_tables(length + new_rank)
-    cos_all = jnp.tile(cosine, (1, heads_here))
-    sin_all = jnp.tile(sine_tab, (1, heads_here))
+    positions = (length + new_rank)[:, None]
+    halves = HEAD_SIZE // 2
+    inverse = ROPE_BASE ** (-2.0 * jnp.arange(halves, dtype=jnp.float32) / HEAD_SIZE)
+    inverse = jnp.tile(inverse, 2 * heads_here)[None, :]
     cache_ok = (jnp.arange(cache_span, dtype=jnp.int32) < length).astype(jnp.int32)[None, :]
     k_rank = jnp.where(live_slot, new_rank, jnp.int32(2**30))[None, :]
     q_rank = new_rank[:, None]
@@ -194,7 +198,7 @@
         for p in range(parts)
     ]
     result = attend_slots(
-        part_rows[0], part_rows[1], part_rows[2], cache_keys, cache_values, cos_all, sin_all,
+        part_rows[0], part_rows[1], part_rows[2], cache_keys, cache_values, positions, inverse,
         turn_matrix(head_cols), q_rank, cache_ok, k_rank, slot_cap,
     )
     returned = lax.all_to_all(

time: 171 us -> 174 us (1.018)
  Pallas kernels: 25 us -> 30.8 us
  local copies, waits for them, and re-layouts: 28.8 us -> 26 us
    pallas_call x1, Pallas kernels: 25 us -> 30.8 us  [attend_slots(): pl.pallas_call(attend_kernel, out_shape=jax.ShapeDtypeStruct((block, slot...]
    another operation x4 -> x2, local copies, waits for them, and re-layouts: 2.75 us -> 0.65 us  [on_device(): inverse = jnp.tile(inverse, 2 * heads_here)[None, :]]
    unnamed x10 -> x12, local copies, waits for them, and re-layouts: 5.23 us -> 4.49 us
  transfers between devices with their start and end apart: 3 -> 3, of which waited for: 2 -> 2; matrix products, arithmetic and copies ran while one was open for 17% -> 15% of each run, Pallas kernels for 15% -> 18%
where the time goes in v9:
time: 174 us; the launch traced here: 172 us
  waiting for transfers between devices  44.7 us (26%)
  starting transfers between devices  31.3 us (18%)
  Pallas kernels  30.8 us (18%)
  local copies, waits for them, and re-layouts  26 us (15%)
  blocking collectives  25.6 us (15%)
  other arithmetic  7.6 us (4%)
  matrix products  4.19 us (2%)
    all_to_all x1, waiting for transfers between devices, on_device(): lax.all_to_all(outgoing, 'req', split_axis=0, concat_axis=0, tiled=True)  31 us
    pallas_call x1, Pallas kernels, attend_slots(): pl.pallas_call(attend_kernel, out_shape=jax.ShapeDtypeStruct((block, slot...  30.8 us
    all_to_all x1, starting transfers between devices, on_device(): lax.all_to_all(outgoing, 'req', split_axis=0, concat_axis=0, tiled=True)  17.3 us
    all_gather x1, blocking collectives, on_device(): attn_all = lax.all_gather(attn_rows, 'tp', axis=1, tiled=True)  15.6 us
    all_to_all x1, waiting for transfers between devices, on_device(): lax.all_to_all(result.reshape(devices, slot_cap * parts, head_cols // par...  13.6 us
    psum x1, blocking collectives, on_device(): square_sum = lax.psum(jnp.sum(hidden * hidden, axis=1), 'tp')  10 us
    all_to_all x1, starting transfers between devices, on_device(): lax.all_to_all(result.reshape(devices, slot_cap * parts, head_cols // par...  9.27 us
    all_to_all x1, starting transfers between devices, on_device(): lax.all_to_all(out_weight, 'tp', split_axis=1, concat_axis=0, tiled=True)  4.68 us
  transfers between devices with their start and end apart: 3, of which 2 were waited for; matrix products, arithmetic and copies ran while one was open for 15% of the time, Pallas kernels for 18%

profile of v9, /device:TPU:56, one launch (start us, length us, event | category | flops | bytes accessed | tf_op | source)
XLA Modules:
  0.0 171.7 jit_solution(11684840026220295174)
XLA Ops:
  0.6 0.0 copy-start
  0.6 0.8 compare_select_fusion.1
  1.5 1.9 %gather_fusion = s32[256]{0:T(256)S(1)} fusion(s32[128]{0:T(128)} %param.11, s32[1024]{0:T(1024)S(1)} %pad_clamp_fusion.2), kind=kCustom, calls=%fused_computation | custom fusion | bytes 3072 | tf_op jit(solution)/shard_map/gather | solution.py:159
  3.3 0.2 convert_reduce_fusion
  3.6 0.1 convert_reduce_fusion.1
  3.7 1.7 fusion
  5.4 0.2 copy.53
  5.6 0.1 broadcast_in_dim.17
  5.7 0.2 pad_maximum_fusion
  5.9 2.1 %copy.54 = bf16[128,16,384]{2,1,0:T(8,128)(2,1)} copy(bf16[128,16,384]{2,0,1:T(8,128)(2,1)S(1)} %pad_maximum_fusion) | data formatting | bytes 3145728 | tf_op jit(solution)/shard_map/concatenate | solution.py:173
  8.0 17.3 %all-to-all-start = ((bf16[128,16,384]{2,1,0:T(8,128)(2,1)}), bf16[128,16,384]{2,1,0:T(8,128)(2,1)S(1)}, u32[]{:S(2)}, u32[]{:S(2)}) async-start(bf16[128,16,384]{2,1,0:T(8,128)(2,1)} %copy.54), calls=%async_computation | async-start | bytes 3145728 | tf_op jit(solution)/shard_map/all_to_all | solution.py:176
  26.0 0.6 broadcast_in_dim_tile.3.inv_ref
  26.6 4.3 %copy.64 = bf16[384,3072]{0,1:T(8,128)(2,1)} copy(bf16[384,3072]{1,0:T(8,128)(2,1)} %param.16) | data formatting | bytes 4718592 | tf_op args[7]
  30.9 0.0 copy-done.4
  30.9 0.0 copy-done
  30.9 1.9 %gather_fusion.1 = bf16[8,2,128,384]{3,2,1,0:T(8,128)(2,1)} fusion(bf16[8,2,128,384]{3,2,1,0:T(8,128)(2,1)S(1)} %copy-done, s32[1024]{0:T(1024)S(1)} %pad_clamp_fusion.1), kind=kCustom, calls=%fused_computation.1 | custom fusion | bytes 3145760 | tf_op jit(solution)/shard_map/gather | solution.py:181
  32.9 1.1 select_convert_fusion.turn_ref
  34.0 31.0 %all-to-all-done = bf16[128,16,384]{2,1,0:T(8,128)(2,1)S(1)} async-done(((bf16[128,16,384]{2,1,0:T(8,128)(2,1)}), bf16[128,16,384]{2,1,0:T(8,128)(2,1)S(1)}, u32[]{:S(2)}, u32[]{:S(2)}) %all-to-all-start) | async-done | bytes 1572896 | tf_op jit(solution)/shard_map/all_to_all | solution.py:176
  65.0 4.7 %all-to-all-start.2 = ((bf16[384,4,768]{0,2,1:T(8,128)(2,1)}), bf16[384,4,768]{0,2,1:T(8,128)(2,1)}, u32[]{:S(2)}, u32[]{:S(2)}) async-start(bf16[384,4,768]{0,2,1:T(8,128)(2,1)} %bitcast.48), calls=%async_computation.2 | async-start | bytes 4718592 | tf_op jit(solution)/shard_map/all_to_all | solution.py:158
  69.7 0.6 compare_convert_fusion.cache_ok_ref
  70.3 2.8 %fusion.19 = (bf16[8,1,128,384]{3,2,1,0:T(8,128)(2,1)}, bf16[8,1,128,384]{3,2,1,0:T(8,128)(2,1)}) fusion(bf16[8,2,128,384]{3,2,1,0:T(8,128)(2,1)} %gather_fusion.1), kind=kLoop, calls=%fused_computation.60 | loop fusion | bytes 3145728 | tf_op jit(solution)/shard_map/slice | solution.py:184
  73.1 0.1 slice_convert_fusion
  73.2 0.2 reduce-window.8
  73.4 0.1 reduce
  73.5 2.4 %fusion.18 = s32[128]{0:T(128)S(1)} fusion(bf16[16,128,384]{2,0,1:T(8,128)(2,1)S(1)} %bitcast.46), kind=kLoop, calls=%fused_computation.59 | loop fusion | flops 128 | bytes 768 | tf_op jit(solution)/shard_map/convert_element_type | solution.py:178
  75.9 0.6 copy_bitcast_fusion
  76.4 0.2 copy.68
  76.6 0.0 copy-start.1
  76.6 0.4 fusion.20
  77.1 0.9 copy.55
  77.9 0.9 copy.56
  78.8 0.9 copy.57
  79.6 0.0 copy-done.1
  79.6 0.7 broadcast_add_fusion.pos_ref
  80.4 30.8 %shard_map.104 = bf16[128,1920]{1,0:T(8,128)(2,1)} custom-call(bf16[640,384]{1,0:T(8,128)(2,1)} %bitcast.54, bf16[640,384]{1,0:T(8,128)(2,1)} %bitcast.55, bf16[640,384]{1,0:T(8,128)(2,1)} %bitcast.56, bf16[1024,384]{1,0:T(8,128)(2,1)} %bitcast.51, bf16[1024,384]{1,0:T(8,128)(2,1)} %bitcast.50, s32[640,1]{1,0:T(8,128)} %broadcast_add_fusion.pos_ref, ...), custom_call_target="tpu_custom_call" | custom-call | tf_op jit(solution)/shard_map/pallas_call | solution.py:113
  111.2 1.3 copy.62
  112.6 1.2 copy.63
  113.8 0.0 all-to-all-done.2
  113.8 9.3 %all-to-all-start.1 = ((bf16[128,15,128]{2,1,0:T(8,128)(2,1)}), bf16[128,15,128]{2,1,0:T(8,128)(2,1)S(1)}, u32[]{:S(2)}, u32[]{:S(2)}) async-start(bf16[128,15,128]{2,1,0:T(8,128)(2,1)} %copy.63), calls=%async_computation.1 | async-start | bytes 1048576 | tf_op jit(solution)/shard_map/all_to_all | solution.py:204
  123.1 4.3 %copy.65 = bf16[4,384,768]{2,1,0:T(8,128)(2,1)} copy(bf16[4,384,768]{1,2,0:T(8,128)(2,1)} %bitcast.19) | data formatting | bytes 4718592 | tf_op jit(solution)/shard_map/all_to_all | solution.py:158
  127.4 13.6 %all-to-all-done.1 = bf16[128,15,128]{2,1,0:T(8,128)(2,1)S(1)} async-done(((bf16[128,15,128]{2,1,0:T(8,128)(2,1)}), bf16[128,15,128]{2,1,0:T(8,128)(2,1)S(1)}, u32[]{:S(2)}, u32[]{:S(2)}) %all-to-all-start.1) | async-done | bytes 491552 | tf_op jit(solution)/shard_map/all_to_all | solution.py:204
  141.0 0.3 reshape.354
  141.3 0.0 copy-start.3
  141.4 1.2 gather_fusion.2
  142.5 15.6 %all-gather = bf16[256,1536]{1,0:T(8,128)(2,1)S(1)} all-gather(bf16[256,384]{1,0:T(8,128)(2,1)S(1)} %gather_fusion.2), channel_id=2, replica_groups=mesh['req'=128,'tp'=4] {'tp'}, dimensions={1}, use_global_device_ids=true | all-gather | bytes 983040 | tf_op jit(solution)/shard_map/all_gather | solution.py:213
  158.1 2.5 %multiply_reduce_fusion = (f32[256]{0:T(256)S(1)}, f32[256,768]{1,0:T(8,128)S(1)}) fusion(bf16[256,1536]{1,0:T(8,128)(2,1)S(1)} %all-gather, bf16[1536,768]{1,0:T(8,128)(2,1)} %bitcast.53, bf16[256,768]{1,0:T(8,128)(2,1)S(1)} %copy-done.3), kind=kOutput, calls=%fused_computation.8 | convolution fusion | flops 604765952 | bytes 4326400 | tf_op jit(solution)/shard_map/dot_general | solution.py:214
  160.6 10.0 %psum.7 = f32[256]{0:T(256)S(1)} all-reduce(f32[256]{0:T(256)S(1)} %get-tuple-element.11), channel_id=1, replica_groups=mesh['req'=128,'tp'=4] {'tp'}, use_global_device_ids=true, to_apply=%region_4.5 | all-reduce | flops 256 | bytes 2048 | tf_op jit(solution)/shard_map/psum | solution.py:216
  170.7 1.0 multiply_convert_fusion
  (22 shorter events, 0.1 us)
Async XLA Ops:
  0.6 30.3 %copy-start = (bf16[8,2,128,384]{3,2,1,0:T(8,128)(2,1)S(1)}, bf16[8,2,128,384]{3,2,1,0:T(8,128)(2,1)}, u32[]{:S(2)}) copy-start(bf16[8,2,128,384]{3,2,1,0:T(8,128)(2,1)} %param.14) | copy-start | bytes 4718596
  8.0 57.0 %all-to-all-start = ((bf16[128,16,384]{2,1,0:T(8,128)(2,1)}), bf16[128,16,384]{2,1,0:T(8,128)(2,1)S(1)}, u32[]{:S(2)}, u32[]{:S(2)}) async-start(bf16[128,16,384]{2,1,0:T(8,128)(2,1)} %copy.54), calls=%async_computation | async-start | bytes 3145728 | tf_op jit(solution)/shard_map/all_to_all | solution.py:176
  26.6 4.3 %copy-start.4 = (s32[1,8]{1,0:T(1,128)S(1)}, s32[1,8]{1,0:T(1,128)}, u32[]{:S(2)}) copy-start(s32[1,8]{1,0:T(1,128)} %param.13) | copy-start | bytes 100
  65.0 48.8 %all-to-all-start.2 = ((bf16[384,4,768]{0,2,1:T(8,128)(2,1)}), bf16[384,4,768]{0,2,1:T(8,128)(2,1)}, u32[]{:S(2)}, u32[]{:S(2)}) async-start(bf16[384,4,768]{0,2,1:T(8,128)(2,1)} %bitcast.48), calls=%async_computation.2 | async-start | bytes 4718592 | tf_op jit(solution)/shard_map/all_to_all | solution.py:158
  76.6 3.0 %copy-start.1 = (s32[1,640]{0,1:T(8,128)}, s32[1,640]{0,1:T(8,128)S(1)}, u32[]{:S(2)}) copy-start(s32[1,640]{0,1:T(8,128)S(1)} %copy.68) | copy-start | bytes 7684
  111.2 11.8 %copy-start.2 = (bf16[768]{0:T(1024)(128)(2,1)S(1)}, bf16[768]{0:T(1024)(128)(2,1)}, u32[]{:S(2)}) copy-start(bf16[768]{0:T(1024)(128)(2,1)} %param.17) | copy-start | bytes 4612
  113.8 27.3 %all-to-all-start.1 = ((bf16[128,15,128]{2,1,0:T(8,128)(2,1)}), bf16[128,15,128]{2,1,0:T(8,128)(2,1)S(1)}, u32[]{:S(2)}, u32[]{:S(2)}) async-start(bf16[128,15,128]{2,1,0:T(8,128)(2,1)} %copy.63), calls=%async_computation.1 | async-start | bytes 1048576 | tf_op jit(solution)/shard_map/all_to_all | solution.py:204
  141.3 16.8 %copy-start.3 = (bf16[256,768]{1,0:T(8,128)(2,1)S(1)}, bf16[256,768]{1,0:T(8,128)(2,1)}, u32[]{:S(2)}) copy-start(bf16[256,768]{1,0:T(8,128)(2,1)} %param.15) | copy-start | bytes 1179652

commit v10 on v6

--- a/solution.py
+++ b/solution.py
@@ -54,34 +54,50 @@
     return (field.astype(jnp.float32) * cos_rows + turned * sin_rows).astype(jnp.bfloat16)
 
 
+def head_select(cols, lanes):
+    heads = cols // HEAD_SIZE
+    head = jnp.arange(heads, dtype=jnp.int32)[:, None, None]
+    col = jnp.arange(cols, dtype=jnp.int32)[None, :, None]
+    lane = jnp.arange(lanes, dtype=jnp.int32)[None, None, :]
+    return ((col == head * HEAD_SIZE + lane) & (lane < HEAD_SIZE)).astype(jnp.bfloat16)
+
+
 def attend_kernel(
-    q_ref, kn_ref, vn_ref, kc_ref, vc_ref, cos_ref, sin_ref, turn_ref, qrank_ref, cache_ok_ref,
-    krank_ref, o_ref, keys_ref,
+    q_ref, kn_ref, vn_ref, kc_ref, vc_ref, cos_ref, sin_ref, turn_ref, sel_ref, selt_ref,
+    qrank_ref, cache_ok_ref, krank_ref, o_ref, keys_ref, values_ref,
 ):
     step = pl.program_id(0)
     block = q_ref.shape[0]
+    heads = sel_ref.shape[0]
 
     @pl.when(step == 0)
     def _():
-        keys_ref[...] = turn_rows(kn_ref[...], cos_ref[...], sin_ref[...], turn_ref[...])
+        rotated = turn_rows(kn_ref[...], cos_ref[...], sin_ref[...], turn_ref[...])
+        fresh = vn_ref[...]
+        for head in range(heads):
+            keys_ref[head] = jnp.dot(
+                rotated, sel_ref[head], preferred_element_type=jnp.float32
+            ).astype(jnp.bfloat16)
+            values_ref[head] = jnp.dot(
+                fresh, sel_ref[head], preferred_element_type=jnp.float32
+            ).astype(jnp.bfloat16)
 
     here = pl.ds(pl.multiple_of(step * block, block), block)
     query = turn_rows(q_ref[...], cos_ref[here, :], sin_ref[here, :], turn_ref[...])
     score_scale = 1.0 / math.sqrt(HEAD_SIZE)
-    cols = query.shape[1]
-    col_head = lax.broadcasted_iota(jnp.int32, (1, cols), 1) // HEAD_SIZE
     cache_ok = cache_ok_ref[...] > 0
     new_ok = krank_ref[...] <= qrank_ref[...]
     contract = (((1,), (1,)), ((), ()))
     total = jnp.zeros(o_ref.shape, jnp.float32)
-    for head in range(cols // HEAD_SIZE):
-        chosen = col_head == head
-        head_query = jnp.where(chosen, query, jnp.zeros_like(query))
+    for head in range(heads):
+        head_query = jnp.dot(query, sel_ref[head], preferred_element_type=jnp.float32).astype(
+            jnp.bfloat16
+        )
         score_c = lax.dot_general(
-            head_query, kc_ref[...], contract, preferred_element_type=jnp.float32
+            head_query, kc_ref[head], contract, preferred_element_type=jnp.float32
         ) * score_scale
         score_n = lax.dot_general(
-            head_query, keys_ref[...], contract, preferred_element_type=jnp.float32
+            head_query, keys_ref[head], contract, preferred_element_type=jnp.float32
         ) * score_scale
         score_c = jnp.where(cache_ok, score_c, -1e30)
         score_n = jnp.where(new_ok, score_n, -1e30)
@@ -93,11 +109,12 @@
         whole = jnp.sum(weight_c, axis=1, keepdims=True) + jnp.sum(weight_n, axis=1, keepdims=True)
         prob_c = (weight_c / whole).astype(jnp.bfloat16)
         prob_n = (weight_n / whole).astype(jnp.bfloat16)
-        head_out = jnp.dot(prob_c, vc_ref[...], preferred_element_type=jnp.float32) + jnp.dot(
-            prob_n, vn_ref[...], preferred_element_type=jnp.float32
-        )
-        head_out = head_out.astype(jnp.bfloat16).astype(jnp.float32)
-        total = total + jnp.where(chosen, head_out, 0.0)
+        head_out = jnp.dot(prob_c, vc_ref[head], preferred_element_type=jnp.float32) + jnp.dot(
+            prob_n, values_ref[head], preferred_element_type=jnp.float32
+        )
+        total = total + jnp.dot(
+            head_out.astype(jnp.bfloat16), selt_ref[head], preferred_element_type=jnp.float32
+        )
     o_ref[...] = total.astype(o_ref.dtype)
 
 
@@ -106,7 +123,15 @@
     rows, cols = query.shape
     block = rows // slot_cap
     span = cache_keys.shape[0]
+    heads = cols // HEAD_SIZE
+    lanes = 128
+    sel = head_select(cols, lanes)
+    sel_t = sel.transpose(0, 2, 1)
+    split = lambda x: jnp.pad(
+        x.reshape(x.shape[0], heads, HEAD_SIZE), ((0, 0), (0, 0), (0, lanes - HEAD_SIZE))
+    ).transpose(1, 0, 2)
     whole = lambda i: (0, 0)
+    whole3 = lambda i: (0, 0, 0)
     return pl.pallas_call(
         attend_kernel,
         out_shape=jax.ShapeDtypeStruct((block, slot_cap * cols), jnp.bfloat16),
@@ -115,20 +140,25 @@
             pl.BlockSpec((block, cols), lambda i: (i, 0)),
             pl.BlockSpec((rows, cols), whole),
             pl.BlockSpec((rows, cols), whole),
-            pl.BlockSpec((span, cols), whole),
-            pl.BlockSpec((span, cols), whole),
+            pl.BlockSpec((heads, span, lanes), whole3),
+            pl.BlockSpec((heads, span, lanes), whole3),
             pl.BlockSpec((rows, cols), whole),
             pl.BlockSpec((rows, cols), whole),
             pl.BlockSpec((cols, cols), whole),
+            pl.BlockSpec((heads, cols, lanes), whole3),
+            pl.BlockSpec((heads, lanes, cols), whole3),
             pl.BlockSpec((block, 1), lambda i: (i, 0)),
             pl.BlockSpec((1, span), whole),
             pl.BlockSpec((1, rows), whole),
         ],
         out_specs=pl.BlockSpec((block, cols), lambda i: (0, i)),
-        scratch_shapes=[pltpu.VMEM((rows, cols), jnp.bfloat16)],
+        scratch_shapes=[
+            pltpu.VMEM((heads, rows, lanes), jnp.bfloat16),
+            pltpu.VMEM((heads, rows, lanes), jnp.bfloat16),
+        ],
         compiler_params=pltpu.CompilerParams(dimension_semantics=("arbitrary",)),
-    )(query, fresh_keys, fresh_values, cache_keys, cache_values, cos_all, sin_all, turn, q_rank,
-      cache_ok, k_rank)
+    )(query, fresh_keys, fresh_values, split(cache_keys), split(cache_values), cos_all, sin_all,
+      turn, sel, sel_t, q_rank, cache_ok, k_rank)
 
 
 def on_device(

time: 171 us -> 169 us (0.988)
  waiting for transfers between devices: 44.7 us -> 26.5 us
  local copies, waits for them, and re-layouts: 28.8 us -> 43.4 us
  other arithmetic: 7.39 us -> 9.31 us
    all_to_all x1, waiting for transfers between devices: 31.1 us -> 12.8 us  [on_device(): lax.all_to_all(outgoing, 'req', split_axis=0, concat_axis=0, tiled=True)]
    another operation x0 -> x4, local copies, waits for them, and re-layouts: none -> 11.2 us  [attend_slots(): x.reshape(x.shape[0], heads, HEAD_SIZE)]
    transpose x0 -> x1, local copies, waits for them, and re-layouts: none -> 3.33 us  [attend_slots(): split = lambda x: jnp.pad(x.reshape(x.shape[0], heads, HEAD_SIZE), ((0, 0...]
    convert_element_type x0 -> x2, other arithmetic: none -> 1.82 us  [head_select(): ((col == head * HEAD_SIZE + lane) & (lane < HEAD_SIZE)).astype(jnp.bfloat16)]
  transfers between devices with their start and end apart: 3 -> 3, of which waited for: 2 -> 2; matrix products, arithmetic and copies ran while one was open for 17% -> 27% of each run, Pallas kernels for 15% -> 15%
where the time goes in v10:
time: 169 us; the launch traced here: 166 us
  local copies, waits for them, and re-layouts  43.4 us (26%)
  starting transfers between devices  31.2 us (18%)
  waiting for transfers between devices  26.5 us (16%)
  blocking collectives  25.6 us (15%)
  Pallas kernels  24.6 us (15%)
  other arithmetic  9.31 us (6%)
  matrix products  4.19 us (2%)
    pallas_call x1, Pallas kernels, attend_slots(): pl.pallas_call(attend_kernel, out_shape=jax.ShapeDtypeStruct((block, slot...  24.6 us
    all_to_all x1, starting transfers between devices, on_device(): lax.all_to_all(outgoing, 'req', split_axis=0, concat_axis=0, tiled=True)  17.5 us
    all_gather x1, blocking collectives, on_device(): attn_all = lax.all_gather(attn_rows, 'tp', axis=1, tiled=True)  15.6 us
    all_to_all x1, waiting for transfers between devices, on_device(): lax.all_to_all(result.reshape(devices, slot_cap * parts, head_cols // par...  13.7 us
    all_to_all x1, waiting for transfers between devices, on_device(): lax.all_to_all(outgoing, 'req', split_axis=0, concat_axis=0, tiled=True)  12.8 us
    another operation x4, local copies, waits for them, and re-layouts, attend_slots(): x.reshape(x.shape[0], heads, HEAD_SIZE)  11.2 us
    psum x1, blocking collectives, on_device(): square_sum = lax.psum(jnp.sum(hidden * hidden, axis=1), 'tp')  10 us
    all_to_all x1, starting transfers between devices, on_device(): lax.all_to_all(result.reshape(devices, slot_cap * parts, head_cols // par...  9.05 us
  transfers between devices with their start and end apart: 3, of which 2 were waited for; matrix products, arithmetic and copies ran while one was open for 27% of the time, Pallas kernels for 15%

profile of v10, /device:TPU:56, one launch (start us, length us, event | category | flops | bytes accessed | tf_op | source)
XLA Modules:
  0.0 166.2 jit_solution(15684461666224842662)
XLA Ops:
  0.6 0.8 compare_select_fusion.1
  1.5 1.9 %gather_fusion = s32[256]{0:T(256)S(1)} fusion(s32[128]{0:T(128)} %param.11, s32[1024]{0:T(1024)S(1)} %pad_clamp_fusion.2), kind=kCustom, calls=%fused_computation | custom fusion | bytes 3072 | tf_op jit(solution)/shard_map/gather | solution.py:186
  3.3 0.1 convert_reduce_fusion.1
  3.5 0.2 convert_reduce_fusion
  3.7 1.7 %fusion = bf16[128,3,5,384]{3,0,1,2:T(8,128)(2,1)S(1)} fusion(bf16[256,3,384]{2,0,1:T(8,128)(2,1)} %param.9, pred[5,256]{1,0:T(8,128)(4,1)S(1)} %iota_compare_fusion.4, pred[256,128]{0,1:T(8,128)(4,1)S(1)} %iota_compare_fusion.3), kind=kOutput, calls=%fused_computation.5 | convolution fusion | flops 378388480 | bytes 2098432 | tf_op jit(solution)/shard_map/jid,ipc->dpjc/dot_general | solution.py:196
  5.4 0.2 copy.56
  5.7 0.2 pad_maximum_fusion
  5.9 2.1 %copy.57 = bf16[128,16,384]{2,1,0:T(8,128)(2,1)} copy(bf16[128,16,384]{2,0,1:T(8,128)(2,1)S(1)} %pad_maximum_fusion) | data formatting | bytes 3145728 | tf_op jit(solution)/shard_map/concatenate | solution.py:200
  7.9 17.5 %all-to-all-start = ((bf16[128,16,384]{2,1,0:T(8,128)(2,1)}), bf16[128,16,384]{2,1,0:T(8,128)(2,1)S(1)}, u32[]{:S(2)}, u32[]{:S(2)}) async-start(bf16[128,16,384]{2,1,0:T(8,128)(2,1)} %copy.57), calls=%async_computation | async-start | bytes 3145728 | tf_op jit(solution)/shard_map/all_to_all | solution.py:203
  25.5 1.9 %gather_fusion.1 = bf16[8,2,128,384]{3,2,1,0:T(8,128)(2,1)} fusion(bf16[8,2,128,384]{3,2,1,0:T(8,128)(2,1)S(1)} %copy-done, s32[1024]{0:T(1024)S(1)} %pad_clamp_fusion.1), kind=kCustom, calls=%fused_computation.1 | custom fusion | bytes 3145760 | tf_op jit(solution)/shard_map/gather | solution.py:208
  27.4 2.7 %fusion.23 = (bf16[8,1,128,384]{3,2,1,0:T(8,128)(2,1)}, bf16[8,1,128,384]{3,2,1,0:T(8,128)(2,1)}) fusion(bf16[8,2,128,384]{3,2,1,0:T(8,128)(2,1)} %gather_fusion.1), kind=kLoop, calls=%fused_computation.75 | loop fusion | bytes 3145728 | tf_op jit(solution)/shard_map/slice | solution.py:211
  30.1 3.2 %reshape.427 = bf16[1024,4,96]{2,1,0:T(4,128)(2,1)} reshape(bf16[8,1,128,384]{3,2,1,0:T(8,128)(2,1)} %get-tuple-element.2) | data formatting | bytes 1572864 | tf_op jit(solution)/shard_map/reshape;reshape;squeeze | solution.py:131
  33.4 2.3 %copy.64 = bf16[1024,4,96]{2,0,1:T(8,128)(2,1)} copy(bf16[1024,4,96]{2,1,0:T(4,128)(2,1)} %reshape.427) | data formatting | bytes 1572864 | tf_op jit(solution)/shard_map/reshape;reshape;squeeze | solution.py:131
  35.7 3.2 %reshape.426 = bf16[1024,4,96]{2,1,0:T(4,128)(2,1)} reshape(bf16[8,1,128,384]{3,2,1,0:T(8,128)(2,1)} %get-tuple-element.3) | data formatting | bytes 1572864 | tf_op jit(solution)/shard_map/reshape;reshape;squeeze | solution.py:131
  38.9 2.4 %copy.62 = bf16[1024,4,96]{2,0,1:T(8,128)(2,1)} copy(bf16[1024,4,96]{2,1,0:T(4,128)(2,1)} %reshape.426) | data formatting | bytes 1572864 | tf_op jit(solution)/shard_map/reshape;reshape;squeeze | solution.py:131
  42.0 4.3 %copy.71 = bf16[384,3072]{0,1:T(8,128)(2,1)} copy(bf16[384,3072]{1,0:T(8,128)(2,1)} %param.16) | data formatting | bytes 4718592 | tf_op args[7]
  46.4 0.6 compare_convert_fusion.cache_ok_ref
  47.0 3.3 %pad_bitcast_fusion = (bf16[4,1024,128]{2,1,0:T(8,128)(2,1)}, bf16[4,1024,128]{2,1,0:T(8,128)(2,1)}) fusion(bf16[1024,4,96]{2,0,1:T(8,128)(2,1)} %copy.64, bf16[1024,4,96]{2,0,1:T(8,128)(2,1)} %copy.62), kind=kLoop, calls=%fused_computation.7 | loop fusion | bytes 3670016 | tf_op jit(solution)/shard_map/transpose | solution.py:132
  50.4 1.1 select_convert_fusion.turn_ref
  51.4 0.9 fusion.2.sel_ref
  52.3 12.8 %all-to-all-done = bf16[128,16,384]{2,1,0:T(8,128)(2,1)S(1)} async-done(((bf16[128,16,384]{2,1,0:T(8,128)(2,1)}), bf16[128,16,384]{2,1,0:T(8,128)(2,1)S(1)}, u32[]{:S(2)}, u32[]{:S(2)}) %all-to-all-start) | async-done | bytes 1572896 | tf_op jit(solution)/shard_map/all_to_all | solution.py:203
  65.1 4.7 %all-to-all-start.2 = ((bf16[384,4,768]{0,2,1:T(8,128)(2,1)}), bf16[384,4,768]{0,2,1:T(8,128)(2,1)}, u32[]{:S(2)}, u32[]{:S(2)}) async-start(bf16[384,4,768]{0,2,1:T(8,128)(2,1)} %bitcast.57), calls=%async_computation.2 | async-start | bytes 4718592 | tf_op jit(solution)/shard_map/all_to_all | solution.py:185
  69.8 0.9 fusion.4.selt_ref
  70.7 0.4 fusion.24
  71.2 0.9 copy.58
  72.1 0.9 copy.59
  72.9 0.9 copy.60
  73.8 0.1 slice_convert_fusion
  73.9 0.2 reduce-window.8
  74.1 0.1 reduce
  74.2 2.4 %fusion.22 = s32[128]{0:T(128)S(1)} fusion(bf16[16,128,384]{2,0,1:T(8,128)(2,1)S(1)} %bitcast.56), kind=kLoop, calls=%fused_computation.74 | loop fusion | flops 128 | bytes 768 | tf_op jit(solution)/shard_map/convert_element_type | solution.py:205
  76.6 0.5 multiply_sine_fusion
  77.2 1.3 copy.66.cos_ref
  78.6 1.4 copy.67.sin_ref
  79.9 0.6 copy_bitcast_fusion
  80.5 0.9 copy.79
  81.4 24.6 %shard_map.104 = bf16[128,1920]{1,0:T(8,128)(2,1)} custom-call(bf16[640,384]{1,0:T(8,128)(2,1)} %bitcast.62, bf16[640,384]{1,0:T(8,128)(2,1)} %bitcast.63, bf16[640,384]{1,0:T(8,128)(2,1)} %bitcast.64, bf16[4,1024,128]{2,1,0:T(8,128)(2,1)} %get-tuple-element.27.kc_ref, bf16[4,1024,128]{2,1,0:T(8,128)(2,1)} %get-tuple-element.26.vc_ref, ...), custom_call_target="tpu_custom_call" | custom-call | tf_op jit(solution)/shard_map/pallas_call | solution.py:135
  106.0 1.3 copy.69
  107.3 1.2 copy.70
  108.6 9.0 %all-to-all-start.1 = ((bf16[128,15,128]{2,1,0:T(8,128)(2,1)}), bf16[128,15,128]{2,1,0:T(8,128)(2,1)S(1)}, u32[]{:S(2)}, u32[]{:S(2)}) async-start(bf16[128,15,128]{2,1,0:T(8,128)(2,1)} %copy.70), calls=%async_computation.1 | async-start | bytes 1048576 | tf_op jit(solution)/shard_map/all_to_all | solution.py:230
  117.7 4.3 %copy.72 = bf16[4,384,768]{2,1,0:T(8,128)(2,1)} copy(bf16[4,384,768]{1,2,0:T(8,128)(2,1)} %bitcast.22) | data formatting | bytes 4718592 | tf_op jit(solution)/shard_map/all_to_all | solution.py:185
  121.9 13.7 %all-to-all-done.1 = bf16[128,15,128]{2,1,0:T(8,128)(2,1)S(1)} async-done(((bf16[128,15,128]{2,1,0:T(8,128)(2,1)}), bf16[128,15,128]{2,1,0:T(8,128)(2,1)S(1)}, u32[]{:S(2)}, u32[]{:S(2)}) %all-to-all-start.1) | async-done | bytes 491552 | tf_op jit(solution)/shard_map/all_to_all | solution.py:230
  135.6 0.3 reshape.395
  135.9 1.2 gather_fusion.2
  137.1 15.6 %all-gather = bf16[256,1536]{1,0:T(8,128)(2,1)S(1)} all-gather(bf16[256,384]{1,0:T(8,128)(2,1)S(1)} %gather_fusion.2), channel_id=2, replica_groups=mesh['req'=128,'tp'=4] {'tp'}, dimensions={1}, use_global_device_ids=true | all-gather | bytes 983040 | tf_op jit(solution)/shard_map/all_gather | solution.py:239
  152.7 2.5 %multiply_reduce_fusion = (f32[256]{0:T(256)S(1)}, f32[256,768]{1,0:T(8,128)S(1)}) fusion(bf16[256,1536]{1,0:T(8,128)(2,1)S(1)} %all-gather, bf16[1536,768]{1,0:T(8,128)(2,1)} %bitcast.61, bf16[256,768]{1,0:T(8,128)(2,1)S(1)} %copy-done.2), kind=kOutput, calls=%fused_computation.10 | convolution fusion | flops 604765952 | bytes 4326400 | tf_op jit(solution)/shard_map/dot_general | solution.py:240
  155.2 10.0 %psum.7 = f32[256]{0:T(256)S(1)} all-reduce(f32[256]{0:T(256)S(1)} %get-tuple-element.14), channel_id=1, replica_groups=mesh['req'=128,'tp'=4] {'tp'}, use_global_device_ids=true, to_apply=%region_4.5 | all-reduce | flops 256 | bytes 2048 | tf_op jit(solution)/shard_map/psum | solution.py:242
  165.2 1.0 multiply_convert_fusion
  (33 shorter events, 0.5 us)
Async XLA Ops:
  0.6 24.8 %copy-start = (bf16[8,2,128,384]{3,2,1,0:T(8,128)(2,1)S(1)}, bf16[8,2,128,384]{3,2,1,0:T(8,128)(2,1)}, u32[]{:S(2)}) copy-start(bf16[8,2,128,384]{3,2,1,0:T(8,128)(2,1)} %param.14) | copy-start | bytes 4718596
  7.9 17.5 %copy-start.3 = (s32[1,8]{1,0:T(1,128)S(1)}, s32[1,8]{1,0:T(1,128)}, u32[]{:S(2)}) copy-start(s32[1,8]{1,0:T(1,128)} %param.13) | copy-start | bytes 100
  7.9 57.2 %all-to-all-start = ((bf16[128,16,384]{2,1,0:T(8,128)(2,1)}), bf16[128,16,384]{2,1,0:T(8,128)(2,1)S(1)}, u32[]{:S(2)}, u32[]{:S(2)}) async-start(bf16[128,16,384]{2,1,0:T(8,128)(2,1)} %copy.57), calls=%async_computation | async-start | bytes 3145728 | tf_op jit(solution)/shard_map/all_to_all | solution.py:203
  65.1 43.5 %all-to-all-start.2 = ((bf16[384,4,768]{0,2,1:T(8,128)(2,1)}), bf16[384,4,768]{0,2,1:T(8,128)(2,1)}, u32[]{:S(2)}, u32[]{:S(2)}) async-start(bf16[384,4,768]{0,2,1:T(8,128)(2,1)} %bitcast.57), calls=%async_computation.2 | async-start | bytes 4718592 | tf_op jit(solution)/shard_map/all_to_all | solution.py:185
  106.0 11.6 %copy-start.1 = (bf16[768]{0:T(1024)(128)(2,1)S(1)}, bf16[768]{0:T(1024)(128)(2,1)}, u32[]{:S(2)}) copy-start(bf16[768]{0:T(1024)(128)(2,1)} %param.17) | copy-start | bytes 4612
  108.6 27.0 %all-to-all-start.1 = ((bf16[128,15,128]{2,1,0:T(8,128)(2,1)}), bf16[128,15,128]{2,1,0:T(8,128)(2,1)S(1)}, u32[]{:S(2)}, u32[]{:S(2)}) async-start(bf16[128,15,128]{2,1,0:T(8,128)(2,1)} %copy.70), calls=%async_computation.1 | async-start | bytes 1048576 | tf_op jit(solution)/shard_map/all_to_all | solution.py:230
  135.9 16.8 %copy-start.2 = (bf16[256,768]{1,0:T(8,128)(2,1)S(1)}, bf16[256,768]{1,0:T(8,128)(2,1)}, u32[]{:S(2)}) copy-start(bf16[256,768]{1,0:T(8,128)(2,1)} %param.15) | copy-start | bytes 1179652

commit v11 on v10

--- a/solution.py
+++ b/solution.py
@@ -239,7 +239,14 @@
     attn_all = lax.all_gather(attn_rows, "tp", axis=1, tiled=True)
     mixed_cols = jnp.dot(attn_all, weight_cols, preferred_element_type=jnp.float32)
     hidden = residual.astype(jnp.float32) + mixed_cols
-    square_sum = lax.psum(jnp.sum(hidden * hidden, axis=1), "tp")
+    square_part = jnp.sum(hidden * hidden, axis=1)
+    tp_size = lax.axis_size("tp")
+    square_sum = jnp.sum(
+        lax.all_to_all(
+            jnp.broadcast_to(square_part[None], (tp_size,) + square_part.shape), "tp", 0, 0, tiled=True
+        ),
+        axis=0,
+    )
     inv_rms = lax.rsqrt(square_sum / D + EPS)
     normed = hidden * inv_rms[:, None] * norm_gain.astype(jnp.float32)[None, :]
     return (hidden.astype(jnp.bfloat16), normed.astype(jnp.bfloat16))

time: 169 us -> 168 us (level)
  blocking collectives: 25.6 us -> 15.6 us
  waiting for transfers between devices: 26.5 us -> 31.7 us
  starting transfers between devices: 31.2 us -> 34.7 us
    psum x1 -> x0, blocking collectives: 10 us -> none  [on_device(): square_sum = lax.psum(jnp.sum(hidden * hidden, axis=1), 'tp')]
    all_to_all x0 -> x1, waiting for transfers between devices: none -> 5.29 us  [on_device(): lax.all_to_all(jnp.broadcast_to(square_part[None], (tp_size,) + square_pa...]
    all_to_all x0 -> x1, starting transfers between devices: none -> 3.57 us  [on_device(): lax.all_to_all(jnp.broadcast_to(square_part[None], (tp_size,) + square_pa...]
  transfers between devices with their start and end apart: 3 -> 4, of which waited for: 2 -> 3; matrix products, arithmetic and copies ran while one was open for 27% -> 27% of each run, Pallas kernels for 15% -> 15%
where the time goes in v11:
time: 168 us; the launch traced here: 166 us
  local copies, waits for them, and re-layouts  44 us (26%)
  starting transfers between devices  34.7 us (21%)
  waiting for transfers between devices  31.7 us (19%)
  Pallas kernels  24.6 us (15%)
  blocking collectives  15.6 us (9%)
  other arithmetic  9.34 us (6%)
  matrix products  4.2 us (2%)
    pallas_call x1, Pallas kernels, attend_slots(): pl.pallas_call(attend_kernel, out_shape=jax.ShapeDtypeStruct((block, slot...  24.6 us
    all_to_all x1, starting transfers between devices, on_device(): lax.all_to_all(outgoing, 'req', split_axis=0, concat_axis=0, tiled=True)  17.5 us
    all_gather x1, blocking collectives, on_device(): attn_all = lax.all_gather(attn_rows, 'tp', axis=1, tiled=True)  15.6 us
    all_to_all x1, waiting for transfers between devices, on_device(): lax.all_to_all(result.reshape(devices, slot_cap * parts, head_cols // par...  13.7 us
    all_to_all x1, waiting for transfers between devices, on_device(): lax.all_to_all(outgoing, 'req', split_axis=0, concat_axis=0, tiled=True)  12.8 us
    another operation x4, local copies, waits for them, and re-layouts, attend_slots(): x.reshape(x.shape[0], heads, HEAD_SIZE)  11.2 us
    all_to_all x1, starting transfers between devices, on_device(): lax.all_to_all(result.reshape(devices, slot_cap * parts, head_cols // par...  9.05 us
    all_to_all x1, waiting for transfers between devices, on_device(): lax.all_to_all(jnp.broadcast_to(square_part[None], (tp_size,) + square_pa...  5.29 us
  transfers between devices with their start and end apart: 4, of which 3 were waited for; matrix products, arithmetic and copies ran while one was open for 27% of the time, Pallas kernels for 15%

profile of v11, /device:TPU:56, one launch (start us, length us, event | category | flops | bytes accessed | tf_op | source)
XLA Modules:
  0.0 165.7 jit_solution(2678834156761690936)
XLA Ops:
  0.6 0.8 compare_select_fusion.1
  1.5 1.9 %gather_fusion = s32[256]{0:T(256)S(1)} fusion(s32[128]{0:T(128)} %param.11, s32[1024]{0:T(1024)S(1)} %pad_clamp_fusion.2), kind=kCustom, calls=%fused_computation | custom fusion | bytes 3072 | tf_op jit(solution)/shard_map/gather | solution.py:186
  3.3 0.1 convert_reduce_fusion.1
  3.5 0.2 convert_reduce_fusion
  3.7 1.7 %fusion = bf16[128,3,5,384]{3,0,1,2:T(8,128)(2,1)S(1)} fusion(bf16[256,3,384]{2,0,1:T(8,128)(2,1)} %param.9, pred[5,256]{1,0:T(8,128)(4,1)S(1)} %iota_compare_fusion.4, pred[256,128]{0,1:T(8,128)(4,1)S(1)} %iota_compare_fusion.3), kind=kOutput, calls=%fused_computation.5 | convolution fusion | flops 378388480 | bytes 2098432 | tf_op jit(solution)/shard_map/jid,ipc->dpjc/dot_general | solution.py:196
  5.4 0.2 copy.73
  5.6 0.2 pad_maximum_fusion
  5.8 2.1 %copy.74 = bf16[128,16,384]{2,1,0:T(8,128)(2,1)} copy(bf16[128,16,384]{2,0,1:T(8,128)(2,1)S(1)} %pad_maximum_fusion) | data formatting | bytes 3145728 | tf_op jit(solution)/shard_map/concatenate | solution.py:200
  7.9 17.5 %all-to-all-start = ((bf16[128,16,384]{2,1,0:T(8,128)(2,1)}), bf16[128,16,384]{2,1,0:T(8,128)(2,1)S(1)}, u32[]{:S(2)}, u32[]{:S(2)}) async-start(bf16[128,16,384]{2,1,0:T(8,128)(2,1)} %copy.74), calls=%async_computation | async-start | bytes 3145728 | tf_op jit(solution)/shard_map/all_to_all | solution.py:203
  25.4 1.9 %gather_fusion.1 = bf16[8,2,128,384]{3,2,1,0:T(8,128)(2,1)} fusion(bf16[8,2,128,384]{3,2,1,0:T(8,128)(2,1)S(1)} %copy-done, s32[1024]{0:T(1024)S(1)} %pad_clamp_fusion.1), kind=kCustom, calls=%fused_computation.1 | custom fusion | bytes 3145760 | tf_op jit(solution)/shard_map/gather | solution.py:208
  27.3 2.8 %fusion.23 = (bf16[8,1,128,384]{3,2,1,0:T(8,128)(2,1)}, bf16[8,1,128,384]{3,2,1,0:T(8,128)(2,1)}) fusion(bf16[8,2,128,384]{3,2,1,0:T(8,128)(2,1)} %gather_fusion.1), kind=kLoop, calls=%fused_computation.75 | loop fusion | bytes 3145728 | tf_op jit(solution)/shard_map/slice | solution.py:211
  30.1 3.2 %reshape.437 = bf16[1024,4,96]{2,1,0:T(4,128)(2,1)} reshape(bf16[8,1,128,384]{3,2,1,0:T(8,128)(2,1)} %get-tuple-element.2) | data formatting | bytes 1572864 | tf_op jit(solution)/shard_map/reshape;reshape;squeeze | solution.py:131
  33.3 2.3 %copy.81 = bf16[1024,4,96]{2,0,1:T(8,128)(2,1)} copy(bf16[1024,4,96]{2,1,0:T(4,128)(2,1)} %reshape.437) | data formatting | bytes 1572864 | tf_op jit(solution)/shard_map/reshape;reshape;squeeze | solution.py:131
  35.7 3.2 %reshape.436 = bf16[1024,4,96]{2,1,0:T(4,128)(2,1)} reshape(bf16[8,1,128,384]{3,2,1,0:T(8,128)(2,1)} %get-tuple-element.3) | data formatting | bytes 1572864 | tf_op jit(solution)/shard_map/reshape;reshape;squeeze | solution.py:131
  38.9 2.4 %copy.79 = bf16[1024,4,96]{2,0,1:T(8,128)(2,1)} copy(bf16[1024,4,96]{2,1,0:T(4,128)(2,1)} %reshape.436) | data formatting | bytes 1572864 | tf_op jit(solution)/shard_map/reshape;reshape;squeeze | solution.py:131
  42.0 4.3 %copy.88 = bf16[384,3072]{0,1:T(8,128)(2,1)} copy(bf16[384,3072]{1,0:T(8,128)(2,1)} %param.16) | data formatting | bytes 4718592 | tf_op args[7]
  46.3 0.6 compare_convert_fusion.cache_ok_ref
  46.9 3.3 %pad_bitcast_fusion = (bf16[4,1024,128]{2,1,0:T(8,128)(2,1)}, bf16[4,1024,128]{2,1,0:T(8,128)(2,1)}) fusion(bf16[1024,4,96]{2,0,1:T(8,128)(2,1)} %copy.81, bf16[1024,4,96]{2,0,1:T(8,128)(2,1)} %copy.79), kind=kLoop, calls=%fused_computation.7 | loop fusion | bytes 3670016 | tf_op jit(solution)/shard_map/transpose | solution.py:132
  50.3 1.1 select_convert_fusion.turn_ref
  51.4 0.9 fusion.2.sel_ref
  52.3 12.8 %all-to-all-done = bf16[128,16,384]{2,1,0:T(8,128)(2,1)S(1)} async-done(((bf16[128,16,384]{2,1,0:T(8,128)(2,1)}), bf16[128,16,384]{2,1,0:T(8,128)(2,1)S(1)}, u32[]{:S(2)}, u32[]{:S(2)}) %all-to-all-start) | async-done | bytes 1572896 | tf_op jit(solution)/shard_map/all_to_all | solution.py:203
  65.0 4.7 %all-to-all-start.2 = ((bf16[384,4,768]{0,2,1:T(8,128)(2,1)}), bf16[384,4,768]{0,2,1:T(8,128)(2,1)}, u32[]{:S(2)}, u32[]{:S(2)}) async-start(bf16[384,4,768]{0,2,1:T(8,128)(2,1)} %bitcast.57), calls=%async_computation.2 | async-start | bytes 4718592 | tf_op jit(solution)/shard_map/all_to_all | solution.py:185
  69.7 0.9 fusion.4.selt_ref
  70.7 0.4 fusion.24
  71.1 0.9 copy.75
  72.0 0.8 copy.76
  72.9 0.8 copy.77
  73.8 0.2 reduce-window.8
  74.1 2.4 %fusion.22 = s32[128]{0:T(128)S(1)} fusion(bf16[16,128,384]{2,0,1:T(8,128)(2,1)S(1)} %bitcast.56), kind=kLoop, calls=%fused_computation.74 | loop fusion | flops 128 | bytes 768 | tf_op jit(solution)/shard_map/convert_element_type | solution.py:205
  76.5 0.5 multiply_sine_fusion
  77.1 1.3 copy.83.cos_ref
  78.5 1.4 copy.84.sin_ref
  79.9 0.6 copy_bitcast_fusion
  80.5 0.9 copy.98
  81.4 24.6 %shard_map.104 = bf16[128,1920]{1,0:T(8,128)(2,1)} custom-call(bf16[640,384]{1,0:T(8,128)(2,1)} %bitcast.62, bf16[640,384]{1,0:T(8,128)(2,1)} %bitcast.63, bf16[640,384]{1,0:T(8,128)(2,1)} %bitcast.64, bf16[4,1024,128]{2,1,0:T(8,128)(2,1)} %get-tuple-element.27.kc_ref, bf16[4,1024,128]{2,1,0:T(8,128)(2,1)} %get-tuple-element.26.vc_ref, ...), custom_call_target="tpu_custom_call" | custom-call | tf_op jit(solution)/shard_map/pallas_call | solution.py:135
  106.0 1.3 copy.86
  107.3 1.2 copy.87
  108.5 9.0 %all-to-all-start.1 = ((bf16[128,15,128]{2,1,0:T(8,128)(2,1)}), bf16[128,15,128]{2,1,0:T(8,128)(2,1)S(1)}, u32[]{:S(2)}, u32[]{:S(2)}) async-start(bf16[128,15,128]{2,1,0:T(8,128)(2,1)} %copy.87), calls=%async_computation.1 | async-start | bytes 1048576 | tf_op jit(solution)/shard_map/all_to_all | solution.py:230
  117.6 4.3 %copy.89 = bf16[4,384,768]{2,1,0:T(8,128)(2,1)} copy(bf16[4,384,768]{1,2,0:T(8,128)(2,1)} %bitcast.22) | data formatting | bytes 4718592 | tf_op jit(solution)/shard_map/all_to_all | solution.py:185
  121.9 13.7 %all-to-all-done.1 = bf16[128,15,128]{2,1,0:T(8,128)(2,1)S(1)} async-done(((bf16[128,15,128]{2,1,0:T(8,128)(2,1)}), bf16[128,15,128]{2,1,0:T(8,128)(2,1)S(1)}, u32[]{:S(2)}, u32[]{:S(2)}) %all-to-all-start.1) | async-done | bytes 491552 | tf_op jit(solution)/shard_map/all_to_all | solution.py:230
  135.5 0.3 reshape.405
  135.9 1.2 gather_fusion.2
  137.0 15.6 %all-gather = bf16[256,1536]{1,0:T(8,128)(2,1)S(1)} all-gather(bf16[256,384]{1,0:T(8,128)(2,1)S(1)} %gather_fusion.2), channel_id=2, replica_groups=mesh['req'=128,'tp'=4] {'tp'}, dimensions={1}, use_global_device_ids=true | all-gather | bytes 983040 | tf_op jit(solution)/shard_map/all_gather | solution.py:239
  152.6 2.5 %multiply_reduce_fusion = (f32[256]{0:T(256)S(1)}, f32[256,768]{1,0:T(8,128)S(1)}) fusion(bf16[256,1536]{1,0:T(8,128)(2,1)S(1)} %all-gather, bf16[1536,768]{1,0:T(8,128)(2,1)} %bitcast.61, bf16[256,768]{1,0:T(8,128)(2,1)S(1)} %copy-done.2), kind=kOutput, calls=%fused_computation.10 | convolution fusion | flops 604765952 | bytes 4326400 | tf_op jit(solution)/shard_map/dot_general | solution.py:240
  155.1 0.6 broadcast_in_dim.25
  155.8 3.6 %all-to-all-start.3 = ((f32[4,1,256]{2,1,0:T(1,128)}), f32[4,1,256]{2,1,0:T(1,128)S(1)}, u32[]{:S(2)}, u32[]{:S(2)}) async-start(f32[4,1,256]{2,1,0:T(1,128)} %broadcast_in_dim.25), calls=%async_computation.3 | async-start | bytes 8192 | tf_op jit(solution)/shard_map/all_to_all | solution.py:245
  159.3 5.3 %all-to-all-done.3 = f32[4,1,256]{2,1,0:T(1,128)S(1)} async-done(((f32[4,1,256]{2,1,0:T(1,128)}), f32[4,1,256]{2,1,0:T(1,128)S(1)}, u32[]{:S(2)}, u32[]{:S(2)}) %all-to-all-start.3) | async-done | bytes 4128 | tf_op jit(solution)/shard_map/all_to_all | solution.py:245
  164.6 1.0 multiply_convert_fusion
  (36 shorter events, 0.7 us)
Async XLA Ops:
  0.6 24.8 %copy-start = (bf16[8,2,128,384]{3,2,1,0:T(8,128)(2,1)S(1)}, bf16[8,2,128,384]{3,2,1,0:T(8,128)(2,1)}, u32[]{:S(2)}) copy-start(bf16[8,2,128,384]{3,2,1,0:T(8,128)(2,1)} %param.14) | copy-start | bytes 4718596
  7.9 17.5 %copy-start.3 = (s32[1,8]{1,0:T(1,128)S(1)}, s32[1,8]{1,0:T(1,128)}, u32[]{:S(2)}) copy-start(s32[1,8]{1,0:T(1,128)} %param.13) | copy-start | bytes 100
  7.9 57.2 %all-to-all-start = ((bf16[128,16,384]{2,1,0:T(8,128)(2,1)}), bf16[128,16,384]{2,1,0:T(8,128)(2,1)S(1)}, u32[]{:S(2)}, u32[]{:S(2)}) async-start(bf16[128,16,384]{2,1,0:T(8,128)(2,1)} %copy.74), calls=%async_computation | async-start | bytes 3145728 | tf_op jit(solution)/shard_map/all_to_all | solution.py:203
  65.0 43.4 %all-to-all-start.2 = ((bf16[384,4,768]{0,2,1:T(8,128)(2,1)}), bf16[384,4,768]{0,2,1:T(8,128)(2,1)}, u32[]{:S(2)}, u32[]{:S(2)}) async-start(bf16[384,4,768]{0,2,1:T(8,128)(2,1)} %bitcast.57), calls=%async_computation.2 | async-start | bytes 4718592 | tf_op jit(solution)/shard_map/all_to_all | solution.py:185
  108.5 27.1 %all-to-all-start.1 = ((bf16[128,15,128]{2,1,0:T(8,128)(2,1)}), bf16[128,15,128]{2,1,0:T(8,128)(2,1)S(1)}, u32[]{:S(2)}, u32[]{:S(2)}) async-start(bf16[128,15,128]{2,1,0:T(8,128)(2,1)} %copy.87), calls=%async_computation.1 | async-start | bytes 1048576 | tf_op jit(solution)/shard_map/all_to_all | solution.py:230
  135.8 16.8 %copy-start.2 = (bf16[256,768]{1,0:T(8,128)(2,1)S(1)}, bf16[256,768]{1,0:T(8,128)(2,1)}, u32[]{:S(2)}) copy-start(bf16[256,768]{1,0:T(8,128)(2,1)} %param.15) | copy-start | bytes 1179652
  152.6 6.7 %copy-start.1 = (bf16[768]{0:T(1024)(128)(2,1)S(1)}, bf16[768]{0:T(1024)(128)(2,1)}, u32[]{:S(2)}) copy-start(bf16[768]{0:T(1024)(128)(2,1)} %param.17) | copy-start | bytes 4612
  155.8 8.9 %all-to-all-start.3 = ((f32[4,1,256]{2,1,0:T(1,128)}), f32[4,1,256]{2,1,0:T(1,128)S(1)}, u32[]{:S(2)}, u32[]{:S(2)}) async-start(f32[4,1,256]{2,1,0:T(1,128)} %broadcast_in_dim.25), calls=%async_computation.3 | async-start | bytes 8192 | tf_op jit(solution)/shard_map/all_to_all | solution.py:245

commit v12 on v11

--- a/solution.py
+++ b/solution.py
@@ -213,9 +213,9 @@
     before = jnp.cumsum(arrived_counts) - arrived_counts
     live_slot = (slot_of < arrived_counts[None, :]).reshape(buffer_len)
     new_rank = (before[None, :] + slot_of).reshape(buffer_len)
-    cosine, sine_tab = rope_tables(length + new_rank)
-    cos_all = jnp.tile(cosine, (1, heads_here))
-    sin_all = jnp.tile(sine_tab, (1, heads_here))
+    cosine, sine_tab = rope_tables(length + jnp.arange(buffer_len, dtype=jnp.int32))
+    cos_all = jnp.take(jnp.tile(cosine, (1, heads_here)), new_rank, axis=0, mode="clip")
+    sin_all = jnp.take(jnp.tile(sine_tab, (1, heads_here)), new_rank, axis=0, mode="clip")
     cache_ok = (jnp.arange(cache_span, dtype=jnp.int32) < length).astype(jnp.int32)[None, :]
     k_rank = jnp.where(live_slot, new_rank, jnp.int32(2**30))[None, :]
     q_rank = new_rank[:, None]

time: 168 us -> 185 us (1.10)
  local copies, waits for them, and re-layouts: 44 us -> 55.7 us
  other arithmetic: 9.34 us -> 14.9 us
    gather x0 -> x2, local copies, waits for them, and re-layouts: none -> 5.94 us  [the longest x1 2.98 us: on_device(): jnp.take(jnp.tile(cosine, (1, heads_here)), new_rank, axis=0, mode='clip')]
    convert_element_type x2, other arithmetic: 2.48 us -> 5.01 us  [on_device(): arrived_counts = planes[slot_cap * parts, :, 0].astype(jnp.int32)]
    another operation x2, other arithmetic: 0.28 us -> 2.54 us
    another operation x4, local copies, waits for them, and re-layouts: 2.8 us -> 4.83 us  [the longest x2 3.49 us: on_device(): jnp.tile(sine_tab, (1, heads_here))]
    slice x4, local copies, waits for them, and re-layouts: 3.05 us -> 4.98 us  [on_device(): planes[p * slot_cap:(p + 1) * slot_cap].reshape(buffer_len, head_cols)]
    unnamed x10 -> x16, local copies, waits for them, and re-layouts: 5.24 us -> 7 us
  transfers between devices with their start and end apart: 4 -> 4, of which waited for: 3 -> 3; matrix products, arithmetic and copies ran while one was open for 27% -> 33% of each run, Pallas kernels for 15% -> 13%
where the time goes in v12:
time: 185 us; the launch traced here: 182 us
  local copies, waits for them, and re-layouts  55.7 us (30%)
  starting transfers between devices  34.8 us (19%)
  waiting for transfers between devices  31.3 us (17%)
  Pallas kernels  24.6 us (13%)
  blocking collectives  15.6 us (8%)
  other arithmetic  14.9 us (8%)
  matrix products  4.2 us (2%)
    pallas_call x1, Pallas kernels, attend_slots(): pl.pallas_call(attend_kernel, out_shape=jax.ShapeDtypeStruct((block, slot...  24.6 us
    all_to_all x1, starting transfers between devices, on_device(): lax.all_to_all(outgoing, 'req', split_axis=0, concat_axis=0, tiled=True)  17.5 us
    all_gather x1, blocking collectives, on_device(): attn_all = lax.all_gather(attn_rows, 'tp', axis=1, tiled=True)  15.6 us
    all_to_all x1, waiting for transfers between devices, on_device(): lax.all_to_all(result.reshape(devices, slot_cap * parts, head_cols // par...  13.6 us
    all_to_all x1, waiting for transfers between devices, on_device(): lax.all_to_all(outgoing, 'req', split_axis=0, concat_axis=0, tiled=True)  12.3 us
    another operation x4, local copies, waits for them, and re-layouts, attend_slots(): x.reshape(x.shape[0], heads, HEAD_SIZE)  11.3 us
    all_to_all x1, starting transfers between devices, on_device(): lax.all_to_all(result.reshape(devices, slot_cap * parts, head_cols // par...  9.05 us
    unnamed x16, local copies, waits for them, and re-layouts  7 us
  transfers between devices with their start and end apart: 4, of which 3 were waited for; matrix products, arithmetic and copies ran while one was open for 33% of the time, Pallas kernels for 13%

profile of v12, /device:TPU:56, one launch (start us, length us, event | category | flops | bytes accessed | tf_op | source)
XLA Modules:
  0.0 182.5 jit_solution(6697104187687719403)
XLA Ops:
  0.6 0.8 compare_select_fusion.1
  1.5 1.9 %gather_fusion = s32[256]{0:T(256)S(1)} fusion(s32[128]{0:T(128)} %param.11, s32[1024]{0:T(1024)S(1)} %pad_clamp_fusion.3), kind=kCustom, calls=%fused_computation | custom fusion | bytes 3072 | tf_op jit(solution)/shard_map/gather | solution.py:186
  4.3 1.7 fusion
  6.4 2.1 %copy.74 = bf16[128,16,384]{2,1,0:T(8,128)(2,1)} copy(bf16[128,16,384]{2,0,1:T(8,128)(2,1)S(1)} %pad_maximum_fusion) | data formatting | bytes 3145728 | tf_op jit(solution)/shard_map/concatenate | solution.py:200
  8.5 17.5 %all-to-all-start = ((bf16[128,16,384]{2,1,0:T(8,128)(2,1)}), bf16[128,16,384]{2,1,0:T(8,128)(2,1)S(1)}, u32[]{:S(2)}, u32[]{:S(2)}) async-start(bf16[128,16,384]{2,1,0:T(8,128)(2,1)} %copy.74), calls=%async_computation | async-start | bytes 3145728 | tf_op jit(solution)/shard_map/all_to_all | solution.py:203
  26.0 1.9 %gather_fusion.1 = bf16[8,2,128,384]{3,2,1,0:T(8,128)(2,1)} fusion(bf16[8,2,128,384]{3,2,1,0:T(8,128)(2,1)S(1)} %copy-done, s32[1024]{0:T(1024)S(1)} %pad_clamp_fusion.2), kind=kCustom, calls=%fused_computation.1 | custom fusion | bytes 3145760 | tf_op jit(solution)/shard_map/gather | solution.py:208
  27.9 2.7 %fusion.24 = (bf16[8,1,128,384]{3,2,1,0:T(8,128)(2,1)}, bf16[8,1,128,384]{3,2,1,0:T(8,128)(2,1)}) fusion(bf16[8,2,128,384]{3,2,1,0:T(8,128)(2,1)} %gather_fusion.1), kind=kLoop, calls=%fused_computation.79 | loop fusion | bytes 3145728 | tf_op jit(solution)/shard_map/slice | solution.py:211
  30.6 3.3 %reshape.455 = bf16[1024,4,96]{2,1,0:T(4,128)(2,1)} reshape(bf16[8,1,128,384]{3,2,1,0:T(8,128)(2,1)} %get-tuple-element.2) | data formatting | bytes 1572864 | tf_op jit(solution)/shard_map/reshape;reshape;squeeze | solution.py:131
  33.9 2.3 %copy.81 = bf16[1024,4,96]{2,0,1:T(8,128)(2,1)} copy(bf16[1024,4,96]{2,1,0:T(4,128)(2,1)} %reshape.455) | data formatting | bytes 1572864 | tf_op jit(solution)/shard_map/reshape;reshape;squeeze | solution.py:131
  36.2 3.2 %reshape.454 = bf16[1024,4,96]{2,1,0:T(4,128)(2,1)} reshape(bf16[8,1,128,384]{3,2,1,0:T(8,128)(2,1)} %get-tuple-element.3) | data formatting | bytes 1572864 | tf_op jit(solution)/shard_map/reshape;reshape;squeeze | solution.py:131
  39.5 2.4 %copy.79 = bf16[1024,4,96]{2,0,1:T(8,128)(2,1)} copy(bf16[1024,4,96]{2,1,0:T(4,128)(2,1)} %reshape.454) | data formatting | bytes 1572864 | tf_op jit(solution)/shard_map/reshape;reshape;squeeze | solution.py:131
  42.6 4.3 %copy.88 = bf16[384,3072]{0,1:T(8,128)(2,1)} copy(bf16[384,3072]{1,0:T(8,128)(2,1)} %param.16) | data formatting | bytes 4718592 | tf_op args[7]
  46.9 0.6 compare_convert_fusion.cache_ok_ref
  48.0 0.8 pad_maximum_fusion.1
  48.8 3.3 %pad_bitcast_fusion = (bf16[4,1024,128]{2,1,0:T(8,128)(2,1)}, bf16[4,1024,128]{2,1,0:T(8,128)(2,1)}) fusion(bf16[1024,4,96]{2,0,1:T(8,128)(2,1)} %copy.81, bf16[1024,4,96]{2,0,1:T(8,128)(2,1)} %copy.79), kind=kLoop, calls=%fused_computation.9 | loop fusion | bytes 3670016 | tf_op jit(solution)/shard_map/transpose | solution.py:132
  52.2 1.1 select_convert_fusion.turn_ref
  53.3 12.3 %all-to-all-done = bf16[128,16,384]{2,1,0:T(8,128)(2,1)S(1)} async-done(((bf16[128,16,384]{2,1,0:T(8,128)(2,1)}), bf16[128,16,384]{2,1,0:T(8,128)(2,1)S(1)}, u32[]{:S(2)}, u32[]{:S(2)}) %all-to-all-start) | async-done | bytes 1572896 | tf_op jit(solution)/shard_map/all_to_all | solution.py:203
  65.6 1.2 copy-done.1
  66.9 4.7 %all-to-all-start.2 = ((bf16[384,4,768]{0,2,1:T(8,128)(2,1)}), bf16[384,4,768]{0,2,1:T(8,128)(2,1)}, u32[]{:S(2)}, u32[]{:S(2)}) async-start(bf16[384,4,768]{0,2,1:T(8,128)(2,1)} %bitcast.57), calls=%async_computation.2 | async-start | bytes 4718592 | tf_op jit(solution)/shard_map/all_to_all | solution.py:185
  71.6 1.0 tile.8
  72.9 2.0 %tile.20 = f32[640,4,96]{0,2,1:T(8,128)} broadcast(f32[640,96]{0,1:T(8,128)} %get-tuple-element.17), dimensions={0,2} | broadcast | bytes 1228800 | tf_op jit(solution)/shard_map/tile | solution.py:218
  74.9 1.5 copy.84
  76.4 0.9 fusion.2.sel_ref
  77.3 0.9 fusion.4.selt_ref
  78.2 2.4 %fusion.25 = (bf16[5,128,384]{2,0,1:T(8,128)(2,1)S(1)}, bf16[5,128,384]{2,0,1:T(8,128)(2,1)S(1)}, bf16[5,128,384]{2,0,1:T(8,128)(2,1)S(1)}) fusion(bf16[16,128,384]{2,0,1:T(8,128)(2,1)} %bitcast.54), kind=kLoop, calls=%fused_computation.80 | loop fusion | bytes 2949120 | tf_op jit(solution)/shard_map/slice | solution.py:223
  80.6 0.8 copy.75
  81.5 0.8 copy.76
  82.3 0.9 copy.77
  83.2 1.7 slice_convert_fusion
  84.9 1.6 reduce-window.8
  86.5 0.9 reduce.1
  87.4 3.3 %fusion.23 = s32[128]{0:T(128)S(1)} fusion(bf16[16,128,384]{2,0,1:T(8,128)(2,1)} %bitcast.56), kind=kLoop, calls=%fused_computation.78 | loop fusion | flops 128 | bytes 768 | tf_op jit(solution)/shard_map/convert_element_type | solution.py:205
  90.8 3.0 %gather_fusion.2 = f32[640,384]{1,0:T(8,128)} fusion(f32[640,384]{1,0:T(8,128)S(1)} %copy.83, s32[1024]{0:T(1024)S(1)} %pad_clamp_fusion.1), kind=kCustom, calls=%fused_computation.2 | custom fusion | bytes 1968640 | tf_op jit(solution)/shard_map/jit(_take)/gather | solution.py:217
  93.8 3.0 %gather_fusion.3 = f32[640,384]{1,0:T(8,128)} fusion(f32[640,384]{1,0:T(8,128)S(1)} %copy.84, s32[1024]{0:T(1024)S(1)} %pad_clamp_fusion.1), kind=kCustom, calls=%fused_computation.3 | custom fusion | bytes 1968640 | tf_op jit(solution)/shard_map/jit(_take)/gather | solution.py:218
  97.3 0.9 copy.98
  98.2 24.6 %shard_map.104 = bf16[128,1920]{1,0:T(8,128)(2,1)} custom-call(bf16[640,384]{1,0:T(8,128)(2,1)} %bitcast.62, bf16[640,384]{1,0:T(8,128)(2,1)} %bitcast.63, bf16[640,384]{1,0:T(8,128)(2,1)} %bitcast.64, bf16[4,1024,128]{2,1,0:T(8,128)(2,1)} %get-tuple-element.27.kc_ref, bf16[4,1024,128]{2,1,0:T(8,128)(2,1)} %get-tuple-element.26.vc_ref, ...), custom_call_target="tpu_custom_call" | custom-call | tf_op jit(solution)/shard_map/pallas_call | solution.py:135
  122.8 1.3 copy.86
  124.1 1.2 copy.87
  125.3 9.0 %all-to-all-start.1 = ((bf16[128,15,128]{2,1,0:T(8,128)(2,1)}), bf16[128,15,128]{2,1,0:T(8,128)(2,1)S(1)}, u32[]{:S(2)}, u32[]{:S(2)}) async-start(bf16[128,15,128]{2,1,0:T(8,128)(2,1)} %copy.87), calls=%async_computation.1 | async-start | bytes 1048576 | tf_op jit(solution)/shard_map/all_to_all | solution.py:230
  134.4 4.3 %copy.89 = bf16[4,384,768]{2,1,0:T(8,128)(2,1)} copy(bf16[4,384,768]{1,2,0:T(8,128)(2,1)} %bitcast.22) | data formatting | bytes 4718592 | tf_op jit(solution)/shard_map/all_to_all | solution.py:185
  138.7 13.6 %all-to-all-done.1 = bf16[128,15,128]{2,1,0:T(8,128)(2,1)S(1)} async-done(((bf16[128,15,128]{2,1,0:T(8,128)(2,1)}), bf16[128,15,128]{2,1,0:T(8,128)(2,1)S(1)}, u32[]{:S(2)}, u32[]{:S(2)}) %all-to-all-start.1) | async-done | bytes 491552 | tf_op jit(solution)/shard_map/all_to_all | solution.py:230
  152.7 1.2 gather_fusion.4
  153.8 15.6 %all-gather = bf16[256,1536]{1,0:T(8,128)(2,1)S(1)} all-gather(bf16[256,384]{1,0:T(8,128)(2,1)S(1)} %gather_fusion.4), channel_id=2, replica_groups=mesh['req'=128,'tp'=4] {'tp'}, dimensions={1}, use_global_device_ids=true | all-gather | bytes 983040 | tf_op jit(solution)/shard_map/all_gather | solution.py:239
  169.4 2.5 %multiply_reduce_fusion = (f32[256]{0:T(256)S(1)}, f32[256,768]{1,0:T(8,128)S(1)}) fusion(bf16[256,1536]{1,0:T(8,128)(2,1)S(1)} %all-gather, bf16[1536,768]{1,0:T(8,128)(2,1)} %bitcast.61, bf16[256,768]{1,0:T(8,128)(2,1)S(1)} %copy-done.5), kind=kOutput, calls=%fused_computation.12 | convolution fusion | flops 604765952 | bytes 4326400 | tf_op jit(solution)/shard_map/dot_general | solution.py:240
  172.0 0.6 broadcast_in_dim.28
  172.6 3.6 %all-to-all-start.3 = ((f32[4,1,256]{2,1,0:T(1,128)}), f32[4,1,256]{2,1,0:T(1,128)S(1)}, u32[]{:S(2)}, u32[]{:S(2)}) async-start(f32[4,1,256]{2,1,0:T(1,128)} %broadcast_in_dim.28), calls=%async_computation.3 | async-start | bytes 8192 | tf_op jit(solution)/shard_map/all_to_all | solution.py:245
  176.1 5.3 %all-to-all-done.3 = f32[4,1,256]{2,1,0:T(1,128)S(1)} async-done(((f32[4,1,256]{2,1,0:T(1,128)}), f32[4,1,256]{2,1,0:T(1,128)S(1)}, u32[]{:S(2)}, u32[]{:S(2)}) %all-to-all-start.3) | async-done | bytes 4128 | tf_op jit(solution)/shard_map/all_to_all | solution.py:245
  181.5 1.0 multiply_convert_fusion
  (46 shorter events, 3.3 us)
Async XLA Ops:
  0.6 25.4 %copy-start = (bf16[8,2,128,384]{3,2,1,0:T(8,128)(2,1)S(1)}, bf16[8,2,128,384]{3,2,1,0:T(8,128)(2,1)}, u32[]{:S(2)}) copy-start(bf16[8,2,128,384]{3,2,1,0:T(8,128)(2,1)} %param.14) | copy-start | bytes 4718596
  3.7 0.6 copy-start.2
  8.5 17.5 %copy-start.6 = (s32[1,8]{1,0:T(1,128)S(1)}, s32[1,8]{1,0:T(1,128)}, u32[]{:S(2)}) copy-start(s32[1,8]{1,0:T(1,128)} %param.13) | copy-start | bytes 100
  8.5 57.2 %all-to-all-start = ((bf16[128,16,384]{2,1,0:T(8,128)(2,1)}), bf16[128,16,384]{2,1,0:T(8,128)(2,1)S(1)}, u32[]{:S(2)}, u32[]{:S(2)}) async-start(bf16[128,16,384]{2,1,0:T(8,128)(2,1)} %copy.74), calls=%async_computation | async-start | bytes 3145728 | tf_op jit(solution)/shard_map/all_to_all | solution.py:203
  65.6 1.2 copy-start.1
  66.9 58.4 %all-to-all-start.2 = ((bf16[384,4,768]{0,2,1:T(8,128)(2,1)}), bf16[384,4,768]{0,2,1:T(8,128)(2,1)}, u32[]{:S(2)}, u32[]{:S(2)}) async-start(bf16[384,4,768]{0,2,1:T(8,128)(2,1)} %bitcast.57), calls=%async_computation.2 | async-start | bytes 4718592 | tf_op jit(solution)/shard_map/all_to_all | solution.py:185
  122.8 11.6 %copy-start.3 = (s32[256]{0:T(256)S(1)}, s32[256]{0:T(256)}, u32[]{:S(2)}) copy-start(s32[256]{0:T(256)} %copy-done.2) | copy-start | bytes 3076
  125.3 27.0 %all-to-all-start.1 = ((bf16[128,15,128]{2,1,0:T(8,128)(2,1)}), bf16[128,15,128]{2,1,0:T(8,128)(2,1)S(1)}, u32[]{:S(2)}, u32[]{:S(2)}) async-start(bf16[128,15,128]{2,1,0:T(8,128)(2,1)} %copy.87), calls=%async_computation.1 | async-start | bytes 1048576 | tf_op jit(solution)/shard_map/all_to_all | solution.py:230
  152.7 16.8 %copy-start.5 = (bf16[256,768]{1,0:T(8,128)(2,1)S(1)}, bf16[256,768]{1,0:T(8,128)(2,1)}, u32[]{:S(2)}) copy-start(bf16[256,768]{1,0:T(8,128)(2,1)} %param.15) | copy-start | bytes 1179652
  169.4 6.7 %copy-start.4 = (bf16[768]{0:T(1024)(128)(2,1)S(1)}, bf16[768]{0:T(1024)(128)(2,1)}, u32[]{:S(2)}) copy-start(bf16[768]{0:T(1024)(128)(2,1)} %param.17) | copy-start | bytes 4612
  172.6 8.9 %all-to-all-start.3 = ((f32[4,1,256]{2,1,0:T(1,128)}), f32[4,1,256]{2,1,0:T(1,128)S(1)}, u32[]{:S(2)}, u32[]{:S(2)}) async-start(f32[4,1,256]{2,1,0:T(1,128)} %broadcast_in_dim.28), calls=%async_computation.3 | async-start | bytes 8192 | tf_op jit(solution)/shard_map/all_to_all | solution.py:245

commit v13 on v11

--- a/solution.py
+++ b/solution.py
@@ -72,8 +72,11 @@
 
     @pl.when(step == 0)
     def _():
-        rotated = turn_rows(kn_ref[...], cos_ref[...], sin_ref[...], turn_ref[...])
-        fresh = vn_ref[...]
+        rows = kn_ref.shape[0] * kn_ref.shape[1]
+        rotated = turn_rows(
+            kn_ref[...].reshape(rows, -1), cos_ref[...], sin_ref[...], turn_ref[...]
+        )
+        fresh = vn_ref[...].reshape(rows, -1)
         for head in range(heads):
             keys_ref[head] = jnp.dot(
                 rotated, sel_ref[head], preferred_element_type=jnp.float32
@@ -118,10 +121,10 @@
     o_ref[...] = total.astype(o_ref.dtype)
 
 
-def attend_slots(query, fresh_keys, fresh_values, cache_keys, cache_values, cos_all, sin_all, turn,
+def attend_slots(planes, cache_keys, cache_values, cos_all, sin_all, turn,
                  q_rank, cache_ok, k_rank, slot_cap):
-    rows, cols = query.shape
-    block = rows // slot_cap
+    _, block, cols = planes.shape
+    rows = slot_cap * block
     span = cache_keys.shape[0]
     heads = cols // HEAD_SIZE
     lanes = 128
@@ -137,9 +140,9 @@
         out_shape=jax.ShapeDtypeStruct((block, slot_cap * cols), jnp.bfloat16),
         grid=(slot_cap,),
         in_specs=[
-            pl.BlockSpec((block, cols), lambda i: (i, 0)),
-            pl.BlockSpec((rows, cols), whole),
-            pl.BlockSpec((rows, cols), whole),
+            pl.BlockSpec((None, block, cols), lambda i: (i, 0, 0)),
+            pl.BlockSpec((slot_cap, block, cols), lambda i: (1, 0, 0)),
+            pl.BlockSpec((slot_cap, block, cols), lambda i: (2, 0, 0)),
             pl.BlockSpec((heads, span, lanes), whole3),
             pl.BlockSpec((heads, span, lanes), whole3),
             pl.BlockSpec((rows, cols), whole),
@@ -157,7 +160,7 @@
             pltpu.VMEM((heads, rows, lanes), jnp.bfloat16),
         ],
         compiler_params=pltpu.CompilerParams(dimension_semantics=("arbitrary",)),
-    )(query, fresh_keys, fresh_values, split(cache_keys), split(cache_values), cos_all, sin_all,
+    )(planes, planes, planes, split(cache_keys), split(cache_values), cos_all, sin_all,
       turn, sel, sel_t, q_rank, cache_ok, k_rank)
 
 
@@ -219,12 +222,8 @@
     cache_ok = (jnp.arange(cache_span, dtype=jnp.int32) < length).astype(jnp.int32)[None, :]
     k_rank = jnp.where(live_slot, new_rank, jnp.int32(2**30))[None, :]
     q_rank = new_rank[:, None]
-    part_rows = [
-        planes[p * slot_cap : (p + 1) * slot_cap].reshape(buffer_len, head_cols)
-        for p in range(parts)
-    ]
     result = attend_slots(
-        part_rows[0], part_rows[1], part_rows[2], cache_keys, cache_values, cos_all, sin_all,
+        planes, cache_keys, cache_values, cos_all, sin_all,
         turn_matrix(head_cols), q_rank, cache_ok, k_rank, slot_cap,
     )
     returned = lax.all_to_all(

time: 168 us -> 171 us (1.018)
  waiting for transfers between devices: 31.7 us -> 36 us
  other arithmetic: 9.34 us -> 6.96 us
    all_to_all x1, waiting for transfers between devices: 12.8 us -> 17 us  [on_device(): lax.all_to_all(outgoing, 'req', split_axis=0, concat_axis=0, tiled=True)]
    slice x4 -> x0, local copies, waits for them, and re-layouts: 3.05 us -> none  [on_device(): planes[p * slot_cap:(p + 1) * slot_cap].reshape(buffer_len, head_cols)]
    convert_element_type x2, other arithmetic: 2.48 us -> 0.12 us  [on_device(): arrived_counts = planes[slot_cap * parts, :, 0].astype(jnp.int32)]
    another operation x2, local copies, waits for them, and re-layouts: 1.35 us -> 3.57 us  [on_device(): cos_all = jnp.tile(cosine, (1, heads_here))]
    unnamed x10 -> x16, local copies, waits for them, and re-layouts: 5.24 us -> 6.4 us
  transfers between devices with their start and end apart: 4 -> 4, of which waited for: 3 -> 3; matrix products, arithmetic and copies ran while one was open for 27% -> 25% of each run, Pallas kernels for 15% -> 15%
where the time goes in v13:
time: 171 us; the launch traced here: 168 us
  local copies, waits for them, and re-layouts  44.6 us (26%)
  waiting for transfers between devices  36 us (21%)
  starting transfers between devices  34.7 us (20%)
  Pallas kernels  24.6 us (14%)
  blocking collectives  15.6 us (9%)
  other arithmetic  6.96 us (4%)
  matrix products  4.2 us (2%)
    pallas_call x1, Pallas kernels, attend_slots(): pl.pallas_call(attend_kernel, out_shape=jax.ShapeDtypeStruct((block, slot...  24.6 us
    all_to_all x1, starting transfers between devices, on_device(): lax.all_to_all(outgoing, 'req', split_axis=0, concat_axis=0, tiled=True)  17.5 us
    all_to_all x1, waiting for transfers between devices, on_device(): lax.all_to_all(outgoing, 'req', split_axis=0, concat_axis=0, tiled=True)  17 us
    all_gather x1, blocking collectives, on_device(): attn_all = lax.all_gather(attn_rows, 'tp', axis=1, tiled=True)  15.6 us
    all_to_all x1, waiting for transfers between devices, on_device(): lax.all_to_all(result.reshape(devices, slot_cap * parts, head_cols // par...  13.7 us
    another operation x4, local copies, waits for them, and re-layouts, attend_slots(): x.reshape(x.shape[0], heads, HEAD_SIZE)  11.2 us
    all_to_all x1, starting transfers between devices, on_device(): lax.all_to_all(result.reshape(devices, slot_cap * parts, head_cols // par...  9.05 us
    unnamed x16, local copies, waits for them, and re-layouts  6.4 us
  transfers between devices with their start and end apart: 4, of which 3 were waited for; matrix products, arithmetic and copies ran while one was open for 25% of the time, Pallas kernels for 15%

profile of v13, /device:TPU:56, one launch (start us, length us, event | category | flops | bytes accessed | tf_op | source)
XLA Modules:
  0.0 168.2 jit_solution(6387764775461420237)
XLA Ops:
  0.6 0.8 compare_select_fusion.1
  1.5 1.9 %gather_fusion = s32[256]{0:T(256)S(1)} fusion(s32[128]{0:T(128)} %param.11, s32[1024]{0:T(1024)S(1)} %pad_clamp_fusion.2), kind=kCustom, calls=%fused_computation | custom fusion | bytes 3072 | tf_op jit(solution)/shard_map/gather | solution.py:189
  3.3 0.1 convert_reduce_fusion.1
  3.5 0.2 convert_reduce_fusion
  3.7 1.7 fusion
  5.4 0.2 copy.80
  5.6 0.2 pad_maximum_fusion
  5.8 2.1 %copy.81 = bf16[128,16,384]{2,1,0:T(8,128)(2,1)} copy(bf16[128,16,384]{2,0,1:T(8,128)(2,1)S(1)} %pad_maximum_fusion) | data formatting | bytes 3145728 | tf_op jit(solution)/shard_map/concatenate | solution.py:203
  7.9 17.5 %all-to-all-start = ((bf16[128,16,384]{2,1,0:T(8,128)(2,1)}), bf16[128,16,384]{2,1,0:T(8,128)(2,1)S(1)}, u32[]{:S(2)}, u32[]{:S(2)}) async-start(bf16[128,16,384]{2,1,0:T(8,128)(2,1)} %copy.81), calls=%async_computation | async-start | bytes 3145728 | tf_op jit(solution)/shard_map/all_to_all | solution.py:206
  25.4 1.9 %gather_fusion.1 = bf16[8,2,128,384]{3,2,1,0:T(8,128)(2,1)} fusion(bf16[8,2,128,384]{3,2,1,0:T(8,128)(2,1)S(1)} %copy-done, s32[1024]{0:T(1024)S(1)} %pad_clamp_fusion.1), kind=kCustom, calls=%fused_computation.1 | custom fusion | bytes 3145760 | tf_op jit(solution)/shard_map/gather | solution.py:211
  27.3 2.7 %fusion.22 = (bf16[8,1,128,384]{3,2,1,0:T(8,128)(2,1)}, bf16[8,1,128,384]{3,2,1,0:T(8,128)(2,1)}) fusion(bf16[8,2,128,384]{3,2,1,0:T(8,128)(2,1)} %gather_fusion.1), kind=kLoop, calls=%fused_computation.76 | loop fusion | bytes 3145728 | tf_op jit(solution)/shard_map/slice | solution.py:214
  30.1 3.2 %reshape.425 = bf16[1024,4,96]{2,1,0:T(4,128)(2,1)} reshape(bf16[8,1,128,384]{3,2,1,0:T(8,128)(2,1)} %get-tuple-element.2) | data formatting | bytes 1572864 | tf_op jit(solution)/shard_map/reshape;reshape;squeeze | solution.py:134
  33.3 2.4 %copy.86 = bf16[1024,4,96]{2,0,1:T(8,128)(2,1)} copy(bf16[1024,4,96]{2,1,0:T(4,128)(2,1)} %reshape.425) | data formatting | bytes 1572864 | tf_op jit(solution)/shard_map/reshape;reshape;squeeze | solution.py:134
  35.7 3.2 %reshape.424 = bf16[1024,4,96]{2,1,0:T(4,128)(2,1)} reshape(bf16[8,1,128,384]{3,2,1,0:T(8,128)(2,1)} %get-tuple-element.3) | data formatting | bytes 1572864 | tf_op jit(solution)/shard_map/reshape;reshape;squeeze | solution.py:134
  38.9 2.3 %copy.84 = bf16[1024,4,96]{2,0,1:T(8,128)(2,1)} copy(bf16[1024,4,96]{2,1,0:T(4,128)(2,1)} %reshape.424) | data formatting | bytes 1572864 | tf_op jit(solution)/shard_map/reshape;reshape;squeeze | solution.py:134
  41.9 4.3 %copy.93 = bf16[384,3072]{0,1:T(8,128)(2,1)} copy(bf16[384,3072]{1,0:T(8,128)(2,1)} %param.16) | data formatting | bytes 4718592 | tf_op args[7]
  46.3 0.6 compare_convert_fusion.cache_ok_ref
  46.9 1.1 select_convert_fusion.turn_ref
  48.0 17.0 %all-to-all-done = bf16[128,16,384]{2,1,0:T(8,128)(2,1)S(1)} async-done(((bf16[128,16,384]{2,1,0:T(8,128)(2,1)}), bf16[128,16,384]{2,1,0:T(8,128)(2,1)S(1)}, u32[]{:S(2)}, u32[]{:S(2)}) %all-to-all-start) | async-done | bytes 1572896 | tf_op jit(solution)/shard_map/all_to_all | solution.py:206
  65.0 1.2 copy-done.2
  66.2 4.7 %all-to-all-start.2 = ((bf16[384,4,768]{0,2,1:T(8,128)(2,1)}), bf16[384,4,768]{0,2,1:T(8,128)(2,1)}, u32[]{:S(2)}, u32[]{:S(2)}) async-start(bf16[384,4,768]{0,2,1:T(8,128)(2,1)} %bitcast.59), calls=%async_computation.2 | async-start | bytes 4718592 | tf_op jit(solution)/shard_map/all_to_all | solution.py:188
  70.9 3.4 %pad_bitcast_fusion = (bf16[4,1024,128]{2,1,0:T(8,128)(2,1)}, bf16[4,1024,128]{2,1,0:T(8,128)(2,1)}) fusion(bf16[1024,4,96]{2,0,1:T(8,128)(2,1)} %copy.86, bf16[1024,4,96]{2,0,1:T(8,128)(2,1)} %copy.84), kind=kLoop, calls=%fused_computation.8 | loop fusion | bytes 3670016 | tf_op jit(solution)/shard_map/transpose | solution.py:135
  74.3 0.9 fusion.2.sel_ref
  75.2 0.9 fusion.4.selt_ref
  76.1 0.4 copy.108
  76.5 0.2 reduce-window.8
  76.7 0.1 reduce.1
  76.8 0.1 convert_reduce_fusion.2
  77.0 0.5 multiply_sine_fusion
  77.5 1.0 tile.8
  78.5 2.6 %copy.88.cos_ref = f32[640,384]{1,0:T(8,128)} copy(f32[640,384]{0,1:T(8,128)} %bitcast.61) | data formatting | bytes 1966080 | tf_op jit(solution)/shard_map/tile | solution.py:220
  81.2 1.3 copy.89.sin_ref
  82.4 0.6 copy_bitcast_fusion.1
  83.0 0.9 copy.103
  83.9 24.6 %shard_map.104 = bf16[128,1920]{1,0:T(8,128)(2,1)} custom-call(bf16[16,128,384]{2,1,0:T(8,128)(2,1)} %bitcast.56, bf16[16,128,384]{2,1,0:T(8,128)(2,1)} %bitcast.57, bf16[16,128,384]{2,1,0:T(8,128)(2,1)} %bitcast.58, bf16[4,1024,128]{2,1,0:T(8,128)(2,1)} %get-tuple-element.24.kc_ref, bf16[4,1024,128]{2,1,0:T(8,128)(2,1)} %get-tuple-element.23.vc_ref, ...), custom_call_target="tpu_custom_call" | custom-call | tf_op jit(solution)/shard_map/pallas_call | solution.py:138
  108.5 1.3 copy.91
  109.8 1.2 copy.92
  111.0 9.0 %all-to-all-start.1 = ((bf16[128,15,128]{2,1,0:T(8,128)(2,1)}), bf16[128,15,128]{2,1,0:T(8,128)(2,1)S(1)}, u32[]{:S(2)}, u32[]{:S(2)}) async-start(bf16[128,15,128]{2,1,0:T(8,128)(2,1)} %copy.92), calls=%async_computation.1 | async-start | bytes 1048576 | tf_op jit(solution)/shard_map/all_to_all | solution.py:229
  120.1 4.3 %copy.94 = bf16[4,384,768]{2,1,0:T(8,128)(2,1)} copy(bf16[4,384,768]{1,2,0:T(8,128)(2,1)} %bitcast.19) | data formatting | bytes 4718592 | tf_op jit(solution)/shard_map/all_to_all | solution.py:188
  124.4 13.7 %all-to-all-done.1 = bf16[128,15,128]{2,1,0:T(8,128)(2,1)S(1)} async-done(((bf16[128,15,128]{2,1,0:T(8,128)(2,1)}), bf16[128,15,128]{2,1,0:T(8,128)(2,1)S(1)}, u32[]{:S(2)}, u32[]{:S(2)}) %all-to-all-start.1) | async-done | bytes 491552 | tf_op jit(solution)/shard_map/all_to_all | solution.py:229
  138.1 0.3 reshape.393
  138.4 1.2 gather_fusion.2
  139.5 15.6 %all-gather = bf16[256,1536]{1,0:T(8,128)(2,1)S(1)} all-gather(bf16[256,384]{1,0:T(8,128)(2,1)S(1)} %gather_fusion.2), channel_id=2, replica_groups=mesh['req'=128,'tp'=4] {'tp'}, dimensions={1}, use_global_device_ids=true | all-gather | bytes 983040 | tf_op jit(solution)/shard_map/all_gather | solution.py:238
  155.1 2.5 %multiply_reduce_fusion = (f32[256]{0:T(256)S(1)}, f32[256,768]{1,0:T(8,128)S(1)}) fusion(bf16[256,1536]{1,0:T(8,128)(2,1)S(1)} %all-gather, bf16[1536,768]{1,0:T(8,128)(2,1)} %bitcast.63, bf16[256,768]{1,0:T(8,128)(2,1)S(1)} %copy-done.5), kind=kOutput, calls=%fused_computation.11 | convolution fusion | flops 604765952 | bytes 4326400 | tf_op jit(solution)/shard_map/dot_general | solution.py:239
  157.7 0.6 broadcast_in_dim.25
  158.3 3.6 %all-to-all-start.3 = ((f32[4,1,256]{2,1,0:T(1,128)}), f32[4,1,256]{2,1,0:T(1,128)S(1)}, u32[]{:S(2)}, u32[]{:S(2)}) async-start(f32[4,1,256]{2,1,0:T(1,128)} %broadcast_in_dim.25), calls=%async_computation.3 | async-start | bytes 8192 | tf_op jit(solution)/shard_map/all_to_all | solution.py:244
  161.8 5.3 %all-to-all-done.3 = f32[4,1,256]{2,1,0:T(1,128)S(1)} async-done(((f32[4,1,256]{2,1,0:T(1,128)}), f32[4,1,256]{2,1,0:T(1,128)S(1)}, u32[]{:S(2)}, u32[]{:S(2)}) %all-to-all-start.3) | async-done | bytes 4128 | tf_op jit(solution)/shard_map/all_to_all | solution.py:244
  167.2 1.0 multiply_convert_fusion
  (39 shorter events, 0.5 us)
Async XLA Ops:
  0.6 24.8 %copy-start = (bf16[8,2,128,384]{3,2,1,0:T(8,128)(2,1)S(1)}, bf16[8,2,128,384]{3,2,1,0:T(8,128)(2,1)}, u32[]{:S(2)}) copy-start(bf16[8,2,128,384]{3,2,1,0:T(8,128)(2,1)} %param.14) | copy-start | bytes 4718596
  7.9 17.5 %copy-start.6 = (s32[1,8]{1,0:T(1,128)S(1)}, s32[1,8]{1,0:T(1,128)}, u32[]{:S(2)}) copy-start(s32[1,8]{1,0:T(1,128)} %param.13) | copy-start | bytes 100
  7.9 57.2 %all-to-all-start = ((bf16[128,16,384]{2,1,0:T(8,128)(2,1)}), bf16[128,16,384]{2,1,0:T(8,128)(2,1)S(1)}, u32[]{:S(2)}, u32[]{:S(2)}) async-start(bf16[128,16,384]{2,1,0:T(8,128)(2,1)} %copy.81), calls=%async_computation | async-start | bytes 3145728 | tf_op jit(solution)/shard_map/all_to_all | solution.py:206
  65.0 1.2 copy-start.2
  66.2 44.8 %all-to-all-start.2 = ((bf16[384,4,768]{0,2,1:T(8,128)(2,1)}), bf16[384,4,768]{0,2,1:T(8,128)(2,1)}, u32[]{:S(2)}, u32[]{:S(2)}) async-start(bf16[384,4,768]{0,2,1:T(8,128)(2,1)} %bitcast.59), calls=%async_computation.2 | async-start | bytes 4718592 | tf_op jit(solution)/shard_map/all_to_all | solution.py:188
  70.9 5.3 %copy-start.3 = (bf16[128,16,384]{2,1,0:T(8,128)(2,1)S(1)}, bf16[128,16,384]{2,1,0:T(8,128)(2,1)}, u32[]{:S(2)}) copy-start(bf16[128,16,384]{2,1,0:T(8,128)(2,1)} %copy-done.2) | copy-start | bytes 4718596
  76.5 4.6 %copy-start.1 = (bf16[128,16,384]{2,0,1:T(8,128)(2,1)}, bf16[128,16,384]{2,0,1:T(8,128)(2,1)S(1)}, u32[]{:S(2)}) copy-start(bf16[128,16,384]{2,0,1:T(8,128)(2,1)S(1)} %copy.108) | copy-start | bytes 4718596
  111.0 27.0 %all-to-all-start.1 = ((bf16[128,15,128]{2,1,0:T(8,128)(2,1)}), bf16[128,15,128]{2,1,0:T(8,128)(2,1)S(1)}, u32[]{:S(2)}, u32[]{:S(2)}) async-start(bf16[128,15,128]{2,1,0:T(8,128)(2,1)} %copy.92), calls=%async_computation.1 | async-start | bytes 1048576 | tf_op jit(solution)/shard_map/all_to_all | solution.py:229
  138.4 16.7 %copy-start.5 = (bf16[256,768]{1,0:T(8,128)(2,1)S(1)}, bf16[256,768]{1,0:T(8,128)(2,1)}, u32[]{:S(2)}) copy-start(bf16[256,768]{1,0:T(8,128)(2,1)} %param.15) | copy-start | bytes 1179652
  155.1 6.7 %copy-start.4 = (bf16[768]{0:T(1024)(128)(2,1)S(1)}, bf16[768]{0:T(1024)(128)(2,1)}, u32[]{:S(2)}) copy-start(bf16[768]{0:T(1024)(128)(2,1)} %param.17) | copy-start | bytes 4612
  158.3 8.9 %all-to-all-start.3 = ((f32[4,1,256]{2,1,0:T(1,128)}), f32[4,1,256]{2,1,0:T(1,128)S(1)}, u32[]{:S(2)}, u32[]{:S(2)}) async-start(f32[4,1,256]{2,1,0:T(1,128)} %broadcast_in_dim.25), calls=%async_computation.3 | async-start | bytes 8192 | tf_op jit(solution)/shard_map/all_to_all | solution.py:244

commit v14 on v11

--- a/solution.py
+++ b/solution.py
@@ -193,13 +193,14 @@
         sends_to[None, :, :]
         & (slot_in[None, :, None] == jnp.arange(slot_cap, dtype=jnp.int32)[:, None, None])
     ).astype(jnp.bfloat16)
-    slots = jnp.einsum(
-        "jid,ipc->dpjc", pick, qkv_rows, preferred_element_type=jnp.float32
+    row_part = jnp.repeat(jnp.arange(parts, dtype=jnp.int32), slot_cap)
+    sources = jnp.concatenate(
+        [qkv_rows[:, row_part, :], jnp.ones((row_count, 1, head_cols), qkv_rows.dtype)], axis=1
+    )
+    picks = jnp.concatenate([jnp.tile(pick, (parts, 1, 1)), sends_to[None].astype(jnp.bfloat16)])
+    outgoing = jnp.einsum(
+        "rid,irc->drc", picks, sources, preferred_element_type=jnp.float32
     ).astype(jnp.bfloat16)
-    count_row = jnp.broadcast_to(counts.astype(jnp.bfloat16)[:, None, None], (devices, 1, head_cols))
-    outgoing = jnp.concatenate(
-        [slots.reshape(devices, slot_cap * parts, head_cols), count_row], axis=1
-    )
     arrived = lax.all_to_all(outgoing, "req", split_axis=0, concat_axis=0, tiled=True)
     planes = arrived.transpose(1, 0, 2)
     arrived_counts = planes[slot_cap * parts, :, 0].astype(jnp.int32)

time: 168 us -> 177 us (1.054)
  local copies, waits for them, and re-layouts: 44 us -> 51 us
    gather x0 -> x2, local copies, waits for them, and re-layouts: none -> 7.21 us  [on_device(): qkv_rows[:, row_part, :]]
    concatenate x1 -> x0, local copies, waits for them, and re-layouts: 2.07 us -> none  [on_device(): jnp.concatenate([slots.reshape(devices, slot_cap * parts, head_cols), cou...]
    unnamed x10 -> x12, local copies, waits for them, and re-layouts: 5.24 us -> 5.22 us
  transfers between devices with their start and end apart: 4 -> 4, of which waited for: 3 -> 3; matrix products, arithmetic and copies ran while one was open for 27% -> 26% of each run, Pallas kernels for 15% -> 14%
where the time goes in v14:
time: 177 us; the launch traced here: 174 us
  local copies, waits for them, and re-layouts  51 us (29%)
  starting transfers between devices  34.8 us (20%)
  waiting for transfers between devices  31.8 us (18%)
  Pallas kernels  24.6 us (14%)
  blocking collectives  15.6 us (9%)
  other arithmetic  9.5 us (5%)
  matrix products  5.37 us (3%)
    pallas_call x1, Pallas kernels, attend_slots(): pl.pallas_call(attend_kernel, out_shape=jax.ShapeDtypeStruct((block, slot...  24.6 us
    all_to_all x1, starting transfers between devices, on_device(): lax.all_to_all(outgoing, 'req', split_axis=0, concat_axis=0, tiled=True)  17.5 us
    all_gather x1, blocking collectives, on_device(): attn_all = lax.all_gather(attn_rows, 'tp', axis=1, tiled=True)  15.6 us
    all_to_all x1, waiting for transfers between devices, on_device(): lax.all_to_all(result.reshape(devices, slot_cap * parts, head_cols // par...  13.7 us
    all_to_all x1, waiting for transfers between devices, on_device(): lax.all_to_all(outgoing, 'req', split_axis=0, concat_axis=0, tiled=True)  12.8 us
    another operation x4, local copies, waits for them, and re-layouts, attend_slots(): x.reshape(x.shape[0], heads, HEAD_SIZE)  11.2 us
    all_to_all x1, starting transfers between devices, on_device(): lax.all_to_all(result.reshape(devices, slot_cap * parts, head_cols // par...  9.05 us
    gather x2, local copies, waits for them, and re-layouts, on_device(): qkv_rows[:, row_part, :]  7.21 us
  transfers between devices with their start and end apart: 4, of which 3 were waited for; matrix products, arithmetic and copies ran while one was open for 26% of the time, Pallas kernels for 14%

profile of v14, /device:TPU:56, one launch (start us, length us, event | category | flops | bytes accessed | tf_op | source)
XLA Modules:
  0.0 174.1 jit_solution(1122326241269656110)
XLA Ops:
  0.7 0.8 compare_select_fusion.1
  1.5 1.9 %gather_fusion.1 = s32[256]{0:T(256)S(1)} fusion(s32[128]{0:T(128)} %param.11, s32[1024]{0:T(1024)S(1)} %pad_clamp_fusion.2), kind=kCustom, calls=%fused_computation.1 | custom fusion | bytes 3072 | tf_op jit(solution)/shard_map/gather | solution.py:186
  3.5 0.2 convert_reduce_fusion
  3.9 2.7 %gather_fusion = bf16[15,256,384]{2,1,0:T(8,128)(2,1)} fusion(bf16[256,3,384]{2,0,1:T(8,128)(2,1)S(1)} %copy-done.1, s32[1024]{0:T(1024)S(1)} %pad_clamp_fusion.3), kind=kCustom, calls=%fused_computation | custom fusion | bytes 5898300 | tf_op jit(solution)/shard_map/gather | solution.py:198
  6.6 4.6 %copy.96 = bf16[15,256,384]{1,2,0:T(8,128)(2,1)} copy(bf16[15,256,384]{2,1,0:T(8,128)(2,1)} %gather_fusion) | data formatting | bytes 5898240 | tf_op jit(solution)/shard_map/gather | solution.py:198
  11.1 0.2 and_convert_fusion
  11.4 0.2 tile.12
  11.6 2.8 %fusion.5 = bf16[128,16,384]{0,2,1:T(8,128)(2,1)S(1)} fusion(bf16[256,15,384]{0,2,1:T(8,128)(2,1)} %bitcast.55, bf16[1,256,128]{2,1,0:T(8,128)(2,1)S(1)} %fusion.18, bf16[15,256,128]{2,1,0:T(8,128)(2,1)S(1)} %bitcast.62), kind=kOutput, calls=%fused_computation.7 | convolution fusion | flops 403963904 | bytes 5570560 | tf_op jit(solution)/shard_map/rid,irc->drc/dot_general | solution.py:201
  14.4 1.9 %copy.97 = bf16[128,16,384]{2,1,0:T(8,128)(2,1)} copy(bf16[128,16,384]{0,2,1:T(8,128)(2,1)S(1)} %fusion.5) | data formatting | bytes 3145728 | tf_op jit(solution)/shard_map/convert_element_type | solution.py:203
  16.3 17.5 %all-to-all-start = ((bf16[128,16,384]{2,1,0:T(8,128)(2,1)}), bf16[128,16,384]{2,1,0:T(8,128)(2,1)S(1)}, u32[]{:S(2)}, u32[]{:S(2)}) async-start(bf16[128,16,384]{2,1,0:T(8,128)(2,1)} %copy.97), calls=%async_computation | async-start | bytes 3145728 | tf_op jit(solution)/shard_map/all_to_all | solution.py:204
  33.9 1.9 %gather_fusion.2 = bf16[8,2,128,384]{3,2,1,0:T(8,128)(2,1)} fusion(bf16[8,2,128,384]{3,2,1,0:T(8,128)(2,1)S(1)} %copy-done, s32[1024]{0:T(1024)S(1)} %pad_clamp_fusion.1), kind=kCustom, calls=%fused_computation.2 | custom fusion | bytes 3145760 | tf_op jit(solution)/shard_map/gather | solution.py:209
  35.8 2.7 %fusion.32 = (bf16[8,1,128,384]{3,2,1,0:T(8,128)(2,1)}, bf16[8,1,128,384]{3,2,1,0:T(8,128)(2,1)}) fusion(bf16[8,2,128,384]{3,2,1,0:T(8,128)(2,1)} %gather_fusion.2), kind=kLoop, calls=%fused_computation.82 | loop fusion | bytes 3145728 | tf_op jit(solution)/shard_map/slice | solution.py:212
  38.5 3.2 %reshape.499 = bf16[1024,4,96]{2,1,0:T(4,128)(2,1)} reshape(bf16[8,1,128,384]{3,2,1,0:T(8,128)(2,1)} %get-tuple-element.2) | data formatting | bytes 1572864 | tf_op jit(solution)/shard_map/reshape;reshape;squeeze | solution.py:131
  41.7 2.3 %copy.104 = bf16[1024,4,96]{2,0,1:T(8,128)(2,1)} copy(bf16[1024,4,96]{2,1,0:T(4,128)(2,1)} %reshape.499) | data formatting | bytes 1572864 | tf_op jit(solution)/shard_map/reshape;reshape;squeeze | solution.py:131
  44.1 3.2 %reshape.498 = bf16[1024,4,96]{2,1,0:T(4,128)(2,1)} reshape(bf16[8,1,128,384]{3,2,1,0:T(8,128)(2,1)} %get-tuple-element.3) | data formatting | bytes 1572864 | tf_op jit(solution)/shard_map/reshape;reshape;squeeze | solution.py:131
  47.3 2.4 %copy.102 = bf16[1024,4,96]{2,0,1:T(8,128)(2,1)} copy(bf16[1024,4,96]{2,1,0:T(4,128)(2,1)} %reshape.498) | data formatting | bytes 1572864 | tf_op jit(solution)/shard_map/reshape;reshape;squeeze | solution.py:131
  50.4 4.3 %copy.111 = bf16[384,3072]{0,1:T(8,128)(2,1)} copy(bf16[384,3072]{1,0:T(8,128)(2,1)} %param.16) | data formatting | bytes 4718592 | tf_op args[7]
  54.7 0.6 compare_convert_fusion.cache_ok_ref
  55.3 3.3 %pad_bitcast_fusion = (bf16[4,1024,128]{2,1,0:T(8,128)(2,1)}, bf16[4,1024,128]{2,1,0:T(8,128)(2,1)}) fusion(bf16[1024,4,96]{2,0,1:T(8,128)(2,1)} %copy.104, bf16[1024,4,96]{2,0,1:T(8,128)(2,1)} %copy.102), kind=kLoop, calls=%fused_computation.12 | loop fusion | bytes 3670016 | tf_op jit(solution)/shard_map/transpose | solution.py:132
  58.7 1.1 select_convert_fusion.turn_ref
  59.8 0.9 fusion.12.sel_ref
  60.7 12.8 %all-to-all-done = bf16[128,16,384]{2,1,0:T(8,128)(2,1)S(1)} async-done(((bf16[128,16,384]{2,1,0:T(8,128)(2,1)}), bf16[128,16,384]{2,1,0:T(8,128)(2,1)S(1)}, u32[]{:S(2)}, u32[]{:S(2)}) %all-to-all-start) | async-done | bytes 1572896 | tf_op jit(solution)/shard_map/all_to_all | solution.py:204
  73.5 4.7 %all-to-all-start.2 = ((bf16[384,4,768]{0,2,1:T(8,128)(2,1)}), bf16[384,4,768]{0,2,1:T(8,128)(2,1)}, u32[]{:S(2)}, u32[]{:S(2)}) async-start(bf16[384,4,768]{0,2,1:T(8,128)(2,1)} %bitcast.52), calls=%async_computation.2 | async-start | bytes 4718592 | tf_op jit(solution)/shard_map/all_to_all | solution.py:185
  78.2 0.9 fusion.14.selt_ref
  79.1 0.4 fusion.33
  79.6 0.9 copy.98
  80.5 0.9 copy.99
  81.4 0.8 copy.100
  82.6 2.4 %fusion.31 = s32[128]{0:T(128)S(1)} fusion(bf16[16,128,384]{2,0,1:T(8,128)(2,1)S(1)} %bitcast.51), kind=kLoop, calls=%fused_computation.81 | loop fusion | flops 128 | bytes 768 | tf_op jit(solution)/shard_map/convert_element_type | solution.py:206
  85.0 0.5 multiply_sine_fusion
  85.6 1.3 copy.106.cos_ref
  87.0 1.4 copy.107.sin_ref
  88.3 0.6 copy_bitcast_fusion
  88.9 0.9 copy.120
  89.8 24.6 %shard_map.104 = bf16[128,1920]{1,0:T(8,128)(2,1)} custom-call(bf16[640,384]{1,0:T(8,128)(2,1)} %bitcast.57, bf16[640,384]{1,0:T(8,128)(2,1)} %bitcast.58, bf16[640,384]{1,0:T(8,128)(2,1)} %bitcast.59, bf16[4,1024,128]{2,1,0:T(8,128)(2,1)} %get-tuple-element.27.kc_ref, bf16[4,1024,128]{2,1,0:T(8,128)(2,1)} %get-tuple-element.26.vc_ref, ...), custom_call_target="tpu_custom_call" | custom-call | tf_op jit(solution)/shard_map/pallas_call | solution.py:135
  114.4 1.3 copy.109
  115.7 1.2 copy.110
  116.9 9.0 %all-to-all-start.1 = ((bf16[128,15,128]{2,1,0:T(8,128)(2,1)}), bf16[128,15,128]{2,1,0:T(8,128)(2,1)S(1)}, u32[]{:S(2)}, u32[]{:S(2)}) async-start(bf16[128,15,128]{2,1,0:T(8,128)(2,1)} %copy.110), calls=%async_computation.1 | async-start | bytes 1048576 | tf_op jit(solution)/shard_map/all_to_all | solution.py:231
  126.0 4.3 %copy.112 = bf16[4,384,768]{2,1,0:T(8,128)(2,1)} copy(bf16[4,384,768]{1,2,0:T(8,128)(2,1)} %bitcast.21) | data formatting | bytes 4718592 | tf_op jit(solution)/shard_map/all_to_all | solution.py:185
  130.3 13.7 %all-to-all-done.1 = bf16[128,15,128]{2,1,0:T(8,128)(2,1)S(1)} async-done(((bf16[128,15,128]{2,1,0:T(8,128)(2,1)}), bf16[128,15,128]{2,1,0:T(8,128)(2,1)S(1)}, u32[]{:S(2)}, u32[]{:S(2)}) %all-to-all-start.1) | async-done | bytes 491552 | tf_op jit(solution)/shard_map/all_to_all | solution.py:231
  144.0 0.3 reshape.461
  144.3 1.2 gather_fusion.3
  145.4 15.6 %all-gather = bf16[256,1536]{1,0:T(8,128)(2,1)S(1)} all-gather(bf16[256,384]{1,0:T(8,128)(2,1)S(1)} %gather_fusion.3), channel_id=2, replica_groups=mesh['req'=128,'tp'=4] {'tp'}, dimensions={1}, use_global_device_ids=true | all-gather | bytes 983040 | tf_op jit(solution)/shard_map/all_gather | solution.py:240
  161.0 2.5 %multiply_reduce_fusion = (f32[256]{0:T(256)S(1)}, f32[256,768]{1,0:T(8,128)S(1)}) fusion(bf16[256,1536]{1,0:T(8,128)(2,1)S(1)} %all-gather, bf16[1536,768]{1,0:T(8,128)(2,1)} %bitcast.56, bf16[256,768]{1,0:T(8,128)(2,1)S(1)} %copy-done.3), kind=kOutput, calls=%fused_computation.15 | convolution fusion | flops 604765952 | bytes 4326400 | tf_op jit(solution)/shard_map/dot_general | solution.py:241
  163.5 0.6 broadcast_in_dim.25
  164.2 3.6 %all-to-all-start.3 = ((f32[4,1,256]{2,1,0:T(1,128)}), f32[4,1,256]{2,1,0:T(1,128)S(1)}, u32[]{:S(2)}, u32[]{:S(2)}) async-start(f32[4,1,256]{2,1,0:T(1,128)} %broadcast_in_dim.25), calls=%async_computation.3 | async-start | bytes 8192 | tf_op jit(solution)/shard_map/all_to_all | solution.py:246
  167.7 5.3 %all-to-all-done.3 = f32[4,1,256]{2,1,0:T(1,128)S(1)} async-done(((f32[4,1,256]{2,1,0:T(1,128)}), f32[4,1,256]{2,1,0:T(1,128)S(1)}, u32[]{:S(2)}, u32[]{:S(2)}) %all-to-all-start.3) | async-done | bytes 4128 | tf_op jit(solution)/shard_map/all_to_all | solution.py:246
  173.0 1.0 multiply_convert_fusion
  (42 shorter events, 1.1 us)
Async XLA Ops:
  0.6 33.2 %copy-start = (bf16[8,2,128,384]{3,2,1,0:T(8,128)(2,1)S(1)}, bf16[8,2,128,384]{3,2,1,0:T(8,128)(2,1)}, u32[]{:S(2)}) copy-start(bf16[8,2,128,384]{3,2,1,0:T(8,128)(2,1)} %param.14) | copy-start | bytes 4718596
  0.6 3.3 %copy-start.1 = (bf16[256,3,384]{2,0,1:T(8,128)(2,1)S(1)}, bf16[256,3,384]{2,0,1:T(8,128)(2,1)}, u32[]{:S(2)}) copy-start(bf16[256,3,384]{2,0,1:T(8,128)(2,1)} %param.9) | copy-start | bytes 1769476
  16.3 17.5 %copy-start.4 = (s32[1,8]{1,0:T(1,128)S(1)}, s32[1,8]{1,0:T(1,128)}, u32[]{:S(2)}) copy-start(s32[1,8]{1,0:T(1,128)} %param.13) | copy-start | bytes 100
  16.3 57.2 %all-to-all-start = ((bf16[128,16,384]{2,1,0:T(8,128)(2,1)}), bf16[128,16,384]{2,1,0:T(8,128)(2,1)S(1)}, u32[]{:S(2)}, u32[]{:S(2)}) async-start(bf16[128,16,384]{2,1,0:T(8,128)(2,1)} %copy.97), calls=%async_computation | async-start | bytes 3145728 | tf_op jit(solution)/shard_map/all_to_all | solution.py:204
  73.5 43.4 %all-to-all-start.2 = ((bf16[384,4,768]{0,2,1:T(8,128)(2,1)}), bf16[384,4,768]{0,2,1:T(8,128)(2,1)}, u32[]{:S(2)}, u32[]{:S(2)}) async-start(bf16[384,4,768]{0,2,1:T(8,128)(2,1)} %bitcast.52), calls=%async_computation.2 | async-start | bytes 4718592 | tf_op jit(solution)/shard_map/all_to_all | solution.py:185
  116.9 27.0 %all-to-all-start.1 = ((bf16[128,15,128]{2,1,0:T(8,128)(2,1)}), bf16[128,15,128]{2,1,0:T(8,128)(2,1)S(1)}, u32[]{:S(2)}, u32[]{:S(2)}) async-start(bf16[128,15,128]{2,1,0:T(8,128)(2,1)} %copy.110), calls=%async_computation.1 | async-start | bytes 1048576 | tf_op jit(solution)/shard_map/all_to_all | solution.py:231
  130.3 30.7 %copy-start.3 = (bf16[256,768]{1,0:T(8,128)(2,1)S(1)}, bf16[256,768]{1,0:T(8,128)(2,1)}, u32[]{:S(2)}) copy-start(bf16[256,768]{1,0:T(8,128)(2,1)} %param.15) | copy-start | bytes 1179652
  161.0 6.7 %copy-start.2 = (bf16[768]{0:T(1024)(128)(2,1)S(1)}, bf16[768]{0:T(1024)(128)(2,1)}, u32[]{:S(2)}) copy-start(bf16[768]{0:T(1024)(128)(2,1)} %param.17) | copy-start | bytes 4612
  164.2 8.9 %all-to-all-start.3 = ((f32[4,1,256]{2,1,0:T(1,128)}), f32[4,1,256]{2,1,0:T(1,128)S(1)}, u32[]{:S(2)}, u32[]{:S(2)}) async-start(f32[4,1,256]{2,1,0:T(1,128)} %broadcast_in_dim.25), calls=%async_computation.3 | async-start | bytes 8192 | tf_op jit(solution)/shard_map/all_to_all | solution.py:246
